TPU v7x, 1024 devices: a whole 8x8x8 slice. The times are simulated.
1024 devices in a mesh: seq: 64 (over z, y_lo, core), chan: 16 (over x, y_hi).
Axes of the slice: x: 8, y: 8 (y_hi: 2, y_lo: 4; y = y_hi * 4 + y_lo), z: 8, core: 2. Of those that a mesh axis runs over, the one named last changes fastest.
Arguments:
- queries: bfloat16 [8192, 4096], P('seq', 'chan'), may hold values from -6 to 6
- keys: bfloat16 [8192, 4096], P('seq', 'chan'), may hold values from -6 to 6
- values: bfloat16 [8192, 4096], P('seq', 'chan'), may hold values from -6 to 6
- short_taps: float32 [3, 3, 4096], P(None, None, 'chan'), may hold values from -3 to 3
- long_filter: float32 [4096, 8192], P(('chan', 'seq')), may hold values from -1 to 1
- skip_gain: float32 [4096], P(('chan', 'seq')), may hold values from -1 to 1
- out_weight: bfloat16 [4096, 4096], P(None, 'chan'), may hold values from -0.09375 to 0.09375
Outputs:
- block_out: bfloat16 [8192, 4096], P('seq', 'chan')
All inputs are finite; a program needn't handle non-finite values.
Results may differ from a plain program's by a relative error of at most 0.012.
Values may be sent and summed in bfloat16 or wider, within the bound.
No kernel may reach another device: no remote copies, remote signals or barrier semaphores. Data moves between devices by JAX's collectives and lax.ppermute only.
A program may use at most 32 MiB of HBM per device.

v0:
```python
import math

import jax
import jax.numpy as jnp
from jax import lax
from jax.sharding import PartitionSpec as P

HIGHEST_MODE = lax.Precision.HIGHEST


def shifted(block, axis, distance):
    devices = range(lax.axis_size(axis))
    route = [(i - distance, i) for i in devices if i - distance in devices]
    return lax.ppermute(block, axis, route)


def tables(count):
    index = jnp.arange(count, dtype=jnp.int32)
    phase = (index[:, None] * index[None, :] % count).astype(jnp.float32) * (2.0 * math.pi / count)
    return (jnp.cos(phase), jnp.sin(phase))


def twiddle(outer, inner, total):
    first = jnp.arange(outer, dtype=jnp.int32)
    second = jnp.arange(inner, dtype=jnp.int32)
    phase = (first[:, None] * second[None, :] % total).astype(jnp.float32) * (2.0 * math.pi / total)
    return (jnp.cos(phase), jnp.sin(phase))


def split_factor(length):
    total = 2 * length
    best = 1
    candidate = 1
    while candidate * candidate <= total:
        if length % candidate == 0:
            best = candidate
        candidate += 1
    return (best, total // best)


def spectrum(signal, inner, outer, outer_tables, inner_tables, turn_tables):
    cos_out, sin_out = outer_tables
    cos_in, sin_in = inner_tables
    turn_cos, turn_sin = turn_tables
    blocks = signal.reshape(signal.shape[0], outer, inner)
    first_re = jnp.einsum("kn,cnm->ckm", cos_out, blocks, precision=HIGHEST_MODE)
    first_im = -jnp.einsum("kn,cnm->ckm", sin_out, blocks, precision=HIGHEST_MODE)
    turned_re = first_re * turn_cos + first_im * turn_sin
    turned_im = first_im * turn_cos - first_re * turn_sin
    real_part = jnp.einsum("ckm,mj->ckj", turned_re, cos_in, precision=HIGHEST_MODE) + jnp.einsum(
        "ckm,mj->ckj", turned_im, sin_in, precision=HIGHEST_MODE
    )
    imag_part = jnp.einsum("ckm,mj->ckj", turned_im, cos_in, precision=HIGHEST_MODE) - jnp.einsum(
        "ckm,mj->ckj", turned_re, sin_in, precision=HIGHEST_MODE
    )
    return (real_part, imag_part)


def long_convolution(mixed, filters, gains):
    channels, length = mixed.shape
    inner, outer = split_factor(length)
    total = 2 * length
    outer_tables = tables(outer)
    inner_tables = tables(inner)
    turn_tables = twiddle(outer, inner, total)
    signal = mixed.astype(jnp.float32)
    padding = jnp.zeros((channels, length), jnp.float32)
    sig_re, sig_im = spectrum(
        jnp.concatenate([signal, padding], 1), inner, outer, outer_tables, inner_tables, turn_tables
    )
    fil_re, fil_im = spectrum(
        jnp.concatenate([filters, padding], 1),
        inner,
        outer,
        outer_tables,
        inner_tables,
        turn_tables,
    )
    prod_re = sig_re * fil_re - sig_im * fil_im
    prod_im = sig_re * fil_im + sig_im * fil_re
    cos_in, sin_in = inner_tables
    back_re = jnp.einsum("ckj,jm->ckm", prod_re, cos_in, precision=HIGHEST_MODE) - jnp.einsum(
        "ckj,jm->ckm", prod_im, sin_in, precision=HIGHEST_MODE
    )
    back_im = jnp.einsum("ckj,jm->ckm", prod_re, sin_in, precision=HIGHEST_MODE) + jnp.einsum(
        "ckj,jm->ckm", prod_im, cos_in, precision=HIGHEST_MODE
    )
    turn_cos, turn_sin = turn_tables
    rot_re = back_re * turn_cos - back_im * turn_sin
    rot_im = back_re * turn_sin + back_im * turn_cos
    cos_out, sin_out = outer_tables
    half = outer // 2
    result = jnp.einsum("nk,ckm->cnm", cos_out[:half], rot_re, precision=HIGHEST_MODE) - jnp.einsum(
        "nk,ckm->cnm", sin_out[:half], rot_im, precision=HIGHEST_MODE
    )
    return result.reshape(channels, length) / total + gains[:, None] * signal


def shifted_filter(current, tail, taps):
    span = taps.shape[0]
    rows = current.shape[0]
    joined = jnp.concatenate([tail, current], 0).astype(jnp.float32)
    total = taps[0] * joined[span - 1 :]
    for offset in range(1, span):
        total = total + taps[offset] * joined[span - 1 - offset : span - 1 - offset + rows]
    return total


def body(queries, keys, values, short_taps, long_filter, skip_gain, out_weight):
    rows, width = queries.shape
    span = short_taps.shape[1]
    edge = rows - (span - 1)
    tails = shifted((queries[edge:], keys[edge:], values[edge:]), "seq", 1)
    short_q = shifted_filter(queries, tails[0], short_taps[0]).astype(jnp.bfloat16)
    mixed = (
        shifted_filter(keys, tails[1], short_taps[1])
        * shifted_filter(values, tails[2], short_taps[2])
    ).astype(jnp.bfloat16)
    groups = lax.axis_size("seq")
    per_group = width // groups
    mixed_t = mixed.T.reshape(groups, per_group, rows)
    empty = jnp.zeros((rows, out_weight.shape[1]), jnp.float32)
    split_mixed = lax.all_to_all(mixed_t, "seq", split_axis=0, concat_axis=2, tiled=True)
    convolved = long_convolution(split_mixed[0], long_filter, skip_gain).astype(jnp.bfloat16)
    returned = lax.all_to_all(convolved[None], "seq", split_axis=2, concat_axis=0, tiled=True)
    gated = (
        short_q.astype(jnp.float32) * returned.reshape(width, rows).T.astype(jnp.float32)
    ).astype(jnp.bfloat16)
    piece = jax.tree.map(lambda a: lax.all_gather(a, "chan", axis=1, tiled=True), gated)
    weight_rows = lax.slice_in_dim(out_weight, 0, piece.shape[1], axis=0)
    result = empty + jnp.dot(piece, weight_rows, preferred_element_type=jnp.float32)
    return result.astype(jnp.bfloat16)


def solution(mesh):
    in_specs = (
        P("seq", "chan"),
        P("seq", "chan"),
        P("seq", "chan"),
        P(None, None, "chan"),
        P(("chan", "seq"), None),
        P(("chan", "seq")),
        P(None, "chan"),
    )
    out_specs = P("seq", "chan")
    return jax.shard_map(body, mesh=mesh, in_specs=in_specs, out_specs=out_specs, check_vma=False)
```

profile of v0, /device:TPU:2, one launch (start us, length us, event | category | flops | bytes accessed | tf_op | source)
XLA Modules:
  0.0 266.0 jit_solution(15370914765499076436)
XLA Ops:
  6.5 0.9 slice.98
  7.4 0.1 copy.142
  7.5 2.4 collective-permute-start.1
  9.9 0.7 slice.105
  10.7 3.9 %collective-permute-start.2 = (bf16[2,256]{0,1:T(8,128)(2,1)S(1)}, bf16[2,256]{0,1:T(8,128)(2,1)}, u32[]{:S(2)}, u32[]{:S(2)}) collective-permute-start(bf16[2,256]{0,1:T(8,128)(2,1)S(1)} %copy.144), channel_id=1, source_target_pairs={{0,16},{16,32},{32,48},{48,64},{64,80},{80,96},{96,112},{112,128},... | collective-permute-start | bytes 3080 | tf_op jit(solution)/shard_map/ppermute | solution.py:14
  14.6 0.3 fusion.68
  14.9 0.3 fusion.67
  15.2 0.9 pad_bitcast_fusion
  16.1 0.7 convolution_bitcast_fusion
  16.8 0.7 fusion
  17.8 0.8 fusion.50
  18.5 0.7 fusion.54
  19.3 0.8 convolution_subtract_fusion.1
  20.1 0.8 convolution_add_fusion.1
  20.8 0.6 fusion.152
  21.7 0.9 maximum_convert_fusion.1
  22.6 0.9 maximum_convert_fusion.2
  23.6 1.0 fusion.19
  24.6 19.7 %all-to-all-start = ((bf16[64,4,128]{2,1,0:T(4,128)(2,1)}), bf16[64,4,128]{2,1,0:T(4,128)(2,1)S(1)}, u32[]{:S(2)}, u32[]{:S(2)}) async-start(bf16[64,4,128]{2,1,0:T(4,128)(2,1)} %bitcast.10), calls=%async_computation | async-start | bytes 131072 | tf_op jit(solution)/shard_map/all_to_all | solution.py:123
  44.3 0.3 fusion.70
  44.6 0.3 fusion.69
  44.9 9.3 %all-to-all-done = bf16[64,4,128]{2,1,0:T(4,128)(2,1)S(1)} async-done(((bf16[64,4,128]{2,1,0:T(4,128)(2,1)}), bf16[64,4,128]{2,1,0:T(4,128)(2,1)S(1)}, u32[]{:S(2)}, u32[]{:S(2)}) %all-to-all-start) | async-done | bytes 65568 | tf_op jit(solution)/shard_map/all_to_all | solution.py:123
  54.3 0.5 convolution_bitcast_fusion.1
  54.8 0.5 fusion.1
  55.4 0.8 fusion.57
  56.1 0.8 fusion.52
  56.9 0.8 convolution_add_fusion.2
  57.7 0.8 multiply_add_fusion
  58.5 0.6 fusion.48
  59.1 0.6 fusion.38
  59.8 0.7 convolution_subtract_fusion
  60.4 0.6 convolution_add_fusion
  61.1 0.5 fusion.9
  61.5 0.5 fusion.3
  62.2 6.8 %copy.168 = bf16[1,4,8192]{1,0,2:T(2,128)(2,1)} copy(bf16[1,4,8192]{2,1,0:T(4,128)(2,1)S(1)} %fusion.27) | data formatting | bytes 131072 | tf_op jit(solution)/shard_map/convert_element_type | solution.py:124
  69.0 0.5 broadcast.211
  69.5 46.8 %reduce = bf16[8192,4]{1,0:T(8,128)(2,1)} reduce(bf16[8192,1,4]{2,1,0:T(2,128)(2,1)} %bitcast.105, bf16[]{:T(256)} %broadcast.211), dimensions={1}, to_apply=%bitcast.93.reduce_sub_computation | reduce | bytes 131074
  116.3 5.6 %reshape.142 = bf16[64,2,256]{2,1,0:T(2,128)(2,1)} reshape(bf16[8192,4]{1,0:T(8,128)(2,1)} %reduce) | data formatting | bytes 131072
  121.9 4.6 %all-to-all-start.1 = ((bf16[64,2,256]{2,1,0:T(2,128)(2,1)}), bf16[64,2,256]{2,1,0:T(2,128)(2,1)S(1)}, u32[]{:S(2)}, u32[]{:S(2)}) async-start(bf16[64,2,256]{2,1,0:T(2,128)(2,1)} %reshape.142), calls=%async_computation.1 | async-start | bytes 131072 | tf_op jit(solution)/shard_map/all_to_all | solution.py:125
  126.7 1.8 collective-permute-start
  128.7 0.8 collective-permute-done
  129.6 6.9 %all-to-all-done.1 = bf16[64,2,256]{2,1,0:T(2,128)(2,1)S(1)} async-done(((bf16[64,2,256]{2,1,0:T(2,128)(2,1)}), bf16[64,2,256]{2,1,0:T(2,128)(2,1)S(1)}, u32[]{:S(2)}, u32[]{:S(2)}) %all-to-all-start.1) | async-done | bytes 65568 | tf_op jit(solution)/shard_map/all_to_all | solution.py:125
  136.5 8.7 %reshape.143 = bf16[8192,1,4]{2,1,0:T(2,128)(2,1)} reshape(bf16[64,2,256]{2,1,0:T(2,128)(2,1)S(1)} %all-to-all-done.1) | data formatting | bytes 131072
  145.2 8.5 %bitcast_convert_fusion = f32[1,4,8192]{1,0,2:T(1,128)} fusion(bf16[8192,1,4]{2,1,0:T(2,128)(2,1)} %reshape.143), kind=kLoop, calls=%fused_computation.181 | loop fusion | flops 32768 | bytes 196608 | tf_op jit(solution)/shard_map/convert_element_type | solution.py:127
  153.7 2.8 %copy.169 = f32[1,4,64,128]{3,1,2,0:T(4,128)S(1)} copy(f32[1,4,64,128]{1,3,2,0:T(8,128)} %bitcast.106) | data formatting | bytes 262144 | tf_op jit(solution)/shard_map/convert_element_type | solution.py:127
  156.5 0.9 multiply_convert_fusion
  157.4 99.3 %all-gather.2.cloned.1.call-done = bf16[128,4096]{0,1:T(8,128)(2,1)} async-done(((bf16[128,256]{0,1:T(8,128)(2,1)}), bf16[128,4096]{0,1:T(8,128)(2,1)}) %all-gather.2.cloned.1.call-update) | async-done | bytes 1048592 | tf_op jit(solution)/shard_map/all_gather | solution.py:129
  256.8 2.4 convolution_convert_fusion
  (34 shorter events, 1.3 us)
Async XLA Ops:
  6.5 250.2 %copy-start = (bf16[4096,256]{1,0:T(8,128)(2,1)S(1)}, bf16[4096,256]{1,0:T(8,128)(2,1)}, u32[]{:S(2)}) copy-start(bf16[4096,256]{1,0:T(8,128)(2,1)} %param.13) | copy-start | bytes 6291460
  6.5 14.9 %copy-start.1 = (bf16[128,256]{1,0:T(8,128)(2,1)S(1)}, bf16[128,256]{1,0:T(8,128)(2,1)}, u32[]{:S(2)}) copy-start(bf16[128,256]{1,0:T(8,128)(2,1)} %param.8) | copy-start | bytes 196612
  6.5 15.0 %copy-start.2 = (bf16[128,256]{1,0:T(8,128)(2,1)S(1)}, bf16[128,256]{1,0:T(8,128)(2,1)}, u32[]{:S(2)}) copy-start(bf16[128,256]{1,0:T(8,128)(2,1)} %param.9) | copy-start | bytes 196612
  6.5 14.3 %copy-start.4 = (f32[3,3,256]{2,1,0:T(4,128)S(1)}, f32[3,3,256]{2,1,0:T(4,128)}, u32[]{:S(2)}) copy-start(f32[3,3,256]{2,1,0:T(4,128)} %param.10) | copy-start | bytes 27652
  7.5 14.1 %collective-permute-start.1 = (bf16[2,256]{0,1:T(8,128)(2,1)S(1)}, bf16[2,256]{0,1:T(8,128)(2,1)}, u32[]{:S(2)}, u32[]{:S(2)}) collective-permute-start(bf16[2,256]{0,1:T(8,128)(2,1)S(1)} %copy.142), channel_id=1, source_target_pairs={{0,16},{16,32},{32,48},{48,64},{64,80},{80,96},{96,112},{112,128},... | collective-permute-start | bytes 3080 | tf_op jit(solution)/shard_map/ppermute | solution.py:14
  10.7 11.9 %collective-permute-start.2 = (bf16[2,256]{0,1:T(8,128)(2,1)S(1)}, bf16[2,256]{0,1:T(8,128)(2,1)}, u32[]{:S(2)}, u32[]{:S(2)}) collective-permute-start(bf16[2,256]{0,1:T(8,128)(2,1)S(1)} %copy.144), channel_id=1, source_target_pairs={{0,16},{16,32},{32,48},{48,64},{64,80},{80,96},{96,112},{112,128},... | collective-permute-start | bytes 3080 | tf_op jit(solution)/shard_map/ppermute | solution.py:14
  24.6 29.5 %all-to-all-start = ((bf16[64,4,128]{2,1,0:T(4,128)(2,1)}), bf16[64,4,128]{2,1,0:T(4,128)(2,1)S(1)}, u32[]{:S(2)}, u32[]{:S(2)}) async-start(bf16[64,4,128]{2,1,0:T(4,128)(2,1)} %bitcast.10), calls=%async_computation | async-start | bytes 131072 | tf_op jit(solution)/shard_map/all_to_all | solution.py:123
  56.9 5.2 %copy-start.7 = (f32[4]{0:T(128)S(1)}, f32[4]{0:T(128)}, u32[]{:S(2)}) copy-start(f32[4]{0:T(128)} %param.12) | copy-start | bytes 52
  69.5 57.1 %copy-start.3 = (bf16[128,256]{1,0:T(8,128)(2,1)S(1)}, bf16[128,256]{1,0:T(8,128)(2,1)}, u32[]{:S(2)}) copy-start(bf16[128,256]{1,0:T(8,128)(2,1)} %param.7) | copy-start | bytes 196612
  121.9 14.6 %all-to-all-start.1 = ((bf16[64,2,256]{2,1,0:T(2,128)(2,1)}), bf16[64,2,256]{2,1,0:T(2,128)(2,1)S(1)}, u32[]{:S(2)}, u32[]{:S(2)}) async-start(bf16[64,2,256]{2,1,0:T(2,128)(2,1)} %reshape.142), calls=%async_computation.1 | async-start | bytes 131072 | tf_op jit(solution)/shard_map/all_to_all | solution.py:125
  126.5 130.2 %all-gather.2.cloned.1.call-start = ((), (), s32[]{:S(2)}) async-start(), calls=%async_computation.2 | async-start | bytes 1114112 | tf_op jit(solution)/shard_map/all_gather | solution.py:129
  126.7 2.7 %collective-permute-start = (bf16[2,256]{0,1:T(8,128)(2,1)S(1)}, bf16[2,256]{0,1:T(8,128)(2,1)S(1)}, u32[]{:S(2)}, u32[]{:S(2)}) collective-permute-start(bf16[2,256]{0,1:T(8,128)(2,1)S(1)} %copy.140), channel_id=1, source_target_pairs={{0,16},{16,32},{32,48},{48,64},{64,80},{80,96},{96,112},{112,128},... | collective-permute-start | bytes 3080 | tf_op jit(solution)/shard_map/ppermute | solution.py:14
  153.7 2.9 %copy-start.5 = (f32[1,1,256]{2,1,0:T(1,128)S(1)}, f32[1,1,256]{2,1,0:T(1,128)}, u32[]{:S(2)}) copy-start(f32[1,1,256]{2,1,0:T(1,128)} %get-tuple-element.14) | copy-start | bytes 3076
  153.7 2.9 %copy-start.6 = (f32[1,1,256]{2,1,0:T(1,128)S(1)}, f32[1,1,256]{2,1,0:T(1,128)}, u32[]{:S(2)}) copy-start(f32[1,1,256]{2,1,0:T(1,128)} %get-tuple-element.15) | copy-start | bytes 3076
Sparse Core Ops, SparseCore 0:
  157.6 99.1 all-gather.1
where the time goes:
time: 267 us; the launch traced here: 266 us
  waiting for transfers between devices  116 us (43%)
  other arithmetic  60.4 us (23%)
  starting transfers between devices  32.5 us (12%)
  local copies, waits for them, and re-layouts  28.6 us (11%)
  matrix products  14.5 us (5%)
  between operations  13.7 us (5%)
    all_gather x1, waiting for transfers between devices, body(): lax.all_gather(a, 'chan', axis=1, tiled=True)  99.3 us
    unnamed x1, other arithmetic  46.8 us
    all_to_all x1, starting transfers between devices, body(): lax.all_to_all(mixed_t, 'seq', split_axis=0, concat_axis=2, tiled=True)  19.7 us
    unnamed x25, local copies, waits for them, and re-layouts  16.2 us
    all_to_all x1, waiting for transfers between devices, body(): lax.all_to_all(mixed_t, 'seq', split_axis=0, concat_axis=2, tiled=True)  9.27 us
    convert_element_type x1, other arithmetic, body(): returned.reshape(width, rows).T.astype(jnp.float32)  8.47 us
    ppermute x3, starting transfers between devices, shifted(): return lax.ppermute(block, axis, route)  8.1 us
    all_to_all x1, waiting for transfers between devices, body(): lax.all_to_all(convolved[None], 'seq', split_axis=2, concat_axis=0, tiled...  6.92 us
  transfers between devices with their start and end apart: 6, of which 4 were waited for; matrix products, arithmetic and copies ran while one was open for 4% of the time, Pallas kernels for 0%

commit v1 on v0

--- a/solution.py
+++ b/solution.py
@@ -110,7 +110,7 @@
     rows, width = queries.shape
     span = short_taps.shape[1]
     edge = rows - (span - 1)
-    tails = shifted((queries[edge:], keys[edge:], values[edge:]), "seq", 1)
+    tails = shifted(jnp.stack([queries[edge:], keys[edge:], values[edge:]]), "seq", 1)
     short_q = shifted_filter(queries, tails[0], short_taps[0]).astype(jnp.bfloat16)
     mixed = (
         shifted_filter(keys, tails[1], short_taps[1])
@@ -119,16 +119,16 @@
     groups = lax.axis_size("seq")
     per_group = width // groups
     mixed_t = mixed.T.reshape(groups, per_group, rows)
-    empty = jnp.zeros((rows, out_weight.shape[1]), jnp.float32)
-    split_mixed = lax.all_to_all(mixed_t, "seq", split_axis=0, concat_axis=2, tiled=True)
-    convolved = long_convolution(split_mixed[0], long_filter, skip_gain).astype(jnp.bfloat16)
-    returned = lax.all_to_all(convolved[None], "seq", split_axis=2, concat_axis=0, tiled=True)
-    gated = (
-        short_q.astype(jnp.float32) * returned.reshape(width, rows).T.astype(jnp.float32)
-    ).astype(jnp.bfloat16)
-    piece = jax.tree.map(lambda a: lax.all_gather(a, "chan", axis=1, tiled=True), gated)
-    weight_rows = lax.slice_in_dim(out_weight, 0, piece.shape[1], axis=0)
-    result = empty + jnp.dot(piece, weight_rows, preferred_element_type=jnp.float32)
+    split_mixed = lax.all_to_all(mixed_t, "seq", split_axis=0, concat_axis=0, tiled=True)
+    signal = split_mixed.transpose(1, 0, 2).reshape(per_group, groups * rows)
+    convolved = long_convolution(signal, long_filter, skip_gain).astype(jnp.bfloat16)
+    outgoing = convolved.reshape(per_group, groups, rows).transpose(1, 0, 2)
+    returned = lax.all_to_all(outgoing, "seq", split_axis=0, concat_axis=0, tiled=True)
+    long_out = returned.reshape(width, rows).T
+    gated = (short_q.astype(jnp.float32) * long_out.astype(jnp.float32)).astype(jnp.bfloat16)
+    pieces = lax.all_gather(gated, "chan", axis=0, tiled=False)
+    weight = out_weight.reshape(pieces.shape[0], width, out_weight.shape[1])
+    result = jnp.einsum("gtc,gcj->tj", pieces, weight, preferred_element_type=jnp.float32)
     return result.astype(jnp.bfloat16)
 
 

time: 267 us -> 179 us (0.67)
  the two profiles are of different devices: /device:TPU:2 before, /device:TPU:4 now
where the time goes in v1:
time: 179 us; the launch traced here: 178 us
  waiting for transfers between devices  113 us (63%)
  starting transfers between devices  28.3 us (16%)
  between operations  13.7 us (8%)
  matrix products  13.1 us (7%)
  local copies, waits for them, and re-layouts  6.94 us (4%)
  other arithmetic  3.27 us (2%)
    all_gather x1, waiting for transfers between devices, body(): pieces = lax.all_gather(gated, 'chan', axis=0, tiled=False)  94.1 us
    all_to_all x1, starting transfers between devices, body(): lax.all_to_all(mixed_t, 'seq', split_axis=0, concat_axis=0, tiled=True)  21.9 us
    all_to_all x1, waiting for transfers between devices, body(): lax.all_to_all(outgoing, 'seq', split_axis=0, concat_axis=0, tiled=True)  9.69 us
    all_to_all x1, waiting for transfers between devices, body(): lax.all_to_all(mixed_t, 'seq', split_axis=0, concat_axis=0, tiled=True)  9.27 us
    all_to_all x1, starting transfers between devices, body(): lax.all_to_all(outgoing, 'seq', split_axis=0, concat_axis=0, tiled=True)  4.62 us
  transfers between devices with their start and end apart: 4, of which 3 were waited for; matrix products, arithmetic and copies ran while one was open for 4% of the time, Pallas kernels for 0%

profile of v1, /device:TPU:4, one launch (start us, length us, event | category | flops | bytes accessed | tf_op | source)
XLA Modules:
  0.0 178.4 jit_solution(11707275728260724588)
XLA Ops:
  6.5 0.8 slice_bitcast_fusion.9
  7.4 0.7 slice_bitcast_fusion.7
  8.1 0.8 copy.53
  8.9 1.7 collective-permute-start
  10.7 0.9 pad_bitcast_fusion
  11.6 0.7 fusion
  12.4 0.7 convolution_bitcast_fusion
  13.1 0.3 fusion.69
  13.4 0.3 fusion.70
  13.6 0.1 copy.60
  13.7 0.1 copy.58
  13.8 0.7 fusion.56
  14.6 0.7 fusion.52
  15.4 0.8 convolution_add_fusion.1
  16.1 0.8 convolution_subtract_fusion.1
  16.9 0.1 copy.56
  17.0 1.0 copy.55
  18.0 0.1 maximum_convert_fusion.2
  18.1 0.1 maximum_convert_fusion.1
  18.2 1.0 fusion.21
  19.3 21.9 %all-to-all-start = ((bf16[64,4,128]{2,1,0:T(4,128)(2,1)}), bf16[64,4,128]{2,1,0:T(4,128)(2,1)S(1)}, u32[]{:S(2)}, u32[]{:S(2)}) async-start(bf16[64,4,128]{2,1,0:T(4,128)(2,1)} %bitcast.17), calls=%async_computation | async-start | bytes 131072 | tf_op jit(solution)/shard_map/all_to_all | solution.py:122
  41.2 0.3 fusion.72
  41.5 0.3 fusion.71
  41.7 9.3 %all-to-all-done = bf16[64,4,128]{2,1,0:T(4,128)(2,1)S(1)} async-done(((bf16[64,4,128]{2,1,0:T(4,128)(2,1)}), bf16[64,4,128]{2,1,0:T(4,128)(2,1)S(1)}, u32[]{:S(2)}, u32[]{:S(2)}) %all-to-all-start) | async-done | bytes 65568 | tf_op jit(solution)/shard_map/all_to_all | solution.py:122
  51.0 0.5 fusion.1
  51.6 0.5 convolution_bitcast_fusion.1
  52.2 0.8 fusion.59
  52.9 0.8 fusion.54
  53.7 0.8 convolution_add_fusion.2
  54.5 0.8 multiply_add_fusion
  55.2 0.0 copy-start.4
  55.2 0.6 fusion.40
  55.9 0.6 fusion.50
  56.6 0.7 convolution_add_fusion
  57.2 0.7 convolution_subtract_fusion
  57.9 0.4 fusion.11
  58.3 0.4 fusion.4
  58.7 0.7 copy.78
  59.4 4.6 %all-to-all-start.1 = ((bf16[64,4,128]{2,1,0:T(4,128)(2,1)}), bf16[64,4,128]{2,1,0:T(4,128)(2,1)S(1)}, u32[]{:S(2)}, u32[]{:S(2)}) async-start(bf16[64,4,128]{2,1,0:T(4,128)(2,1)} %copy.78), calls=%async_computation.1 | async-start | bytes 131072 | tf_op jit(solution)/shard_map/all_to_all | solution.py:126
  64.0 0.0 all-gather.3.cloned.1.call-start
  64.1 0.1 copy.54
  64.2 0.1 maximum_convert_fusion
  64.3 9.7 %all-to-all-done.1 = bf16[64,4,128]{2,1,0:T(4,128)(2,1)S(1)} async-done(((bf16[64,4,128]{2,1,0:T(4,128)(2,1)}), bf16[64,4,128]{2,1,0:T(4,128)(2,1)S(1)}, u32[]{:S(2)}, u32[]{:S(2)}) %all-to-all-start.1) | async-done | bytes 65568 | tf_op jit(solution)/shard_map/all_to_all | solution.py:126
  74.0 0.9 fusion.29
  74.9 0.0 all-gather.3.cloned.1.call-update
  74.9 94.1 %all-gather.3.cloned.1.call-done = bf16[2048,256]{0,1:T(8,128)(2,1)} async-done(((bf16[128,256]{0,1:T(8,128)(2,1)}), bf16[2048,256]{0,1:T(8,128)(2,1)}) %all-gather.3.cloned.1.call-update) | async-done | bytes 1048592 | tf_op jit(solution)/shard_map/all_gather | solution.py:129
  169.0 1.5 copy.79
  170.5 1.1 fusion.5
  (14 shorter events, 0.1 us)
Async XLA Ops:
  6.5 164.0 %copy-start = (bf16[4096,256]{1,0:T(8,128)(2,1)S(1)}, bf16[4096,256]{1,0:T(8,128)(2,1)}, u32[]{:S(2)}) copy-start(bf16[4096,256]{1,0:T(8,128)(2,1)} %param.13) | copy-start | bytes 6291460
  8.9 9.1 %collective-permute-start = (bf16[3,2,256]{1,2,0:T(8,128)(2,1)}, bf16[3,2,256]{1,2,0:T(8,128)(2,1)S(1)}, u32[]{:S(2)}, u32[]{:S(2)}) collective-permute-start(bf16[3,2,256]{1,2,0:T(8,128)(2,1)} %copy.53), channel_id=1, source_target_pairs={{0,16},{16,32},{32,48},{48,64},{64,80},{80,96},{96,112},{112,128},... | collective-permute-start | bytes 9224 | tf_op jit(solution)/shard_map/ppermute | solution.py:14
  13.8 3.1 %copy-start.3 = (f32[3,3,256]{2,1,0:T(4,128)S(1)}, f32[3,3,256]{2,1,0:T(4,128)}, u32[]{:S(2)}) copy-start(f32[3,3,256]{2,1,0:T(4,128)} %param.10) | copy-start | bytes 27652
  13.8 3.1 %copy-start.1 = (bf16[128,256]{1,0:T(8,128)(2,1)S(1)}, bf16[128,256]{1,0:T(8,128)(2,1)}, u32[]{:S(2)}) copy-start(bf16[128,256]{1,0:T(8,128)(2,1)} %param.9) | copy-start | bytes 196612
  19.3 31.7 %all-to-all-start = ((bf16[64,4,128]{2,1,0:T(4,128)(2,1)}), bf16[64,4,128]{2,1,0:T(4,128)(2,1)S(1)}, u32[]{:S(2)}, u32[]{:S(2)}) async-start(bf16[64,4,128]{2,1,0:T(4,128)(2,1)} %bitcast.17), calls=%async_computation | async-start | bytes 131072 | tf_op jit(solution)/shard_map/all_to_all | solution.py:122
  55.2 3.1 %copy-start.4 = (f32[4]{0:T(128)S(1)}, f32[4]{0:T(128)}, u32[]{:S(2)}) copy-start(f32[4]{0:T(128)} %param.12) | copy-start | bytes 52
  55.9 8.2 %copy-start.2 = (bf16[128,256]{1,0:T(8,128)(2,1)S(1)}, bf16[128,256]{1,0:T(8,128)(2,1)}, u32[]{:S(2)}) copy-start(bf16[128,256]{1,0:T(8,128)(2,1)} %param.7) | copy-start | bytes 196612
  59.4 14.6 %all-to-all-start.1 = ((bf16[64,4,128]{2,1,0:T(4,128)(2,1)}), bf16[64,4,128]{2,1,0:T(4,128)(2,1)S(1)}, u32[]{:S(2)}, u32[]{:S(2)}) async-start(bf16[64,4,128]{2,1,0:T(4,128)(2,1)} %copy.78), calls=%async_computation.1 | async-start | bytes 131072 | tf_op jit(solution)/shard_map/all_to_all | solution.py:126
  64.0 105.0 %all-gather.3.cloned.1.call-start = ((), (), s32[]{:S(2)}) async-start(), calls=%async_computation.2 | async-start | bytes 1114112 | tf_op jit(solution)/shard_map/all_gather | solution.py:129
Sparse Core Ops, SparseCore 0:
  75.0 93.9 all-gather.2

commit v2 on v1

--- a/solution.py
+++ b/solution.py
@@ -106,6 +106,36 @@
     return total
 
 
+def chan_route(size, step):
+    pairs = size // 2
+    return [(x * 2 + h, ((x + step) % pairs) * 2 + h) for x in range(pairs) for h in range(2)]
+
+
+def gather_chan(block):
+    size = lax.axis_size("chan")
+    pairs = size // 2
+    me = lax.axis_index("chan")
+    mine_x = me // 2
+    mine_h = me % 2
+    partner = lax.ppermute(block, "chan", [(i, i ^ 1) for i in range(size)])
+    held = jnp.stack([block, partner])
+    slots = [held]
+    places = [mine_x]
+    right = held
+    left = held
+    for step in range(1, pairs // 2 + 1):
+        right = lax.ppermute(right, "chan", chan_route(size, 1))
+        slots.append(right)
+        places.append((mine_x - step) % pairs)
+        if step < pairs - step:
+            left = lax.ppermute(left, "chan", chan_route(size, -1))
+            slots.append(left)
+            places.append((mine_x + step) % pairs)
+    place = jnp.stack(places)
+    order = jnp.stack([place * 2 + mine_h, place * 2 + (1 - mine_h)], axis=1)
+    return jnp.stack(slots), order
+
+
 def body(queries, keys, values, short_taps, long_filter, skip_gain, out_weight):
     rows, width = queries.shape
     span = short_taps.shape[1]
@@ -126,9 +156,9 @@
     returned = lax.all_to_all(outgoing, "seq", split_axis=0, concat_axis=0, tiled=True)
     long_out = returned.reshape(width, rows).T
     gated = (short_q.astype(jnp.float32) * long_out.astype(jnp.float32)).astype(jnp.bfloat16)
-    pieces = lax.all_gather(gated, "chan", axis=0, tiled=False)
-    weight = out_weight.reshape(pieces.shape[0], width, out_weight.shape[1])
-    result = jnp.einsum("gtc,gcj->tj", pieces, weight, preferred_element_type=jnp.float32)
+    pieces, order = gather_chan(gated)
+    weight = out_weight.reshape(-1, width, out_weight.shape[1])[order]
+    result = jnp.einsum("pqtc,pqcj->tj", pieces, weight, preferred_element_type=jnp.float32)
     return result.astype(jnp.bfloat16)
 
 

time: 179 us -> 112 us (0.63)
  the two profiles are of different devices: /device:TPU:4 before, /device:TPU:24 now
where the time goes in v2:
time: 112 us
  starting transfers between devices  60.2 us (54%)
  waiting for transfers between devices  29.1 us (26%)
  matrix products  13.1 us (12%)
  local copies, waits for them, and re-layouts  6.43 us (6%)
  other arithmetic  2.41 us (2%)
    all_to_all x1, starting transfers between devices, body(): lax.all_to_all(mixed_t, 'seq', split_axis=0, concat_axis=0, tiled=True)  21.4 us
    ppermute x3, starting transfers between devices, gather_chan(): left = lax.ppermute(left, 'chan', chan_route(size, -1))  14.8 us
    all_to_all x1, waiting for transfers between devices, body(): lax.all_to_all(outgoing, 'seq', split_axis=0, concat_axis=0, tiled=True)  9.11 us
    ppermute x4, starting transfers between devices, gather_chan(): right = lax.ppermute(right, 'chan', chan_route(size, 1))  8.37 us
    all_to_all x1, waiting for transfers between devices, body(): lax.all_to_all(mixed_t, 'seq', split_axis=0, concat_axis=0, tiled=True)  8.3 us
    ppermute x1, starting transfers between devices, gather_chan(): partner = lax.ppermute(block, 'chan', [(i, i ^ 1) for i in range(size)])  8.18 us
    ppermute x4, waiting for transfers between devices, gather_chan(): right = lax.ppermute(right, 'chan', chan_route(size, 1))  8.01 us
    all_to_all x1, starting transfers between devices, body(): lax.all_to_all(outgoing, 'seq', split_axis=0, concat_axis=0, tiled=True)  5.43 us
  transfers between devices with their start and end apart: 11, of which 6 were waited for; matrix products, arithmetic and copies ran while one was open for 8% of the time, Pallas kernels for 0%

profile of v2, /device:TPU:24, one launch (start us, length us, event | category | flops | bytes accessed | tf_op | source)
XLA Modules:
  0.0 111.9 jit_solution(14946860243516597142)
XLA Ops:
  0.0 0.8 slice_bitcast_fusion.9
  0.8 0.7 slice_bitcast_fusion.7
  1.6 1.9 %collective-permute-start = (bf16[3,2,256]{2,1,0:T(2,128)(2,1)S(1)}, bf16[3,2,256]{2,1,0:T(2,128)(2,1)S(1)}, u32[]{:S(2)}, u32[]{:S(2)}) collective-permute-start(bf16[3,2,256]{2,1,0:T(2,128)(2,1)S(1)} %pad_maximum_fusion.1), channel_id=1, source_target_pairs={{0,16},{16,32},{32,48},{48,64},{64,80},{80,96},{96,112},{112,128},... | collective-permute-start | bytes 9224 | tf_op jit(solution)/shard_map/ppermute | solution.py:14
  3.5 0.3 fusion.69
  3.8 0.3 fusion.68
  4.0 0.9 pad_bitcast_fusion
  5.0 0.7 fusion
  5.7 0.7 convolution_bitcast_fusion
  6.7 0.7 fusion.51
  7.4 0.7 fusion.55
  8.2 0.8 convolution_subtract_fusion.1
  8.9 0.8 convolution_add_fusion.1
  10.0 0.1 copy.55
  10.1 0.1 copy.53
  10.5 1.0 fusion.21
  11.5 21.4 %all-to-all-start = ((bf16[64,4,128]{2,1,0:T(4,128)(2,1)}), bf16[64,4,128]{2,1,0:T(4,128)(2,1)S(1)}, u32[]{:S(2)}, u32[]{:S(2)}) async-start(bf16[64,4,128]{2,1,0:T(4,128)(2,1)} %bitcast.17), calls=%async_computation | async-start | bytes 131072 | tf_op jit(solution)/shard_map/all_to_all | solution.py:152
  33.0 0.3 fusion.71
  33.5 0.3 fusion.70
  33.8 8.3 %all-to-all-done = bf16[64,4,128]{2,1,0:T(4,128)(2,1)S(1)} async-done(((bf16[64,4,128]{2,1,0:T(4,128)(2,1)}), bf16[64,4,128]{2,1,0:T(4,128)(2,1)S(1)}, u32[]{:S(2)}, u32[]{:S(2)}) %all-to-all-start) | async-done | bytes 65568 | tf_op jit(solution)/shard_map/all_to_all | solution.py:152
  42.1 0.5 convolution_bitcast_fusion.1
  42.7 0.5 fusion.1
  43.2 0.8 fusion.53
  44.0 0.8 fusion.58
  44.7 0.8 convolution_add_fusion.2
  45.5 0.8 multiply_add_fusion
  46.3 0.7 fusion.39
  47.0 0.6 fusion.49
  47.6 0.6 convolution_add_fusion
  48.3 0.6 convolution_subtract_fusion
  48.9 0.4 fusion.11
  49.3 0.4 fusion.4
  49.8 0.7 copy.78
  50.5 5.4 %all-to-all-start.1 = ((bf16[64,4,128]{2,1,0:T(4,128)(2,1)}), bf16[64,4,128]{2,1,0:T(4,128)(2,1)S(1)}, u32[]{:S(2)}, u32[]{:S(2)}) async-start(bf16[64,4,128]{2,1,0:T(4,128)(2,1)} %copy.78), calls=%async_computation.1 | async-start | bytes 131072 | tf_op jit(solution)/shard_map/all_to_all | solution.py:156
  55.9 9.1 %all-to-all-done.1 = bf16[64,4,128]{2,1,0:T(4,128)(2,1)S(1)} async-done(((bf16[64,4,128]{2,1,0:T(4,128)(2,1)}), bf16[64,4,128]{2,1,0:T(4,128)(2,1)S(1)}, u32[]{:S(2)}, u32[]{:S(2)}) %all-to-all-start.1) | async-done | bytes 65568 | tf_op jit(solution)/shard_map/all_to_all | solution.py:156
  65.2 8.2 %collective-permute-start.1 = (bf16[128,256]{1,0:T(8,128)(2,1)S(1)}, bf16[128,256]{1,0:T(8,128)(2,1)S(1)}, u32[]{:S(2)}, u32[]{:S(2)}) collective-permute-start(bf16[128,256]{1,0:T(8,128)(2,1)S(1)} %fusion.28), channel_id=1, source_target_pairs={{0,1},{1,0},{2,3},{3,2},{4,5},{5,4},{6,7},{7,6},{8,9},{9,8},{10,11... | collective-permute-start | bytes 196616 | tf_op jit(solution)/shard_map/ppermute | solution.py:120
  73.6 3.7 %collective-permute-done.1 = bf16[128,256]{1,0:T(8,128)(2,1)S(1)} collective-permute-done((bf16[128,256]{1,0:T(8,128)(2,1)S(1)}, bf16[128,256]{1,0:T(8,128)(2,1)S(1)}, u32[]{:S(2)}, u32[]{:S(2)}) %collective-permute-start.1) | collective-permute-done | bytes 65568 | tf_op jit(solution)/shard_map/ppermute | solution.py:120
  77.3 2.5 %collective-permute-start.2 = (bf16[2,128,256]{2,1,0:T(8,128)(2,1)S(1)}, bf16[2,128,256]{2,1,0:T(8,128)(2,1)S(1)}, u32[]{:S(2)}, u32[]{:S(2)}) collective-permute-start(bf16[2,128,256]{2,1,0:T(8,128)(2,1)S(1)} %pad_maximum_fusion), channel_id=1, source_target_pairs={{0,2},{1,3},{2,4},{3,5},{4,6},{5,7},{6,8},{7,9},{8,10},{9,11},{10,... | collective-permute-start | bytes 393224 | tf_op jit(solution)/shard_map/ppermute | solution.py:127
  79.8 4.5 %collective-permute-start.3 = (bf16[2,128,256]{2,1,0:T(8,128)(2,1)S(1)}, bf16[2,128,256]{2,1,0:T(8,128)(2,1)S(1)}, u32[]{:S(2)}, u32[]{:S(2)}) collective-permute-start(bf16[2,128,256]{2,1,0:T(8,128)(2,1)S(1)} %pad_maximum_fusion), channel_id=1, source_target_pairs={{0,14},{1,15},{2,0},{3,1},{4,2},{5,3},{6,4},{7,5},{8,6},{9,7},{10,... | collective-permute-start | bytes 393224 | tf_op jit(solution)/shard_map/ppermute | solution.py:131
  84.4 2.0 %gather_fusion = bf16[16,256,256]{2,1,0:T(8,128)(2,1)} fusion(bf16[16,256,256]{2,1,0:T(8,128)(2,1)S(1)} %bitcast.143, s32[1024]{0:T(1024)S(1)} %pad_clamp_fusion), kind=kCustom, calls=%fused_computation | custom fusion | bytes 4194368 | tf_op jit(solution)/shard_map/gather | solution.py:160
  86.4 2.1 %collective-permute-start.4 = (bf16[2,128,256]{2,1,0:T(8,128)(2,1)S(1)}, bf16[2,128,256]{2,1,0:T(8,128)(2,1)S(1)}, u32[]{:S(2)}, u32[]{:S(2)}) collective-permute-start(bf16[2,128,256]{2,1,0:T(8,128)(2,1)S(1)} %collective-permute-done.2), channel_id=1, source_target_pairs={{0,2},{1,3},{2,4},{3,5},{4,6},{5,7},{6,8},{7,9},{8,10},{9,11},{10,... | collective-permute-start | bytes 393224 | tf_op jit(solution)/shard_map/ppermute | solution.py:127
  88.5 5.1 %collective-permute-start.5 = (bf16[2,128,256]{2,1,0:T(8,128)(2,1)S(1)}, bf16[2,128,256]{2,1,0:T(8,128)(2,1)S(1)}, u32[]{:S(2)}, u32[]{:S(2)}) collective-permute-start(bf16[2,128,256]{2,1,0:T(8,128)(2,1)S(1)} %collective-permute-done.3), channel_id=1, source_target_pairs={{0,14},{1,15},{2,0},{3,1},{4,2},{5,3},{6,4},{7,5},{8,6},{9,7},{10,... | collective-permute-start | bytes 393224 | tf_op jit(solution)/shard_map/ppermute | solution.py:131
  93.7 1.0 collective-permute-done.4
  94.6 1.9 %collective-permute-start.6 = (bf16[2,128,256]{2,1,0:T(8,128)(2,1)S(1)}, bf16[2,128,256]{2,1,0:T(8,128)(2,1)S(1)}, u32[]{:S(2)}, u32[]{:S(2)}) collective-permute-start(bf16[2,128,256]{2,1,0:T(8,128)(2,1)S(1)} %collective-permute-done.4), channel_id=1, source_target_pairs={{0,2},{1,3},{2,4},{3,5},{4,6},{5,7},{6,8},{7,9},{8,10},{9,11},{10,... | collective-permute-start | bytes 393224 | tf_op jit(solution)/shard_map/ppermute | solution.py:127
  96.6 5.1 %collective-permute-start.7 = (bf16[2,128,256]{2,1,0:T(8,128)(2,1)S(1)}, bf16[2,128,256]{2,1,0:T(8,128)(2,1)S(1)}, u32[]{:S(2)}, u32[]{:S(2)}) collective-permute-start(bf16[2,128,256]{2,1,0:T(8,128)(2,1)S(1)} %collective-permute-done.5), channel_id=1, source_target_pairs={{0,14},{1,15},{2,0},{3,1},{4,2},{5,3},{6,4},{7,5},{8,6},{9,7},{10,... | collective-permute-start | bytes 393224 | tf_op jit(solution)/shard_map/ppermute | solution.py:131
  101.8 1.0 collective-permute-done.6
  102.7 1.9 %collective-permute-start.8 = (bf16[2,128,256]{2,1,0:T(8,128)(2,1)S(1)}, bf16[2,128,256]{2,1,0:T(8,128)(2,1)S(1)}, u32[]{:S(2)}, u32[]{:S(2)}) collective-permute-start(bf16[2,128,256]{2,1,0:T(8,128)(2,1)S(1)} %collective-permute-done.6), channel_id=1, source_target_pairs={{0,2},{1,3},{2,4},{3,5},{4,6},{5,7},{6,8},{7,9},{8,10},{9,11},{10,... | collective-permute-start | bytes 393224 | tf_op jit(solution)/shard_map/ppermute | solution.py:127
  104.7 6.1 %collective-permute-done.8 = bf16[2,128,256]{2,1,0:T(8,128)(2,1)S(1)} collective-permute-done((bf16[2,128,256]{2,1,0:T(8,128)(2,1)S(1)}, bf16[2,128,256]{2,1,0:T(8,128)(2,1)S(1)}, u32[]{:S(2)}, u32[]{:S(2)}) %collective-permute-start.8) | collective-permute-done | bytes 131104 | tf_op jit(solution)/shard_map/ppermute | solution.py:127
  110.8 1.1 fusion.5
  (47 shorter events, 1.3 us)
Async XLA Ops:
  0.0 84.4 %copy-start = (bf16[4096,256]{1,0:T(8,128)(2,1)S(1)}, bf16[4096,256]{1,0:T(8,128)(2,1)}, u32[]{:S(2)}) copy-start(bf16[4096,256]{1,0:T(8,128)(2,1)} %param.13) | copy-start | bytes 6291460
  1.6 8.4 %collective-permute-start = (bf16[3,2,256]{2,1,0:T(2,128)(2,1)S(1)}, bf16[3,2,256]{2,1,0:T(2,128)(2,1)S(1)}, u32[]{:S(2)}, u32[]{:S(2)}) collective-permute-start(bf16[3,2,256]{2,1,0:T(2,128)(2,1)S(1)} %pad_maximum_fusion.1), channel_id=1, source_target_pairs={{0,16},{16,32},{32,48},{48,64},{64,80},{80,96},{96,112},{112,128},... | collective-permute-start | bytes 9224 | tf_op jit(solution)/shard_map/ppermute | solution.py:14
  6.6 3.1 %copy-start.5 = (f32[3,3,256]{2,1,0:T(4,128)S(1)}, f32[3,3,256]{2,1,0:T(4,128)}, u32[]{:S(2)}) copy-start(f32[3,3,256]{2,1,0:T(4,128)} %param.10) | copy-start | bytes 27652
  6.6 3.1 %copy-start.3 = (bf16[128,256]{1,0:T(8,128)(2,1)S(1)}, bf16[128,256]{1,0:T(8,128)(2,1)}, u32[]{:S(2)}) copy-start(bf16[128,256]{1,0:T(8,128)(2,1)} %param.8) | copy-start | bytes 196612
  6.7 3.2 %copy-start.4 = (bf16[128,256]{1,0:T(8,128)(2,1)S(1)}, bf16[128,256]{1,0:T(8,128)(2,1)}, u32[]{:S(2)}) copy-start(bf16[128,256]{1,0:T(8,128)(2,1)} %param.9) | copy-start | bytes 196612
  11.5 30.5 %all-to-all-start = ((bf16[64,4,128]{2,1,0:T(4,128)(2,1)}), bf16[64,4,128]{2,1,0:T(4,128)(2,1)S(1)}, u32[]{:S(2)}, u32[]{:S(2)}) async-start(bf16[64,4,128]{2,1,0:T(4,128)(2,1)} %bitcast.17), calls=%async_computation | async-start | bytes 131072 | tf_op jit(solution)/shard_map/all_to_all | solution.py:152
  46.3 3.1 %copy-start.6 = (f32[4]{0:T(128)S(1)}, f32[4]{0:T(128)}, u32[]{:S(2)}) copy-start(f32[4]{0:T(128)} %param.12) | copy-start | bytes 52
  47.0 9.0 %copy-start.2 = (bf16[128,256]{1,0:T(8,128)(2,1)S(1)}, bf16[128,256]{1,0:T(8,128)(2,1)}, u32[]{:S(2)}) copy-start(bf16[128,256]{1,0:T(8,128)(2,1)} %param.7) | copy-start | bytes 196612
  50.5 14.6 %all-to-all-start.1 = ((bf16[64,4,128]{2,1,0:T(4,128)(2,1)}), bf16[64,4,128]{2,1,0:T(4,128)(2,1)S(1)}, u32[]{:S(2)}, u32[]{:S(2)}) async-start(bf16[64,4,128]{2,1,0:T(4,128)(2,1)} %copy.78), calls=%async_computation.1 | async-start | bytes 131072 | tf_op jit(solution)/shard_map/all_to_all | solution.py:156
  65.2 12.1 %collective-permute-start.1 = (bf16[128,256]{1,0:T(8,128)(2,1)S(1)}, bf16[128,256]{1,0:T(8,128)(2,1)S(1)}, u32[]{:S(2)}, u32[]{:S(2)}) collective-permute-start(bf16[128,256]{1,0:T(8,128)(2,1)S(1)} %fusion.28), channel_id=1, source_target_pairs={{0,1},{1,0},{2,3},{3,2},{4,5},{5,4},{6,7},{7,6},{8,9},{9,8},{10,11... | collective-permute-start | bytes 196616 | tf_op jit(solution)/shard_map/ppermute | solution.py:120
  77.3 9.1 %collective-permute-start.2 = (bf16[2,128,256]{2,1,0:T(8,128)(2,1)S(1)}, bf16[2,128,256]{2,1,0:T(8,128)(2,1)S(1)}, u32[]{:S(2)}, u32[]{:S(2)}) collective-permute-start(bf16[2,128,256]{2,1,0:T(8,128)(2,1)S(1)} %pad_maximum_fusion), channel_id=1, source_target_pairs={{0,2},{1,3},{2,4},{3,5},{4,6},{5,7},{6,8},{7,9},{8,10},{9,11},{10,... | collective-permute-start | bytes 393224 | tf_op jit(solution)/shard_map/ppermute | solution.py:127
  79.8 8.7 %collective-permute-start.3 = (bf16[2,128,256]{2,1,0:T(8,128)(2,1)S(1)}, bf16[2,128,256]{2,1,0:T(8,128)(2,1)S(1)}, u32[]{:S(2)}, u32[]{:S(2)}) collective-permute-start(bf16[2,128,256]{2,1,0:T(8,128)(2,1)S(1)} %pad_maximum_fusion), channel_id=1, source_target_pairs={{0,14},{1,15},{2,0},{3,1},{4,2},{5,3},{6,4},{7,5},{8,6},{9,7},{10,... | collective-permute-start | bytes 393224 | tf_op jit(solution)/shard_map/ppermute | solution.py:131
  86.4 24.4 %copy-start.1 = (bf16[16,256,256]{2,1,0:T(8,128)(2,1)S(1)}, bf16[16,256,256]{2,1,0:T(8,128)(2,1)}, u32[]{:S(2)}) copy-start(bf16[16,256,256]{2,1,0:T(8,128)(2,1)} %gather_fusion) | copy-start | bytes 6291460
  86.4 8.2 %collective-permute-start.4 = (bf16[2,128,256]{2,1,0:T(8,128)(2,1)S(1)}, bf16[2,128,256]{2,1,0:T(8,128)(2,1)S(1)}, u32[]{:S(2)}, u32[]{:S(2)}) collective-permute-start(bf16[2,128,256]{2,1,0:T(8,128)(2,1)S(1)} %collective-permute-done.2), channel_id=1, source_target_pairs={{0,2},{1,3},{2,4},{3,5},{4,6},{5,7},{6,8},{7,9},{8,10},{9,11},{10,... | collective-permute-start | bytes 393224 | tf_op jit(solution)/shard_map/ppermute | solution.py:127
  88.5 8.1 %collective-permute-start.5 = (bf16[2,128,256]{2,1,0:T(8,128)(2,1)S(1)}, bf16[2,128,256]{2,1,0:T(8,128)(2,1)S(1)}, u32[]{:S(2)}, u32[]{:S(2)}) collective-permute-start(bf16[2,128,256]{2,1,0:T(8,128)(2,1)S(1)} %collective-permute-done.3), channel_id=1, source_target_pairs={{0,14},{1,15},{2,0},{3,1},{4,2},{5,3},{6,4},{7,5},{8,6},{9,7},{10,... | collective-permute-start | bytes 393224 | tf_op jit(solution)/shard_map/ppermute | solution.py:131
  94.6 8.1 %collective-permute-start.6 = (bf16[2,128,256]{2,1,0:T(8,128)(2,1)S(1)}, bf16[2,128,256]{2,1,0:T(8,128)(2,1)S(1)}, u32[]{:S(2)}, u32[]{:S(2)}) collective-permute-start(bf16[2,128,256]{2,1,0:T(8,128)(2,1)S(1)} %collective-permute-done.4), channel_id=1, source_target_pairs={{0,2},{1,3},{2,4},{3,5},{4,6},{5,7},{6,8},{7,9},{8,10},{9,11},{10,... | collective-permute-start | bytes 393224 | tf_op jit(solution)/shard_map/ppermute | solution.py:127
  96.6 8.1 %collective-permute-start.7 = (bf16[2,128,256]{2,1,0:T(8,128)(2,1)S(1)}, bf16[2,128,256]{2,1,0:T(8,128)(2,1)S(1)}, u32[]{:S(2)}, u32[]{:S(2)}) collective-permute-start(bf16[2,128,256]{2,1,0:T(8,128)(2,1)S(1)} %collective-permute-done.5), channel_id=1, source_target_pairs={{0,14},{1,15},{2,0},{3,1},{4,2},{5,3},{6,4},{7,5},{8,6},{9,7},{10,... | collective-permute-start | bytes 393224 | tf_op jit(solution)/shard_map/ppermute | solution.py:131
  102.7 8.1 %collective-permute-start.8 = (bf16[2,128,256]{2,1,0:T(8,128)(2,1)S(1)}, bf16[2,128,256]{2,1,0:T(8,128)(2,1)S(1)}, u32[]{:S(2)}, u32[]{:S(2)}) collective-permute-start(bf16[2,128,256]{2,1,0:T(8,128)(2,1)S(1)} %collective-permute-done.6), channel_id=1, source_target_pairs={{0,2},{1,3},{2,4},{3,5},{4,6},{5,7},{6,8},{7,9},{8,10},{9,11},{10,... | collective-permute-start | bytes 393224 | tf_op jit(solution)/shard_map/ppermute | solution.py:127

commit v3 on v2

--- a/solution.py
+++ b/solution.py
@@ -156,9 +156,12 @@
     returned = lax.all_to_all(outgoing, "seq", split_axis=0, concat_axis=0, tiled=True)
     long_out = returned.reshape(width, rows).T
     gated = (short_q.astype(jnp.float32) * long_out.astype(jnp.float32)).astype(jnp.bfloat16)
-    pieces, order = gather_chan(gated)
-    weight = out_weight.reshape(-1, width, out_weight.shape[1])[order]
-    result = jnp.einsum("pqtc,pqcj->tj", pieces, weight, preferred_element_type=jnp.float32)
+    size = lax.axis_size("chan")
+    pieces = lax.all_to_all(
+        jnp.broadcast_to(gated[None], (size,) + gated.shape), "chan", split_axis=0, concat_axis=0, tiled=True
+    )
+    weight = out_weight.reshape(size, width, out_weight.shape[1])
+    result = jnp.einsum("gtc,gcj->tj", pieces, weight, preferred_element_type=jnp.float32)
     return result.astype(jnp.bfloat16)
 
 

time: 112 us -> 115 us (1.027)
  the two profiles are of different devices: /device:TPU:24 before, /device:TPU:8 now
where the time goes in v3:
time: 115 us; the launch traced here: 114 us
  blocking collectives  44.7 us (39%)
  starting transfers between devices  28.3 us (25%)
  waiting for transfers between devices  19 us (17%)
  matrix products  13.1 us (11%)
  local copies, waits for them, and re-layouts  5.91 us (5%)
  other arithmetic  2.64 us (2%)
    all_to_all x1, blocking collectives, body(): lax.all_to_all(jnp.broadcast_to(gated[None], (size,) + gated.shape), 'cha...  44.7 us
    all_to_all x1, starting transfers between devices, body(): lax.all_to_all(mixed_t, 'seq', split_axis=0, concat_axis=0, tiled=True)  21.2 us
    all_to_all x1, waiting for transfers between devices, body(): lax.all_to_all(outgoing, 'seq', split_axis=0, concat_axis=0, tiled=True)  9.73 us
    all_to_all x1, waiting for transfers between devices, body(): lax.all_to_all(mixed_t, 'seq', split_axis=0, concat_axis=0, tiled=True)  9.27 us
    all_to_all x1, starting transfers between devices, body(): lax.all_to_all(outgoing, 'seq', split_axis=0, concat_axis=0, tiled=True)  4.62 us
    ppermute x1, starting transfers between devices, shifted(): return lax.ppermute(block, axis, route)  2.42 us
  transfers between devices with their start and end apart: 3, of which 2 were waited for; matrix products, arithmetic and copies ran while one was open for 7% of the time, Pallas kernels for 0%

profile of v3, /device:TPU:8, one launch (start us, length us, event | category | flops | bytes accessed | tf_op | source)
XLA Modules:
  0.0 114.0 jit_solution(4387691624823914809)
XLA Ops:
  0.0 0.8 slice_bitcast_fusion.9
  0.8 0.7 slice_bitcast_fusion.7
  1.6 0.2 copy.53
  1.8 2.4 %collective-permute-start = (bf16[3,2,256]{1,2,0:T(8,128)(2,1)S(1)}, bf16[3,2,256]{1,2,0:T(8,128)(2,1)}, u32[]{:S(2)}, u32[]{:S(2)}) collective-permute-start(bf16[3,2,256]{1,2,0:T(8,128)(2,1)S(1)} %copy.53), channel_id=1, source_target_pairs={{0,16},{16,32},{32,48},{48,64},{64,80},{80,96},{96,112},{112,128},... | collective-permute-start | bytes 9224 | tf_op jit(solution)/shard_map/ppermute | solution.py:14
  4.2 0.9 pad_bitcast_fusion
  5.1 0.7 fusion
  5.9 0.7 convolution_bitcast_fusion
  6.6 0.3 fusion.69
  6.9 0.3 fusion.70
  7.1 0.1 copy.60
  7.2 0.1 copy.58
  7.3 0.7 fusion.56
  8.1 0.7 fusion.52
  8.8 0.8 convolution_add_fusion.1
  9.6 0.8 convolution_subtract_fusion.1
  10.4 0.1 copy.56
  10.5 1.0 copy.55
  11.5 0.9 slice_bitcast_fusion.2
  12.4 0.1 maximum_convert_fusion.2
  12.5 0.1 maximum_convert_fusion.1
  12.6 1.0 fusion.21
  13.7 21.2 %all-to-all-start = ((bf16[64,4,128]{2,1,0:T(4,128)(2,1)}), bf16[64,4,128]{2,1,0:T(4,128)(2,1)S(1)}, u32[]{:S(2)}, u32[]{:S(2)}) async-start(bf16[64,4,128]{2,1,0:T(4,128)(2,1)} %bitcast.17), calls=%async_computation | async-start | bytes 131072 | tf_op jit(solution)/shard_map/all_to_all | solution.py:152
  34.9 0.3 fusion.72
  35.2 0.3 fusion.71
  35.4 9.3 %all-to-all-done = bf16[64,4,128]{2,1,0:T(4,128)(2,1)S(1)} async-done(((bf16[64,4,128]{2,1,0:T(4,128)(2,1)}), bf16[64,4,128]{2,1,0:T(4,128)(2,1)S(1)}, u32[]{:S(2)}, u32[]{:S(2)}) %all-to-all-start) | async-done | bytes 65568 | tf_op jit(solution)/shard_map/all_to_all | solution.py:152
  44.8 0.5 fusion.1
  45.3 0.5 convolution_bitcast_fusion.1
  45.9 0.8 fusion.59
  46.6 0.8 fusion.54
  47.4 0.8 convolution_add_fusion.2
  48.2 0.8 multiply_add_fusion
  49.0 0.0 copy-start.4
  49.0 0.6 fusion.40
  49.6 0.6 fusion.50
  50.3 0.7 convolution_add_fusion
  50.9 0.6 convolution_subtract_fusion
  51.6 0.4 fusion.11
  52.0 0.4 fusion.4
  52.4 0.7 copy.78
  53.1 4.6 %all-to-all-start.1 = ((bf16[64,4,128]{2,1,0:T(4,128)(2,1)}), bf16[64,4,128]{2,1,0:T(4,128)(2,1)S(1)}, u32[]{:S(2)}, u32[]{:S(2)}) async-start(bf16[64,4,128]{2,1,0:T(4,128)(2,1)} %copy.78), calls=%async_computation.1 | async-start | bytes 131072 | tf_op jit(solution)/shard_map/all_to_all | solution.py:156
  57.8 0.1 copy.54
  57.9 0.1 maximum_convert_fusion
  58.0 9.7 %all-to-all-done.1 = bf16[64,4,128]{2,1,0:T(4,128)(2,1)S(1)} async-done(((bf16[64,4,128]{2,1,0:T(4,128)(2,1)}), bf16[64,4,128]{2,1,0:T(4,128)(2,1)S(1)}, u32[]{:S(2)}, u32[]{:S(2)}) %all-to-all-start.1) | async-done | bytes 65568 | tf_op jit(solution)/shard_map/all_to_all | solution.py:156
  67.7 0.2 fusion.29
  68.0 0.1 copy.79
  68.1 0.1 broadcast_in_dim.2
  68.2 44.7 %all_to_all.15 = bf16[16,128,256]{2,1,0:T(8,128)(2,1)S(1)} all-to-all(bf16[16,128,256]{2,1,0:T(8,128)(2,1)S(1)} %broadcast_in_dim.2), channel_id=1, replica_groups=mesh['seq'=64,'chan'=16] {'chan'}, dimensions={0} | all-to-all | bytes 2097152 | tf_op jit(solution)/shard_map/all_to_all | solution.py:160
  112.9 1.1 fusion.5
  (13 shorter events, 0.1 us)
Async XLA Ops:
  0.0 112.9 %copy-start = (bf16[4096,256]{1,0:T(8,128)(2,1)S(1)}, bf16[4096,256]{1,0:T(8,128)(2,1)}, u32[]{:S(2)}) copy-start(bf16[4096,256]{1,0:T(8,128)(2,1)} %param.13) | copy-start | bytes 6291460
  1.8 9.7 %collective-permute-start = (bf16[3,2,256]{1,2,0:T(8,128)(2,1)S(1)}, bf16[3,2,256]{1,2,0:T(8,128)(2,1)}, u32[]{:S(2)}, u32[]{:S(2)}) collective-permute-start(bf16[3,2,256]{1,2,0:T(8,128)(2,1)S(1)} %copy.53), channel_id=1, source_target_pairs={{0,16},{16,32},{32,48},{48,64},{64,80},{80,96},{96,112},{112,128},... | collective-permute-start | bytes 9224 | tf_op jit(solution)/shard_map/ppermute | solution.py:14
  7.3 3.1 %copy-start.3 = (f32[3,3,256]{2,1,0:T(4,128)S(1)}, f32[3,3,256]{2,1,0:T(4,128)}, u32[]{:S(2)}) copy-start(f32[3,3,256]{2,1,0:T(4,128)} %param.10) | copy-start | bytes 27652
  7.3 3.1 %copy-start.1 = (bf16[128,256]{1,0:T(8,128)(2,1)S(1)}, bf16[128,256]{1,0:T(8,128)(2,1)}, u32[]{:S(2)}) copy-start(bf16[128,256]{1,0:T(8,128)(2,1)} %param.9) | copy-start | bytes 196612
  13.7 31.1 %all-to-all-start = ((bf16[64,4,128]{2,1,0:T(4,128)(2,1)}), bf16[64,4,128]{2,1,0:T(4,128)(2,1)S(1)}, u32[]{:S(2)}, u32[]{:S(2)}) async-start(bf16[64,4,128]{2,1,0:T(4,128)(2,1)} %bitcast.17), calls=%async_computation | async-start | bytes 131072 | tf_op jit(solution)/shard_map/all_to_all | solution.py:152
  49.0 3.1 %copy-start.4 = (f32[4]{0:T(128)S(1)}, f32[4]{0:T(128)}, u32[]{:S(2)}) copy-start(f32[4]{0:T(128)} %param.12) | copy-start | bytes 52
  49.6 8.1 %copy-start.2 = (bf16[128,256]{1,0:T(8,128)(2,1)S(1)}, bf16[128,256]{1,0:T(8,128)(2,1)}, u32[]{:S(2)}) copy-start(bf16[128,256]{1,0:T(8,128)(2,1)} %param.7) | copy-start | bytes 196612
  53.1 14.6 %all-to-all-start.1 = ((bf16[64,4,128]{2,1,0:T(4,128)(2,1)}), bf16[64,4,128]{2,1,0:T(4,128)(2,1)S(1)}, u32[]{:S(2)}, u32[]{:S(2)}) async-start(bf16[64,4,128]{2,1,0:T(4,128)(2,1)} %copy.78), calls=%async_computation.1 | async-start | bytes 131072 | tf_op jit(solution)/shard_map/all_to_all | solution.py:156

commit v4 on v1

--- a/solution.py
+++ b/solution.py
@@ -3,7 +3,7 @@
 import jax
 import jax.numpy as jnp
 from jax import lax
-from jax.sharding import PartitionSpec as P
+from jax.sharding import Mesh, PartitionSpec as P
 
 HIGHEST_MODE = lax.Precision.HIGHEST
 
@@ -106,41 +106,68 @@
     return total
 
 
+SEQ = ("z", "ylo", "core")
+CHAN = ("x", "yh")
+
+
+def swap_half(block):
+    return lax.ppermute(block, "yh", [(0, 1), (1, 0)])
+
+
 def body(queries, keys, values, short_taps, long_filter, skip_gain, out_weight):
     rows, width = queries.shape
     span = short_taps.shape[1]
     edge = rows - (span - 1)
-    tails = shifted(jnp.stack([queries[edge:], keys[edge:], values[edge:]]), "seq", 1)
+    planes = lax.axis_size("x")
+    half = lax.axis_index("yh")
+    groups = lax.axis_size(SEQ)
+    seq_index = lax.axis_index(SEQ)
+    columns = out_weight.shape[1]
+    by_group = out_weight.reshape(planes, 2, width, columns)
+    other_rows = lax.dynamic_index_in_dim(by_group, 1 - half, axis=1, keepdims=False)
+    piece_rows = other_rows.reshape(planes * width, columns)
+    chunk = piece_rows.shape[0] // groups
+    sent_piece = lax.dynamic_slice_in_dim(piece_rows, seq_index * chunk, chunk, axis=0)
+    partner_piece = swap_half(sent_piece)
+    partner_weight = lax.all_gather(partner_piece, SEQ, axis=0, tiled=True)
+    tails = shifted(jnp.stack([queries[edge:], keys[edge:], values[edge:]]), SEQ, 1)
     short_q = shifted_filter(queries, tails[0], short_taps[0]).astype(jnp.bfloat16)
     mixed = (
         shifted_filter(keys, tails[1], short_taps[1])
         * shifted_filter(values, tails[2], short_taps[2])
     ).astype(jnp.bfloat16)
-    groups = lax.axis_size("seq")
     per_group = width // groups
     mixed_t = mixed.T.reshape(groups, per_group, rows)
-    split_mixed = lax.all_to_all(mixed_t, "seq", split_axis=0, concat_axis=0, tiled=True)
+    split_mixed = lax.all_to_all(mixed_t, SEQ, split_axis=0, concat_axis=0, tiled=True)
     signal = split_mixed.transpose(1, 0, 2).reshape(per_group, groups * rows)
     convolved = long_convolution(signal, long_filter, skip_gain).astype(jnp.bfloat16)
     outgoing = convolved.reshape(per_group, groups, rows).transpose(1, 0, 2)
-    returned = lax.all_to_all(outgoing, "seq", split_axis=0, concat_axis=0, tiled=True)
+    returned = lax.all_to_all(outgoing, SEQ, split_axis=0, concat_axis=0, tiled=True)
     long_out = returned.reshape(width, rows).T
     gated = (short_q.astype(jnp.float32) * long_out.astype(jnp.float32)).astype(jnp.bfloat16)
-    pieces = lax.all_gather(gated, "chan", axis=0, tiled=False)
-    weight = out_weight.reshape(pieces.shape[0], width, out_weight.shape[1])
-    result = jnp.einsum("gtc,gcj->tj", pieces, weight, preferred_element_type=jnp.float32)
+    pieces = lax.all_to_all(
+        jnp.broadcast_to(gated[None], (planes,) + gated.shape), "x", split_axis=0, concat_axis=0, tiled=True
+    )
+    own_rows = lax.dynamic_index_in_dim(by_group, half, axis=1, keepdims=False)
+    own_part = jnp.einsum("gtc,gcj->tj", pieces, own_rows, preferred_element_type=jnp.float32)
+    other_part = jnp.einsum(
+        "gtc,gcj->tj", pieces, partner_weight.reshape(planes, width, columns), preferred_element_type=jnp.float32
+    )
+    result = own_part + swap_half(other_part)
     return result.astype(jnp.bfloat16)
 
 
 def solution(mesh):
+    shape = mesh.devices.shape
+    fine = Mesh(mesh.devices.reshape(shape[0] // 8, 4, 2, shape[1] // 2, 2), SEQ + CHAN)
     in_specs = (
-        P("seq", "chan"),
-        P("seq", "chan"),
-        P("seq", "chan"),
-        P(None, None, "chan"),
-        P(("chan", "seq"), None),
-        P(("chan", "seq")),
-        P(None, "chan"),
+        P(SEQ, CHAN),
+        P(SEQ, CHAN),
+        P(SEQ, CHAN),
+        P(None, None, CHAN),
+        P(CHAN + SEQ, None),
+        P(CHAN + SEQ),
+        P(None, CHAN),
     )
-    out_specs = P("seq", "chan")
-    return jax.shard_map(body, mesh=mesh, in_specs=in_specs, out_specs=out_specs, check_vma=False)
+    out_specs = P(SEQ, CHAN)
+    return jax.shard_map(body, mesh=fine, in_specs=in_specs, out_specs=out_specs, check_vma=False)

time: 179 us -> 193 us (1.078)
  the two profiles are of different devices: /device:TPU:4 before, /device:TPU:80 now
where the time goes in v4:
time: 193 us
  waiting for transfers between devices  114 us (59%)
  starting transfers between devices  40.8 us (21%)
  matrix products  13.9 us (7%)
  between operations  13.8 us (7%)
  local copies, waits for them, and re-layouts  6.78 us (4%)
  other arithmetic  3.28 us (2%)
    all_gather x1, waiting for transfers between devices, body(): partner_weight = lax.all_gather(partner_piece, SEQ, axis=0, tiled=True)  68.3 us
    all_to_all x1, starting transfers between devices, body(): lax.all_to_all(mixed_t, SEQ, split_axis=0, concat_axis=0, tiled=True)  21.8 us
    all_to_all x1, waiting for transfers between devices, body(): lax.all_to_all(jnp.broadcast_to(gated[None], (planes,) + gated.shape), 'x...  17.8 us
    ppermute x2, waiting for transfers between devices, swap_half(): return lax.ppermute(block, 'yh', [(0, 1), (1, 0)])  11.6 us
    all_to_all x1, waiting for transfers between devices, body(): lax.all_to_all(outgoing, SEQ, split_axis=0, concat_axis=0, tiled=True)  8.99 us
    all_to_all x1, waiting for transfers between devices, body(): lax.all_to_all(mixed_t, SEQ, split_axis=0, concat_axis=0, tiled=True)  7.67 us
    all_to_all x1, starting transfers between devices, body(): lax.all_to_all(jnp.broadcast_to(gated[None], (planes,) + gated.shape), 'x...  6.76 us
    all_to_all x1, starting transfers between devices, body(): lax.all_to_all(outgoing, SEQ, split_axis=0, concat_axis=0, tiled=True)  5.43 us
  transfers between devices with their start and end apart: 7, of which 5 were waited for; matrix products, arithmetic and copies ran while one was open for 10% of the time, Pallas kernels for 0%

profile of v4, /device:TPU:80, one launch (start us, length us, event | category | flops | bytes accessed | tf_op | source)
XLA Modules:
  0.0 192.9 jit_solution(1371869375607233235)
XLA Ops:
  6.5 0.8 slice_bitcast_fusion.9
  7.4 0.7 slice_bitcast_fusion.7
  8.1 0.8 copy.55
  8.9 1.9 collective-permute-start
  11.0 0.6 constant_dynamic-slice_fusion
  11.6 2.4 %collective-permute-start.1 = (bf16[32,256]{1,0:T(8,128)(2,1)}, bf16[32,256]{1,0:T(8,128)(2,1)S(1)}, u32[]{:S(2)}, u32[]{:S(2)}) collective-permute-start(bf16[32,256]{1,0:T(8,128)(2,1)} %constant_dynamic-slice_fusion), channel_id=1, source_target_pairs={{0,1},{1,0},{2,3},{3,2},{4,5},{5,4},{6,7},{7,6},{8,9},{9,8},{10,11... | collective-permute-start | bytes 49160 | tf_op jit(solution)/shard_map/ppermute | solution.py:114
  14.1 0.7 fusion
  14.8 0.7 convolution_bitcast_fusion
  15.6 0.3 fusion.70
  15.8 0.3 fusion.71
  16.3 0.7 fusion.57
  17.1 0.7 fusion.53
  17.8 0.8 convolution_add_fusion.1
  18.6 0.8 convolution_subtract_fusion.1
  19.5 1.0 copy.57
  20.7 1.0 fusion.22
  21.7 21.8 %all-to-all-start = ((bf16[64,4,128]{2,1,0:T(4,128)(2,1)}), bf16[64,4,128]{2,1,0:T(4,128)(2,1)S(1)}, u32[]{:S(2)}, u32[]{:S(2)}) async-start(bf16[64,4,128]{2,1,0:T(4,128)(2,1)} %bitcast.17), calls=%async_computation | async-start | bytes 131072 | tf_op jit(solution)/shard_map/all_to_all | solution.py:141
  43.5 0.2 all-gather.2.cloned.1.call-start
  43.8 0.3 fusion.73
  44.0 0.3 fusion.72
  44.3 0.6 copy-done.4
  44.9 7.7 %all-to-all-done = bf16[64,4,128]{2,1,0:T(4,128)(2,1)S(1)} async-done(((bf16[64,4,128]{2,1,0:T(4,128)(2,1)}), bf16[64,4,128]{2,1,0:T(4,128)(2,1)S(1)}, u32[]{:S(2)}, u32[]{:S(2)}) %all-to-all-start) | async-done | bytes 65568 | tf_op jit(solution)/shard_map/all_to_all | solution.py:141
  52.6 0.5 fusion.1
  53.2 0.5 convolution_bitcast_fusion.1
  53.8 0.8 fusion.60
  54.5 0.8 fusion.55
  55.3 0.8 convolution_add_fusion.2
  56.1 0.8 multiply_add_fusion
  56.8 0.7 fusion.41
  57.5 0.6 convolution_add_fusion
  58.2 0.6 fusion.51
  58.8 0.6 convolution_subtract_fusion
  59.5 0.4 fusion.12
  59.9 0.4 fusion.4
  60.3 0.7 copy.80
  61.0 5.4 %all-to-all-start.1 = ((bf16[64,4,128]{2,1,0:T(4,128)(2,1)}), bf16[64,4,128]{2,1,0:T(4,128)(2,1)S(1)}, u32[]{:S(2)}, u32[]{:S(2)}) async-start(bf16[64,4,128]{2,1,0:T(4,128)(2,1)} %copy.80), calls=%async_computation.1 | async-start | bytes 131072 | tf_op jit(solution)/shard_map/all_to_all | solution.py:145
  66.4 0.1 copy.56
  66.7 9.0 %all-to-all-done.1 = bf16[64,4,128]{2,1,0:T(4,128)(2,1)S(1)} async-done(((bf16[64,4,128]{2,1,0:T(4,128)(2,1)}), bf16[64,4,128]{2,1,0:T(4,128)(2,1)S(1)}, u32[]{:S(2)}, u32[]{:S(2)}) %all-to-all-start.1) | async-done | bytes 65568 | tf_op jit(solution)/shard_map/all_to_all | solution.py:145
  75.7 0.2 fusion.30
  76.0 0.8 broadcast_in_dim.2
  76.9 6.8 %all-to-all-start.2 = ((bf16[8,128,256]{2,1,0:T(8,128)(2,1)}), bf16[8,128,256]{2,1,0:T(8,128)(2,1)S(1)}, u32[]{:S(2)}, u32[]{:S(2)}) async-start(bf16[8,128,256]{2,1,0:T(8,128)(2,1)} %broadcast_in_dim.2), calls=%async_computation.2 | async-start | bytes 1048576 | tf_op jit(solution)/shard_map/all_to_all | solution.py:148
  83.6 17.8 %all-to-all-done.2 = bf16[8,128,256]{2,1,0:T(8,128)(2,1)S(1)} async-done(((bf16[8,128,256]{2,1,0:T(8,128)(2,1)}), bf16[8,128,256]{2,1,0:T(8,128)(2,1)S(1)}, u32[]{:S(2)}, u32[]{:S(2)}) %all-to-all-start.2) | async-done | bytes 524320 | tf_op jit(solution)/shard_map/all_to_all | solution.py:148
  101.4 68.3 %all-gather.2.cloned.1.call-done = bf16[2048,256]{1,0:T(8,128)(2,1)} async-done(((bf16[32,256]{1,0:T(8,128)(2,1)}), bf16[2048,256]{1,0:T(8,128)(2,1)}) %all-gather.2.cloned.1.call-update) | async-done | bytes 1048592 | tf_op jit(solution)/shard_map/all_gather | solution.py:132
  169.7 1.5 convolution_bitcast_fusion.2
  171.2 2.3 %collective-permute-start.2 = (f32[128,256]{1,0:T(8,128)S(1)}, f32[128,256]{1,0:T(8,128)S(1)}, u32[]{:S(2)}, u32[]{:S(2)}) collective-permute-start(f32[128,256]{1,0:T(8,128)S(1)} %convolution_bitcast_fusion.2), channel_id=1, source_target_pairs={{0,1},{1,0},{2,3},{3,2},{4,5},{5,4},{6,7},{7,6},{8,9},{9,8},{10,11... | collective-permute-start | bytes 393224 | tf_op jit(solution)/shard_map/ppermute | solution.py:114
  173.5 0.3 convolution_bitcast_fusion.3
  173.8 11.6 %collective-permute-done.2 = f32[128,256]{1,0:T(8,128)S(1)} collective-permute-done((f32[128,256]{1,0:T(8,128)S(1)}, f32[128,256]{1,0:T(8,128)S(1)}, u32[]{:S(2)}, u32[]{:S(2)}) %collective-permute-start.2) | collective-permute-done | bytes 131104 | tf_op jit(solution)/shard_map/ppermute | solution.py:114
  185.4 0.6 add_convert_fusion
  (29 shorter events, 1.0 us)
Async XLA Ops:
  6.5 4.3 %copy-start = (bf16[4096,256]{1,0:T(8,128)(2,1)S(1)}, bf16[4096,256]{1,0:T(8,128)(2,1)}, u32[]{:S(2)}) copy-start(bf16[4096,256]{1,0:T(8,128)(2,1)} %param.13) | copy-start | bytes 6291460
  6.5 7.5 %copy-start.1 = (f32[4,8192]{1,0:T(4,128)S(1)}, f32[4,8192]{1,0:T(4,128)}, u32[]{:S(2)}) copy-start(f32[4,8192]{1,0:T(4,128)} %param.11) | copy-start | bytes 393220
  8.9 11.5 %collective-permute-start = (bf16[3,2,256]{1,2,0:T(8,128)(2,1)}, bf16[3,2,256]{1,2,0:T(8,128)(2,1)S(1)}, u32[]{:S(2)}, u32[]{:S(2)}) collective-permute-start(bf16[3,2,256]{1,2,0:T(8,128)(2,1)} %copy.55), channel_id=1, source_target_pairs={{0,16},{16,32},{32,48},{48,64},{64,80},{80,96},{96,112},{112,128},... | collective-permute-start | bytes 9224 | tf_op jit(solution)/shard_map/ppermute | solution.py:14
  11.6 32.7 %collective-permute-start.1 = (bf16[32,256]{1,0:T(8,128)(2,1)}, bf16[32,256]{1,0:T(8,128)(2,1)S(1)}, u32[]{:S(2)}, u32[]{:S(2)}) collective-permute-start(bf16[32,256]{1,0:T(8,128)(2,1)} %constant_dynamic-slice_fusion), channel_id=1, source_target_pairs={{0,1},{1,0},{2,3},{3,2},{4,5},{5,4},{6,7},{7,6},{8,9},{9,8},{10,11... | collective-permute-start | bytes 49160 | tf_op jit(solution)/shard_map/ppermute | solution.py:114
  16.3 3.1 %copy-start.5 = (f32[3,3,256]{2,1,0:T(4,128)S(1)}, f32[3,3,256]{2,1,0:T(4,128)}, u32[]{:S(2)}) copy-start(f32[3,3,256]{2,1,0:T(4,128)} %param.10) | copy-start | bytes 27652
  16.3 3.1 %copy-start.2 = (bf16[128,256]{1,0:T(8,128)(2,1)S(1)}, bf16[128,256]{1,0:T(8,128)(2,1)}, u32[]{:S(2)}) copy-start(bf16[128,256]{1,0:T(8,128)(2,1)} %param.9) | copy-start | bytes 196612
  21.7 30.9 %all-to-all-start = ((bf16[64,4,128]{2,1,0:T(4,128)(2,1)}), bf16[64,4,128]{2,1,0:T(4,128)(2,1)S(1)}, u32[]{:S(2)}, u32[]{:S(2)}) async-start(bf16[64,4,128]{2,1,0:T(4,128)(2,1)} %bitcast.17), calls=%async_computation | async-start | bytes 131072 | tf_op jit(solution)/shard_map/all_to_all | solution.py:141
  43.5 126.1 %all-gather.2.cloned.1.call-start = ((), (), s32[]{:S(2)}) async-start(), calls=%async_computation.3 | async-start | bytes 1064960 | tf_op jit(solution)/shard_map/all_gather | solution.py:132
  44.3 0.6 copy-start.4
  56.8 3.1 %copy-start.6 = (f32[4]{0:T(128)S(1)}, f32[4]{0:T(128)}, u32[]{:S(2)}) copy-start(f32[4]{0:T(128)} %param.12) | copy-start | bytes 52
  57.5 8.9 %copy-start.3 = (bf16[128,256]{1,0:T(8,128)(2,1)S(1)}, bf16[128,256]{1,0:T(8,128)(2,1)}, u32[]{:S(2)}) copy-start(bf16[128,256]{1,0:T(8,128)(2,1)} %param.7) | copy-start | bytes 196612
  61.0 14.7 %all-to-all-start.1 = ((bf16[64,4,128]{2,1,0:T(4,128)(2,1)}), bf16[64,4,128]{2,1,0:T(4,128)(2,1)S(1)}, u32[]{:S(2)}, u32[]{:S(2)}) async-start(bf16[64,4,128]{2,1,0:T(4,128)(2,1)} %copy.80), calls=%async_computation.1 | async-start | bytes 131072 | tf_op jit(solution)/shard_map/all_to_all | solution.py:145
  76.9 24.5 %all-to-all-start.2 = ((bf16[8,128,256]{2,1,0:T(8,128)(2,1)}), bf16[8,128,256]{2,1,0:T(8,128)(2,1)S(1)}, u32[]{:S(2)}, u32[]{:S(2)}) async-start(bf16[8,128,256]{2,1,0:T(8,128)(2,1)} %broadcast_in_dim.2), calls=%async_computation.2 | async-start | bytes 1048576 | tf_op jit(solution)/shard_map/all_to_all | solution.py:148
  171.2 14.2 %collective-permute-start.2 = (f32[128,256]{1,0:T(8,128)S(1)}, f32[128,256]{1,0:T(8,128)S(1)}, u32[]{:S(2)}, u32[]{:S(2)}) collective-permute-start(f32[128,256]{1,0:T(8,128)S(1)} %convolution_bitcast_fusion.2), channel_id=1, source_target_pairs={{0,1},{1,0},{2,3},{3,2},{4,5},{5,4},{6,7},{7,6},{8,9},{9,8},{10,11... | collective-permute-start | bytes 393224 | tf_op jit(solution)/shard_map/ppermute | solution.py:114
Sparse Core Ops, SparseCore 0:
  47.1 122.5 all-gather.1

commit v5 on v2

--- a/solution.py
+++ b/solution.py
@@ -118,39 +118,43 @@
     mine_x = me // 2
     mine_h = me % 2
     partner = lax.ppermute(block, "chan", [(i, i ^ 1) for i in range(size)])
-    held = jnp.stack([block, partner])
-    slots = [held]
+    moving = jnp.stack([block, partner])
+    slots = [moving]
     places = [mine_x]
-    right = held
-    left = held
-    for step in range(1, pairs // 2 + 1):
-        right = lax.ppermute(right, "chan", chan_route(size, 1))
-        slots.append(right)
+    for step in range(1, pairs):
+        moving = lax.ppermute(moving, "chan", chan_route(size, 1))
+        slots.append(moving)
         places.append((mine_x - step) % pairs)
-        if step < pairs - step:
-            left = lax.ppermute(left, "chan", chan_route(size, -1))
-            slots.append(left)
-            places.append((mine_x + step) % pairs)
     place = jnp.stack(places)
     order = jnp.stack([place * 2 + mine_h, place * 2 + (1 - mine_h)], axis=1)
     return jnp.stack(slots), order
+
+
+def causal_filter(signal, taps):
+    length = signal.shape[-1]
+    total = taps[0][:, None] * signal
+    for offset in range(1, taps.shape[0]):
+        moved = jnp.concatenate(
+            [jnp.zeros(signal.shape[:-1] + (offset,), signal.dtype), signal[..., : length - offset]], -1
+        )
+        total = total + taps[offset][:, None] * moved
+    return total
 
 
 def body(queries, keys, values, short_taps, long_filter, skip_gain, out_weight):
     rows, width = queries.shape
     span = short_taps.shape[1]
     edge = rows - (span - 1)
-    tails = shifted(jnp.stack([queries[edge:], keys[edge:], values[edge:]]), "seq", 1)
-    short_q = shifted_filter(queries, tails[0], short_taps[0]).astype(jnp.bfloat16)
-    mixed = (
-        shifted_filter(keys, tails[1], short_taps[1])
-        * shifted_filter(values, tails[2], short_taps[2])
-    ).astype(jnp.bfloat16)
     groups = lax.axis_size("seq")
     per_group = width // groups
-    mixed_t = mixed.T.reshape(groups, per_group, rows)
-    split_mixed = lax.all_to_all(mixed_t, "seq", split_axis=0, concat_axis=0, tiled=True)
-    signal = split_mixed.transpose(1, 0, 2).reshape(per_group, groups * rows)
+    seq_index = lax.axis_index("seq")
+    raw = jnp.stack([keys.T, values.T]).reshape(2, groups, per_group, rows).transpose(1, 0, 2, 3)
+    split_raw = lax.all_to_all(raw, "seq", split_axis=0, concat_axis=0, tiled=True)
+    whole = split_raw.transpose(1, 2, 0, 3).reshape(2, per_group, groups * rows).astype(jnp.float32)
+    own_taps = lax.dynamic_slice_in_dim(short_taps, seq_index * per_group, per_group, axis=2)
+    signal = (causal_filter(whole[0], own_taps[1]) * causal_filter(whole[1], own_taps[2])).astype(jnp.bfloat16)
+    tail = shifted(queries[edge:], "seq", 1)
+    short_q = shifted_filter(queries, tail, short_taps[0]).astype(jnp.bfloat16)
     convolved = long_convolution(signal, long_filter, skip_gain).astype(jnp.bfloat16)
     outgoing = convolved.reshape(per_group, groups, rows).transpose(1, 0, 2)
     returned = lax.all_to_all(outgoing, "seq", split_axis=0, concat_axis=0, tiled=True)

time: 112 us -> 142 us (1.27)
  the two profiles are of different devices: /device:TPU:24 before, /device:TPU:112 now
where the time goes in v5:
time: 142 us; the launch traced here: 141 us
  waiting for transfers between devices  56.8 us (40%)
  starting transfers between devices  53.4 us (38%)
  matrix products  13.7 us (10%)
  local copies, waits for them, and re-layouts  10.6 us (7%)
  other arithmetic  5.86 us (4%)
    ppermute x7, waiting for transfers between devices, gather_chan(): moving = lax.ppermute(moving, 'chan', chan_route(size, 1))  40.8 us
    all_to_all x1, starting transfers between devices, body(): lax.all_to_all(raw, 'seq', split_axis=0, concat_axis=0, tiled=True)  23.9 us
    ppermute x7, starting transfers between devices, gather_chan(): moving = lax.ppermute(moving, 'chan', chan_route(size, 1))  15.1 us
    all_to_all x1, starting transfers between devices, body(): lax.all_to_all(outgoing, 'seq', split_axis=0, concat_axis=0, tiled=True)  10.6 us
    ppermute x1, waiting for transfers between devices, gather_chan(): partner = lax.ppermute(block, 'chan', [(i, i ^ 1) for i in range(size)])  9.05 us
    all_to_all x1, waiting for transfers between devices, body(): lax.all_to_all(outgoing, 'seq', split_axis=0, concat_axis=0, tiled=True)  6.96 us
    unnamed x24, local copies, waits for them, and re-layouts  2.97 us
  transfers between devices with their start and end apart: 11, of which 9 were waited for; matrix products, arithmetic and copies ran while one was open for 19% of the time, Pallas kernels for 0%

profile of v5, /device:TPU:112, one launch (start us, length us, event | category | flops | bytes accessed | tf_op | source)
XLA Modules:
  0.0 140.9 jit_solution(9263093456845990023)
XLA Ops:
  0.0 1.4 %slice.87 = bf16[2,256]{1,0:T(2,128)(2,1)} slice(bf16[128,256]{1,0:T(8,128)(2,1)} %param.7), slice={[126:128], [0:256]} | slice | bytes 2048 | tf_op jit(solution)/shard_map/slice | solution.py:156
  1.4 1.9 %collective-permute-start = (bf16[2,256]{1,0:T(2,128)(2,1)}, bf16[2,256]{1,0:T(2,128)(2,1)}, u32[]{:S(2)}, u32[]{:S(2)}) collective-permute-start(bf16[2,256]{1,0:T(2,128)(2,1)} %slice.87), channel_id=1, source_target_pairs={{0,16},{16,32},{32,48},{48,64},{64,80},{80,96},{96,112},{112,128},... | collective-permute-start | bytes 3080 | tf_op jit(solution)/shard_map/ppermute | solution.py:14
  3.3 1.0 copy.52
  4.3 1.0 copy.53
  5.4 0.7 copy.54
  6.1 23.9 %all-to-all-start = ((bf16[64,2,4,128]{3,2,1,0:T(4,128)(2,1)}), bf16[64,2,4,128]{3,2,1,0:T(4,128)(2,1)}, u32[]{:S(2)}, u32[]{:S(2)}) async-start(bf16[64,2,4,128]{3,2,1,0:T(4,128)(2,1)} %copy.54), calls=%async_computation | async-start | bytes 262144 | tf_op jit(solution)/shard_map/all_to_all | solution.py:152
  30.0 0.9 fusion.67
  30.9 0.9 fusion.66
  32.3 0.9 pad_bitcast_fusion
  33.2 0.7 fusion
  34.0 0.7 convolution_bitcast_fusion
  34.9 0.8 fusion.46
  35.6 0.8 fusion.50
  36.4 0.8 fusion.148
  37.2 0.8 convolution_subtract_fusion.1
  38.0 1.5 %dynamic-slice_bitcast_fusion.5 = (f32[4]{0:T(128)S(1)}, f32[4]{0:T(128)}, f32[4]{0:T(128)}, f32[4]{0:T(128)}, f32[4]{0:T(128)}, /*index=5*/f32[4]{0:T(128)}) fusion(f32[3,3,256]{2,1,0:T(4,128)} %param.10, s32[]{:T(128)S(6)} %add.256, s32[]{:T(128)S(6)} %select_n.127, s32[]{:T(128)S(6)} %add.260), kind=kLoop, calls=%fused_computation.124 | loop fusion | bytes 204 | tf_op jit(solution)/shard_map/mul | solution.py:135
  40.1 0.8 convolution_add_fusion.1
  40.9 0.9 convert_bitcast_fusion
  41.9 1.0 fusion.63
  42.9 0.7 fusion.1
  43.7 0.7 convolution_bitcast_fusion.1
  44.4 0.8 fusion.48
  45.2 0.8 fusion.53
  45.9 0.8 convolution_add_fusion.2
  46.7 0.8 multiply_add_fusion
  48.2 0.8 fusion.44
  51.3 0.7 fusion.33
  52.0 10.6 %all-to-all-start.1 = ((bf16[64,4,128]{2,1,0:T(4,128)(2,1)}), bf16[64,4,128]{2,1,0:T(4,128)(2,1)S(1)}, u32[]{:S(2)}, u32[]{:S(2)}) async-start(bf16[64,4,128]{2,1,0:T(4,128)(2,1)} %fusion.33), calls=%async_computation.1 | async-start | bytes 131072 | tf_op jit(solution)/shard_map/all_to_all | solution.py:160
  62.7 0.7 maximum_convert_fusion
  63.3 7.0 %all-to-all-done.1 = bf16[64,4,128]{2,1,0:T(4,128)(2,1)S(1)} async-done(((bf16[64,4,128]{2,1,0:T(4,128)(2,1)}), bf16[64,4,128]{2,1,0:T(4,128)(2,1)S(1)}, u32[]{:S(2)}, u32[]{:S(2)}) %all-to-all-start.1) | async-done | bytes 65568 | tf_op jit(solution)/shard_map/all_to_all | solution.py:160
  70.5 1.9 %collective-permute-start.1 = (bf16[128,256]{1,0:T(8,128)(2,1)S(1)}, bf16[128,256]{1,0:T(8,128)(2,1)S(1)}, u32[]{:S(2)}, u32[]{:S(2)}) collective-permute-start(bf16[128,256]{1,0:T(8,128)(2,1)S(1)} %fusion.24), channel_id=1, source_target_pairs={{0,1},{1,0},{2,3},{3,2},{4,5},{5,4},{6,7},{7,6},{8,9},{9,8},{10,11... | collective-permute-start | bytes 196616 | tf_op jit(solution)/shard_map/ppermute | solution.py:120
  72.6 9.1 %collective-permute-done.1 = bf16[128,256]{1,0:T(8,128)(2,1)S(1)} collective-permute-done((bf16[128,256]{1,0:T(8,128)(2,1)S(1)}, bf16[128,256]{1,0:T(8,128)(2,1)S(1)}, u32[]{:S(2)}, u32[]{:S(2)}) %collective-permute-start.1) | collective-permute-done | bytes 65568 | tf_op jit(solution)/shard_map/ppermute | solution.py:120
  81.7 3.4 %collective-permute-start.2 = (bf16[2,128,256]{2,1,0:T(8,128)(2,1)S(1)}, bf16[2,128,256]{2,1,0:T(8,128)(2,1)S(1)}, u32[]{:S(2)}, u32[]{:S(2)}) collective-permute-start(bf16[2,128,256]{2,1,0:T(8,128)(2,1)S(1)} %pad_maximum_fusion), channel_id=1, source_target_pairs={{0,2},{1,3},{2,4},{3,5},{4,6},{5,7},{6,8},{7,9},{8,10},{9,11},{10,... | collective-permute-start | bytes 393224 | tf_op jit(solution)/shard_map/ppermute | solution.py:125
  85.1 2.0 %gather_fusion = bf16[16,256,256]{2,1,0:T(8,128)(2,1)} fusion(bf16[16,256,256]{2,1,0:T(8,128)(2,1)S(1)} %bitcast.166, s32[1024]{0:T(1024)S(1)} %pad_clamp_fusion), kind=kCustom, calls=%fused_computation | custom fusion | bytes 4194368 | tf_op jit(solution)/shard_map/gather | solution.py:164
  87.1 2.6 %collective-permute-done.2 = bf16[2,128,256]{2,1,0:T(8,128)(2,1)S(1)} collective-permute-done((bf16[2,128,256]{2,1,0:T(8,128)(2,1)S(1)}, bf16[2,128,256]{2,1,0:T(8,128)(2,1)S(1)}, u32[]{:S(2)}, u32[]{:S(2)}) %collective-permute-start.2) | collective-permute-done | bytes 131104 | tf_op jit(solution)/shard_map/ppermute | solution.py:125
  89.7 2.2 %collective-permute-start.3 = (bf16[2,128,256]{2,1,0:T(8,128)(2,1)S(1)}, bf16[2,128,256]{2,1,0:T(8,128)(2,1)S(1)}, u32[]{:S(2)}, u32[]{:S(2)}) collective-permute-start(bf16[2,128,256]{2,1,0:T(8,128)(2,1)S(1)} %collective-permute-done.2), channel_id=1, source_target_pairs={{0,2},{1,3},{2,4},{3,5},{4,6},{5,7},{6,8},{7,9},{8,10},{9,11},{10,... | collective-permute-start | bytes 393224 | tf_op jit(solution)/shard_map/ppermute | solution.py:125
  91.9 5.8 %collective-permute-done.3 = bf16[2,128,256]{2,1,0:T(8,128)(2,1)S(1)} collective-permute-done((bf16[2,128,256]{2,1,0:T(8,128)(2,1)S(1)}, bf16[2,128,256]{2,1,0:T(8,128)(2,1)S(1)}, u32[]{:S(2)}, u32[]{:S(2)}) %collective-permute-start.3) | collective-permute-done | bytes 131104 | tf_op jit(solution)/shard_map/ppermute | solution.py:125
  97.8 1.9 %collective-permute-start.4 = (bf16[2,128,256]{2,1,0:T(8,128)(2,1)S(1)}, bf16[2,128,256]{2,1,0:T(8,128)(2,1)S(1)}, u32[]{:S(2)}, u32[]{:S(2)}) collective-permute-start(bf16[2,128,256]{2,1,0:T(8,128)(2,1)S(1)} %collective-permute-done.3), channel_id=1, source_target_pairs={{0,2},{1,3},{2,4},{3,5},{4,6},{5,7},{6,8},{7,9},{8,10},{9,11},{10,... | collective-permute-start | bytes 393224 | tf_op jit(solution)/shard_map/ppermute | solution.py:125
  99.7 6.1 %collective-permute-done.4 = bf16[2,128,256]{2,1,0:T(8,128)(2,1)S(1)} collective-permute-done((bf16[2,128,256]{2,1,0:T(8,128)(2,1)S(1)}, bf16[2,128,256]{2,1,0:T(8,128)(2,1)S(1)}, u32[]{:S(2)}, u32[]{:S(2)}) %collective-permute-start.4) | collective-permute-done | bytes 131104 | tf_op jit(solution)/shard_map/ppermute | solution.py:125
  105.9 1.9 %collective-permute-start.5 = (bf16[2,128,256]{2,1,0:T(8,128)(2,1)S(1)}, bf16[2,128,256]{2,1,0:T(8,128)(2,1)S(1)}, u32[]{:S(2)}, u32[]{:S(2)}) collective-permute-start(bf16[2,128,256]{2,1,0:T(8,128)(2,1)S(1)} %collective-permute-done.4), channel_id=1, source_target_pairs={{0,2},{1,3},{2,4},{3,5},{4,6},{5,7},{6,8},{7,9},{8,10},{9,11},{10,... | collective-permute-start | bytes 393224 | tf_op jit(solution)/shard_map/ppermute | solution.py:125
  107.8 7.3 %collective-permute-done.5 = bf16[2,128,256]{2,1,0:T(8,128)(2,1)S(1)} collective-permute-done((bf16[2,128,256]{2,1,0:T(8,128)(2,1)S(1)}, bf16[2,128,256]{2,1,0:T(8,128)(2,1)S(1)}, u32[]{:S(2)}, u32[]{:S(2)}) %collective-permute-start.5) | collective-permute-done | bytes 131104 | tf_op jit(solution)/shard_map/ppermute | solution.py:125
  115.1 1.9 %collective-permute-start.6 = (bf16[2,128,256]{2,1,0:T(8,128)(2,1)S(1)}, bf16[2,128,256]{2,1,0:T(8,128)(2,1)S(1)}, u32[]{:S(2)}, u32[]{:S(2)}) collective-permute-start(bf16[2,128,256]{2,1,0:T(8,128)(2,1)S(1)} %collective-permute-done.5), channel_id=1, source_target_pairs={{0,2},{1,3},{2,4},{3,5},{4,6},{5,7},{6,8},{7,9},{8,10},{9,11},{10,... | collective-permute-start | bytes 393224 | tf_op jit(solution)/shard_map/ppermute | solution.py:125
  117.0 6.7 %collective-permute-done.6 = bf16[2,128,256]{2,1,0:T(8,128)(2,1)S(1)} collective-permute-done((bf16[2,128,256]{2,1,0:T(8,128)(2,1)S(1)}, bf16[2,128,256]{2,1,0:T(8,128)(2,1)S(1)}, u32[]{:S(2)}, u32[]{:S(2)}) %collective-permute-start.6) | collective-permute-done | bytes 131104 | tf_op jit(solution)/shard_map/ppermute | solution.py:125
  123.7 1.9 %collective-permute-start.7 = (bf16[2,128,256]{2,1,0:T(8,128)(2,1)S(1)}, bf16[2,128,256]{2,1,0:T(8,128)(2,1)S(1)}, u32[]{:S(2)}, u32[]{:S(2)}) collective-permute-start(bf16[2,128,256]{2,1,0:T(8,128)(2,1)S(1)} %collective-permute-done.6), channel_id=1, source_target_pairs={{0,2},{1,3},{2,4},{3,5},{4,6},{5,7},{6,8},{7,9},{8,10},{9,11},{10,... | collective-permute-start | bytes 393224 | tf_op jit(solution)/shard_map/ppermute | solution.py:125
  125.6 6.1 %collective-permute-done.7 = bf16[2,128,256]{2,1,0:T(8,128)(2,1)S(1)} collective-permute-done((bf16[2,128,256]{2,1,0:T(8,128)(2,1)S(1)}, bf16[2,128,256]{2,1,0:T(8,128)(2,1)S(1)}, u32[]{:S(2)}, u32[]{:S(2)}) %collective-permute-start.7) | collective-permute-done | bytes 131104 | tf_op jit(solution)/shard_map/ppermute | solution.py:125
  131.7 1.9 %collective-permute-start.8 = (bf16[2,128,256]{2,1,0:T(8,128)(2,1)S(1)}, bf16[2,128,256]{2,1,0:T(8,128)(2,1)S(1)}, u32[]{:S(2)}, u32[]{:S(2)}) collective-permute-start(bf16[2,128,256]{2,1,0:T(8,128)(2,1)S(1)} %collective-permute-done.7), channel_id=1, source_target_pairs={{0,2},{1,3},{2,4},{3,5},{4,6},{5,7},{6,8},{7,9},{8,10},{9,11},{10,... | collective-permute-start | bytes 393224 | tf_op jit(solution)/shard_map/ppermute | solution.py:125
  133.7 6.1 %collective-permute-done.8 = bf16[2,128,256]{2,1,0:T(8,128)(2,1)S(1)} collective-permute-done((bf16[2,128,256]{2,1,0:T(8,128)(2,1)S(1)}, bf16[2,128,256]{2,1,0:T(8,128)(2,1)S(1)}, u32[]{:S(2)}, u32[]{:S(2)}) %collective-permute-start.8) | collective-permute-done | bytes 131104 | tf_op jit(solution)/shard_map/ppermute | solution.py:125
  139.8 1.1 fusion.4
  (45 shorter events, 4.8 us)
Async XLA Ops:
  0.0 85.1 %copy-start = (bf16[4096,256]{1,0:T(8,128)(2,1)S(1)}, bf16[4096,256]{1,0:T(8,128)(2,1)}, u32[]{:S(2)}) copy-start(bf16[4096,256]{1,0:T(8,128)(2,1)} %param.13) | copy-start | bytes 6291460
  1.4 61.2 %collective-permute-start = (bf16[2,256]{1,0:T(2,128)(2,1)}, bf16[2,256]{1,0:T(2,128)(2,1)}, u32[]{:S(2)}, u32[]{:S(2)}) collective-permute-start(bf16[2,256]{1,0:T(2,128)(2,1)} %slice.87), channel_id=1, source_target_pairs={{0,16},{16,32},{32,48},{48,64},{64,80},{80,96},{96,112},{112,128},... | collective-permute-start | bytes 3080 | tf_op jit(solution)/shard_map/ppermute | solution.py:14
  6.1 34.8 %all-to-all-start = ((bf16[64,2,4,128]{3,2,1,0:T(4,128)(2,1)}), bf16[64,2,4,128]{3,2,1,0:T(4,128)(2,1)}, u32[]{:S(2)}, u32[]{:S(2)}) async-start(bf16[64,2,4,128]{3,2,1,0:T(4,128)(2,1)} %copy.54), calls=%async_computation | async-start | bytes 262144 | tf_op jit(solution)/shard_map/all_to_all | solution.py:152
  46.7 3.6 %copy-start.2 = (f32[128,128]{1,0:T(8,128)S(1)}, f32[128,128]{1,0:T(8,128)}, u32[]{:S(2)}) copy-start(f32[128,128]{1,0:T(8,128)} %fusion.67) | copy-start | bytes 196612
  47.5 3.3 %copy-start.3 = (f32[128,128]{1,0:T(8,128)S(1)}, f32[128,128]{1,0:T(8,128)}, u32[]{:S(2)}) copy-start(f32[128,128]{1,0:T(8,128)} %fusion.66) | copy-start | bytes 196612
  47.5 3.8 %copy-start.6 = (f32[4]{0:T(128)S(1)}, f32[4]{0:T(128)}, u32[]{:S(2)}) copy-start(f32[4]{0:T(128)} %param.12) | copy-start | bytes 52
  48.2 14.4 %copy-start.5 = (s32[8,1]{0,1:T(1,128)S(1)}, s32[8,1]{0,1:T(1,128)}, u32[]{:S(2)}) copy-start(s32[8,1]{0,1:T(1,128)} %stack.104) | copy-start | bytes 100
  48.2 14.5 %copy-start.4 = (bf16[128,256]{1,0:T(8,128)(2,1)S(1)}, bf16[128,256]{1,0:T(8,128)(2,1)}, u32[]{:S(2)}) copy-start(bf16[128,256]{1,0:T(8,128)(2,1)} %param.7) | copy-start | bytes 196612
  52.0 18.3 %all-to-all-start.1 = ((bf16[64,4,128]{2,1,0:T(4,128)(2,1)}), bf16[64,4,128]{2,1,0:T(4,128)(2,1)S(1)}, u32[]{:S(2)}, u32[]{:S(2)}) async-start(bf16[64,4,128]{2,1,0:T(4,128)(2,1)} %fusion.33), calls=%async_computation.1 | async-start | bytes 131072 | tf_op jit(solution)/shard_map/all_to_all | solution.py:160
  70.5 11.2 %collective-permute-start.1 = (bf16[128,256]{1,0:T(8,128)(2,1)S(1)}, bf16[128,256]{1,0:T(8,128)(2,1)S(1)}, u32[]{:S(2)}, u32[]{:S(2)}) collective-permute-start(bf16[128,256]{1,0:T(8,128)(2,1)S(1)} %fusion.24), channel_id=1, source_target_pairs={{0,1},{1,0},{2,3},{3,2},{4,5},{5,4},{6,7},{7,6},{8,9},{9,8},{10,11... | collective-permute-start | bytes 196616 | tf_op jit(solution)/shard_map/ppermute | solution.py:120
  81.7 8.1 %collective-permute-start.2 = (bf16[2,128,256]{2,1,0:T(8,128)(2,1)S(1)}, bf16[2,128,256]{2,1,0:T(8,128)(2,1)S(1)}, u32[]{:S(2)}, u32[]{:S(2)}) collective-permute-start(bf16[2,128,256]{2,1,0:T(8,128)(2,1)S(1)} %pad_maximum_fusion), channel_id=1, source_target_pairs={{0,2},{1,3},{2,4},{3,5},{4,6},{5,7},{6,8},{7,9},{8,10},{9,11},{10,... | collective-permute-start | bytes 393224 | tf_op jit(solution)/shard_map/ppermute | solution.py:125
  87.1 52.7 %copy-start.1 = (bf16[16,256,256]{2,1,0:T(8,128)(2,1)S(1)}, bf16[16,256,256]{2,1,0:T(8,128)(2,1)}, u32[]{:S(2)}) copy-start(bf16[16,256,256]{2,1,0:T(8,128)(2,1)} %gather_fusion) | copy-start | bytes 6291460
  89.7 8.1 %collective-permute-start.3 = (bf16[2,128,256]{2,1,0:T(8,128)(2,1)S(1)}, bf16[2,128,256]{2,1,0:T(8,128)(2,1)S(1)}, u32[]{:S(2)}, u32[]{:S(2)}) collective-permute-start(bf16[2,128,256]{2,1,0:T(8,128)(2,1)S(1)} %collective-permute-done.2), channel_id=1, source_target_pairs={{0,2},{1,3},{2,4},{3,5},{4,6},{5,7},{6,8},{7,9},{8,10},{9,11},{10,... | collective-permute-start | bytes 393224 | tf_op jit(solution)/shard_map/ppermute | solution.py:125
  97.8 8.1 %collective-permute-start.4 = (bf16[2,128,256]{2,1,0:T(8,128)(2,1)S(1)}, bf16[2,128,256]{2,1,0:T(8,128)(2,1)S(1)}, u32[]{:S(2)}, u32[]{:S(2)}) collective-permute-start(bf16[2,128,256]{2,1,0:T(8,128)(2,1)S(1)} %collective-permute-done.3), channel_id=1, source_target_pairs={{0,2},{1,3},{2,4},{3,5},{4,6},{5,7},{6,8},{7,9},{8,10},{9,11},{10,... | collective-permute-start | bytes 393224 | tf_op jit(solution)/shard_map/ppermute | solution.py:125
  105.9 9.2 %collective-permute-start.5 = (bf16[2,128,256]{2,1,0:T(8,128)(2,1)S(1)}, bf16[2,128,256]{2,1,0:T(8,128)(2,1)S(1)}, u32[]{:S(2)}, u32[]{:S(2)}) collective-permute-start(bf16[2,128,256]{2,1,0:T(8,128)(2,1)S(1)} %collective-permute-done.4), channel_id=1, source_target_pairs={{0,2},{1,3},{2,4},{3,5},{4,6},{5,7},{6,8},{7,9},{8,10},{9,11},{10,... | collective-permute-start | bytes 393224 | tf_op jit(solution)/shard_map/ppermute | solution.py:125
  115.1 8.6 %collective-permute-start.6 = (bf16[2,128,256]{2,1,0:T(8,128)(2,1)S(1)}, bf16[2,128,256]{2,1,0:T(8,128)(2,1)S(1)}, u32[]{:S(2)}, u32[]{:S(2)}) collective-permute-start(bf16[2,128,256]{2,1,0:T(8,128)(2,1)S(1)} %collective-permute-done.5), channel_id=1, source_target_pairs={{0,2},{1,3},{2,4},{3,5},{4,6},{5,7},{6,8},{7,9},{8,10},{9,11},{10,... | collective-permute-start | bytes 393224 | tf_op jit(solution)/shard_map/ppermute | solution.py:125
  123.7 8.1 %collective-permute-start.7 = (bf16[2,128,256]{2,1,0:T(8,128)(2,1)S(1)}, bf16[2,128,256]{2,1,0:T(8,128)(2,1)S(1)}, u32[]{:S(2)}, u32[]{:S(2)}) collective-permute-start(bf16[2,128,256]{2,1,0:T(8,128)(2,1)S(1)} %collective-permute-done.6), channel_id=1, source_target_pairs={{0,2},{1,3},{2,4},{3,5},{4,6},{5,7},{6,8},{7,9},{8,10},{9,11},{10,... | collective-permute-start | bytes 393224 | tf_op jit(solution)/shard_map/ppermute | solution.py:125
  131.7 8.1 %collective-permute-start.8 = (bf16[2,128,256]{2,1,0:T(8,128)(2,1)S(1)}, bf16[2,128,256]{2,1,0:T(8,128)(2,1)S(1)}, u32[]{:S(2)}, u32[]{:S(2)}) collective-permute-start(bf16[2,128,256]{2,1,0:T(8,128)(2,1)S(1)} %collective-permute-done.7), channel_id=1, source_target_pairs={{0,2},{1,3},{2,4},{3,5},{4,6},{5,7},{6,8},{7,9},{8,10},{9,11},{10,... | collective-permute-start | bytes 393224 | tf_op jit(solution)/shard_map/ppermute | solution.py:125

commit v6 on v1

--- a/solution.py
+++ b/solution.py
@@ -106,6 +106,26 @@
     return total
 
 
+def chan_route(size, step):
+    pairs = size // 2
+    return [(x * 2 + h, ((x + step) % pairs) * 2 + h) for x in range(pairs) for h in range(2)]
+
+
+def gather_chan(block):
+    size = lax.axis_size("chan")
+    pairs = size // 2
+    me = lax.axis_index("chan")
+    mine_x = me // 2
+    mine_h = me % 2
+    partner = lax.ppermute(block, "chan", [(i, i ^ 1) for i in range(size)])
+    shifts = [d for d in range(1 - pairs // 2, pairs // 2 + 1) if d != 0]
+    own = [block] + [lax.ppermute(block, "chan", chan_route(size, d)) for d in shifts]
+    other = [partner] + [lax.ppermute(partner, "chan", chan_route(size, d)) for d in shifts]
+    place = jnp.stack([mine_x] + [(mine_x - d) % pairs for d in shifts])
+    order = jnp.concatenate([place * 2 + mine_h, place * 2 + (1 - mine_h)])
+    return jnp.stack(own + other), order
+
+
 def body(queries, keys, values, short_taps, long_filter, skip_gain, out_weight):
     rows, width = queries.shape
     span = short_taps.shape[1]
@@ -126,8 +146,8 @@
     returned = lax.all_to_all(outgoing, "seq", split_axis=0, concat_axis=0, tiled=True)
     long_out = returned.reshape(width, rows).T
     gated = (short_q.astype(jnp.float32) * long_out.astype(jnp.float32)).astype(jnp.bfloat16)
-    pieces = lax.all_gather(gated, "chan", axis=0, tiled=False)
-    weight = out_weight.reshape(pieces.shape[0], width, out_weight.shape[1])
+    pieces, order = gather_chan(gated)
+    weight = out_weight.reshape(-1, width, out_weight.shape[1])[order]
     result = jnp.einsum("gtc,gcj->tj", pieces, weight, preferred_element_type=jnp.float32)
     return result.astype(jnp.bfloat16)
 

time: 179 us -> 159 us (0.89)
  waiting for transfers between devices: 113 us -> 41.2 us
  starting transfers between devices: 28.3 us -> 88.7 us
  between operations: 13.7 us -> 0.73 us
  local copies, waits for them, and re-layouts: 6.94 us -> 9.25 us
    all_gather x1 -> x0, waiting for transfers between devices: 94.1 us -> none  [body(): pieces = lax.all_gather(gated, 'chan', axis=0, tiled=False)]
    ppermute x0 -> x15, starting transfers between devices: none -> 60.3 us  [the longest x7 27.6 us: gather_chan(): lax.ppermute(block, 'chan', chan_route(size, d))]
    ppermute x0 -> x15, waiting for transfers between devices: none -> 22 us  [the longest x7 17.8 us: gather_chan(): lax.ppermute(partner, 'chan', chan_route(size, d))]
    gather x0 -> x1, local copies, waits for them, and re-layouts: none -> 2.03 us  [body(): weight = out_weight.reshape(-1, width, out_weight.shape[1])[order]]
  transfers between devices with their start and end apart: 4 -> 18, of which waited for: 3 -> 7; matrix products, arithmetic and copies ran while one was open for 4% -> 7% of each run, Pallas kernels for 0% -> 0%
where the time goes in v6:
time: 159 us; the launch traced here: 158 us
  starting transfers between devices  88.7 us (56%)
  waiting for transfers between devices  41.2 us (26%)
  matrix products  14.7 us (9%)
  local copies, waits for them, and re-layouts  9.25 us (6%)
  other arithmetic  3.71 us (2%)
    ppermute x7, starting transfers between devices, gather_chan(): lax.ppermute(block, 'chan', chan_route(size, d))  27.6 us
    ppermute x7, starting transfers between devices, gather_chan(): lax.ppermute(partner, 'chan', chan_route(size, d))  24.5 us
    all_to_all x1, starting transfers between devices, body(): lax.all_to_all(mixed_t, 'seq', split_axis=0, concat_axis=0, tiled=True)  21.5 us
    ppermute x7, waiting for transfers between devices, gather_chan(): lax.ppermute(partner, 'chan', chan_route(size, d))  17.8 us
    all_to_all x1, waiting for transfers between devices, body(): lax.all_to_all(outgoing, 'seq', split_axis=0, concat_axis=0, tiled=True)  9.88 us
    all_to_all x1, waiting for transfers between devices, body(): lax.all_to_all(mixed_t, 'seq', split_axis=0, concat_axis=0, tiled=True)  9.27 us
    ppermute x1, starting transfers between devices, gather_chan(): partner = lax.ppermute(block, 'chan', [(i, i ^ 1) for i in range(size)])  8.18 us
    all_to_all x1, starting transfers between devices, body(): lax.all_to_all(outgoing, 'seq', split_axis=0, concat_axis=0, tiled=True)  4.62 us
  transfers between devices with their start and end apart: 18, of which 7 were waited for; matrix products, arithmetic and copies ran while one was open for 7% of the time, Pallas kernels for 0%

profile of v6, /device:TPU:4, one launch (start us, length us, event | category | flops | bytes accessed | tf_op | source)
XLA Modules:
  0.0 158.2 jit_solution(173896462911049566)
XLA Ops:
  0.0 0.9 slice_bitcast_fusion.9
  0.9 0.7 slice_bitcast_fusion.7
  2.2 2.3 %collective-permute-start = (bf16[3,2,256]{2,1,0:T(2,128)(2,1)}, bf16[3,2,256]{2,1,0:T(2,128)(2,1)}, u32[]{:S(2)}, u32[]{:S(2)}) collective-permute-start(bf16[3,2,256]{2,1,0:T(2,128)(2,1)} %pad_maximum_fusion), channel_id=1, source_target_pairs={{0,16},{16,32},{32,48},{48,64},{64,80},{80,96},{96,112},{112,128},... | collective-permute-start | bytes 9224 | tf_op jit(solution)/shard_map/ppermute | solution.py:14
  5.0 0.9 pad_bitcast_fusion
  5.9 0.7 fusion
  6.7 0.7 convolution_bitcast_fusion
  7.6 0.8 fusion.51
  8.4 0.7 fusion.55
  9.8 0.8 convolution_subtract_fusion.1
  10.5 0.8 convolution_add_fusion.1
  11.4 1.0 copy.52
  12.4 1.0 copy.54
  13.4 0.7 slice_bitcast_fusion.6
  14.6 1.7 %fusion.21 = bf16[128,256]{0,1:T(8,128)(2,1)} fusion(f32[130,256]{0,1:T(8,128)S(1)} %maximum_convert_fusion.1, f32[130,256]{0,1:T(8,128)S(1)} %maximum_convert_fusion, f32[256]{0:T(256)} %bitcast.165, f32[256]{0:T(256)} %bitcast.166, f32[256]{0:T(256)S(1)} %bitcast.161, f32[256]{0:T(256)S(1)} %bitcast.162, f32[256]{0:T(256)S(1)} %bitcast.163, f32[256]{0:T(256)} %bitcast.164), kind=kLoop, calls=%fused_computation.42 | loop fusion | flops 393216 | bytes 858112 | tf_op jit(solution)/shard_map/convert_element_type | solution.py:138
  16.3 21.5 %all-to-all-start = ((bf16[64,4,128]{2,1,0:T(4,128)(2,1)}), bf16[64,4,128]{2,1,0:T(4,128)(2,1)S(1)}, u32[]{:S(2)}, u32[]{:S(2)}) async-start(bf16[64,4,128]{2,1,0:T(4,128)(2,1)} %bitcast.17), calls=%async_computation | async-start | bytes 131072 | tf_op jit(solution)/shard_map/all_to_all | solution.py:142
  38.3 9.3 %all-to-all-done = bf16[64,4,128]{2,1,0:T(4,128)(2,1)S(1)} async-done(((bf16[64,4,128]{2,1,0:T(4,128)(2,1)}), bf16[64,4,128]{2,1,0:T(4,128)(2,1)S(1)}, u32[]{:S(2)}, u32[]{:S(2)}) %all-to-all-start) | async-done | bytes 65568 | tf_op jit(solution)/shard_map/all_to_all | solution.py:142
  48.7 0.8 fusion.53
  49.5 0.8 fusion.58
  50.3 0.8 convolution_add_fusion.2
  51.0 0.8 multiply_add_fusion
  51.8 0.7 fusion.39
  53.2 0.7 convolution_add_fusion
  53.8 0.6 convolution_subtract_fusion
  55.3 0.7 copy.76
  56.0 4.6 %all-to-all-start.1 = ((bf16[64,4,128]{2,1,0:T(4,128)(2,1)}), bf16[64,4,128]{2,1,0:T(4,128)(2,1)S(1)}, u32[]{:S(2)}, u32[]{:S(2)}) async-start(bf16[64,4,128]{2,1,0:T(4,128)(2,1)} %copy.76), calls=%async_computation.1 | async-start | bytes 131072 | tf_op jit(solution)/shard_map/all_to_all | solution.py:146
  60.7 9.9 %all-to-all-done.1 = bf16[64,4,128]{2,1,0:T(4,128)(2,1)S(1)} async-done(((bf16[64,4,128]{2,1,0:T(4,128)(2,1)}), bf16[64,4,128]{2,1,0:T(4,128)(2,1)S(1)}, u32[]{:S(2)}, u32[]{:S(2)}) %all-to-all-start.1) | async-done | bytes 65568 | tf_op jit(solution)/shard_map/all_to_all | solution.py:146
  70.8 4.7 %collective-permute-start.1 = (bf16[128,256]{1,0:T(8,128)(2,1)S(1)}, bf16[128,256]{1,0:T(8,128)(2,1)S(1)}, u32[]{:S(2)}, u32[]{:S(2)}) collective-permute-start(bf16[128,256]{1,0:T(8,128)(2,1)S(1)} %get-tuple-element.6), channel_id=1, source_target_pairs={{0,10},{1,11},{2,12},{3,13},{4,14},{5,15},{6,0},{7,1},{8,2},{9,3},... | collective-permute-start | bytes 196616 | tf_op jit(solution)/shard_map/ppermute | solution.py:122
  75.6 2.0 %gather_fusion = bf16[16,256,256]{2,1,0:T(8,128)(2,1)} fusion(bf16[16,256,256]{2,1,0:T(8,128)(2,1)S(1)} %bitcast.155, s32[1024]{0:T(1024)S(1)} %pad_clamp_fusion), kind=kCustom, calls=%fused_computation | custom fusion | bytes 4194368 | tf_op jit(solution)/shard_map/gather | solution.py:150
  77.6 5.0 %collective-permute-start.7 = (bf16[128,256]{1,0:T(8,128)(2,1)S(1)}, bf16[128,256]{1,0:T(8,128)(2,1)S(1)}, u32[]{:S(2)}, u32[]{:S(2)}) collective-permute-start(bf16[128,256]{1,0:T(8,128)(2,1)S(1)} %get-tuple-element.6), channel_id=1, source_target_pairs={{0,8},{1,9},{2,10},{3,11},{4,12},{5,13},{6,14},{7,15},{8,0},{9,1},... | collective-permute-start | bytes 196616 | tf_op jit(solution)/shard_map/ppermute | solution.py:122
  82.6 4.7 %collective-permute-start.6 = (bf16[128,256]{1,0:T(8,128)(2,1)S(1)}, bf16[128,256]{1,0:T(8,128)(2,1)S(1)}, u32[]{:S(2)}, u32[]{:S(2)}) collective-permute-start(bf16[128,256]{1,0:T(8,128)(2,1)S(1)} %get-tuple-element.6), channel_id=1, source_target_pairs={{0,6},{1,7},{2,8},{3,9},{4,10},{5,11},{6,12},{7,13},{8,14},{9,15},... | collective-permute-start | bytes 196616 | tf_op jit(solution)/shard_map/ppermute | solution.py:122
  87.3 1.9 %collective-permute-start.5 = (bf16[128,256]{1,0:T(8,128)(2,1)S(1)}, bf16[128,256]{1,0:T(8,128)(2,1)S(1)}, u32[]{:S(2)}, u32[]{:S(2)}) collective-permute-start(bf16[128,256]{1,0:T(8,128)(2,1)S(1)} %get-tuple-element.6), channel_id=1, source_target_pairs={{0,4},{1,5},{2,6},{3,7},{4,8},{5,9},{6,10},{7,11},{8,12},{9,13},{1... | collective-permute-start | bytes 196616 | tf_op jit(solution)/shard_map/ppermute | solution.py:122
  89.2 3.9 %collective-permute-start.3 = (bf16[128,256]{1,0:T(8,128)(2,1)S(1)}, bf16[128,256]{1,0:T(8,128)(2,1)S(1)}, u32[]{:S(2)}, u32[]{:S(2)}) collective-permute-start(bf16[128,256]{1,0:T(8,128)(2,1)S(1)} %get-tuple-element.6), channel_id=1, source_target_pairs={{0,14},{1,15},{2,0},{3,1},{4,2},{5,3},{6,4},{7,5},{8,6},{9,7},{10,... | collective-permute-start | bytes 196616 | tf_op jit(solution)/shard_map/ppermute | solution.py:122
  93.2 5.4 %collective-permute-start.2 = (bf16[128,256]{1,0:T(8,128)(2,1)S(1)}, bf16[128,256]{1,0:T(8,128)(2,1)S(1)}, u32[]{:S(2)}, u32[]{:S(2)}) collective-permute-start(bf16[128,256]{1,0:T(8,128)(2,1)S(1)} %get-tuple-element.6), channel_id=1, source_target_pairs={{0,12},{1,13},{2,14},{3,15},{4,0},{5,1},{6,2},{7,3},{8,4},{9,5},{1... | collective-permute-start | bytes 196616 | tf_op jit(solution)/shard_map/ppermute | solution.py:122
  98.7 3.2 %collective-permute-done.2 = bf16[128,256]{1,0:T(8,128)(2,1)S(1)} collective-permute-done((bf16[128,256]{1,0:T(8,128)(2,1)S(1)}, bf16[128,256]{1,0:T(8,128)(2,1)S(1)}, u32[]{:S(2)}, u32[]{:S(2)}) %collective-permute-start.2) | collective-permute-done | bytes 65568 | tf_op jit(solution)/shard_map/ppermute | solution.py:122
  101.8 8.2 %collective-permute-start.8 = (bf16[128,256]{1,0:T(8,128)(2,1)S(1)}, bf16[128,256]{1,0:T(8,128)(2,1)S(1)}, u32[]{:S(2)}, u32[]{:S(2)}) collective-permute-start(bf16[128,256]{1,0:T(8,128)(2,1)S(1)} %get-tuple-element.6), channel_id=1, source_target_pairs={{0,1},{1,0},{2,3},{3,2},{4,5},{5,4},{6,7},{7,6},{8,9},{9,8},{10,11... | collective-permute-start | bytes 196616 | tf_op jit(solution)/shard_map/ppermute | solution.py:120
  110.0 1.9 %collective-permute-start.4 = (bf16[128,256]{1,0:T(8,128)(2,1)S(1)}, bf16[128,256]{1,0:T(8,128)(2,1)S(1)}, u32[]{:S(2)}, u32[]{:S(2)}) collective-permute-start(bf16[128,256]{1,0:T(8,128)(2,1)S(1)} %get-tuple-element.6), channel_id=1, source_target_pairs={{0,2},{1,3},{2,4},{3,5},{4,6},{5,7},{6,8},{7,9},{8,10},{9,11},{10,... | collective-permute-start | bytes 196616 | tf_op jit(solution)/shard_map/ppermute | solution.py:122
  112.0 1.0 collective-permute-done.8
  112.9 5.2 %collective-permute-start.15 = (bf16[128,256]{1,0:T(8,128)(2,1)S(1)}, bf16[128,256]{1,0:T(8,128)(2,1)S(1)}, u32[]{:S(2)}, u32[]{:S(2)}) collective-permute-start(bf16[128,256]{1,0:T(8,128)(2,1)S(1)} %collective-permute-done.8), channel_id=1, source_target_pairs={{0,8},{1,9},{2,10},{3,11},{4,12},{5,13},{6,14},{7,15},{8,0},{9,1},... | collective-permute-start | bytes 196616 | tf_op jit(solution)/shard_map/ppermute | solution.py:123
  118.2 4.1 %collective-permute-start.14 = (bf16[128,256]{1,0:T(8,128)(2,1)S(1)}, bf16[128,256]{1,0:T(8,128)(2,1)S(1)}, u32[]{:S(2)}, u32[]{:S(2)}) collective-permute-start(bf16[128,256]{1,0:T(8,128)(2,1)S(1)} %collective-permute-done.8), channel_id=1, source_target_pairs={{0,6},{1,7},{2,8},{3,9},{4,10},{5,11},{6,12},{7,13},{8,14},{9,15},... | collective-permute-start | bytes 196616 | tf_op jit(solution)/shard_map/ppermute | solution.py:123
  122.3 3.4 %collective-permute-start.13 = (bf16[128,256]{1,0:T(8,128)(2,1)S(1)}, bf16[128,256]{1,0:T(8,128)(2,1)S(1)}, u32[]{:S(2)}, u32[]{:S(2)}) collective-permute-start(bf16[128,256]{1,0:T(8,128)(2,1)S(1)} %collective-permute-done.8), channel_id=1, source_target_pairs={{0,4},{1,5},{2,6},{3,7},{4,8},{5,9},{6,10},{7,11},{8,12},{9,13},{1... | collective-permute-start | bytes 196616 | tf_op jit(solution)/shard_map/ppermute | solution.py:123
  125.8 4.7 %collective-permute-start.12 = (bf16[128,256]{1,0:T(8,128)(2,1)S(1)}, bf16[128,256]{1,0:T(8,128)(2,1)S(1)}, u32[]{:S(2)}, u32[]{:S(2)}) collective-permute-start(bf16[128,256]{1,0:T(8,128)(2,1)S(1)} %collective-permute-done.8), channel_id=1, source_target_pairs={{0,2},{1,3},{2,4},{3,5},{4,6},{5,7},{6,8},{7,9},{8,10},{9,11},{10,... | collective-permute-start | bytes 196616 | tf_op jit(solution)/shard_map/ppermute | solution.py:123
  130.5 3.2 %collective-permute-start.9 = (bf16[128,256]{1,0:T(8,128)(2,1)S(1)}, bf16[128,256]{1,0:T(8,128)(2,1)S(1)}, u32[]{:S(2)}, u32[]{:S(2)}) collective-permute-start(bf16[128,256]{1,0:T(8,128)(2,1)S(1)} %collective-permute-done.8), channel_id=1, source_target_pairs={{0,10},{1,11},{2,12},{3,13},{4,14},{5,15},{6,0},{7,1},{8,2},{9,3},... | collective-permute-start | bytes 196616 | tf_op jit(solution)/shard_map/ppermute | solution.py:123
  133.8 6.2 %collective-permute-done.9 = bf16[128,256]{1,0:T(8,128)(2,1)S(1)} collective-permute-done((bf16[128,256]{1,0:T(8,128)(2,1)S(1)}, bf16[128,256]{1,0:T(8,128)(2,1)S(1)}, u32[]{:S(2)}, u32[]{:S(2)}) %collective-permute-start.9) | collective-permute-done | bytes 65568 | tf_op jit(solution)/shard_map/ppermute | solution.py:123
  139.9 1.9 %collective-permute-start.10 = (bf16[128,256]{1,0:T(8,128)(2,1)S(1)}, bf16[128,256]{1,0:T(8,128)(2,1)S(1)}, u32[]{:S(2)}, u32[]{:S(2)}) collective-permute-start(bf16[128,256]{1,0:T(8,128)(2,1)S(1)} %collective-permute-done.8), channel_id=1, source_target_pairs={{0,12},{1,13},{2,14},{3,15},{4,0},{5,1},{6,2},{7,3},{8,4},{9,5},{1... | collective-permute-start | bytes 196616 | tf_op jit(solution)/shard_map/ppermute | solution.py:123
  141.9 7.5 %collective-permute-done.10 = bf16[128,256]{1,0:T(8,128)(2,1)S(1)} collective-permute-done((bf16[128,256]{1,0:T(8,128)(2,1)S(1)}, bf16[128,256]{1,0:T(8,128)(2,1)S(1)}, u32[]{:S(2)}, u32[]{:S(2)}) %collective-permute-start.10) | collective-permute-done | bytes 65568 | tf_op jit(solution)/shard_map/ppermute | solution.py:123
  149.3 1.9 %collective-permute-start.11 = (bf16[128,256]{1,0:T(8,128)(2,1)S(1)}, bf16[128,256]{1,0:T(8,128)(2,1)S(1)}, u32[]{:S(2)}, u32[]{:S(2)}) collective-permute-start(bf16[128,256]{1,0:T(8,128)(2,1)S(1)} %collective-permute-done.8), channel_id=1, source_target_pairs={{0,14},{1,15},{2,0},{3,1},{4,2},{5,3},{6,4},{7,5},{8,6},{9,7},{10,... | collective-permute-start | bytes 196616 | tf_op jit(solution)/shard_map/ppermute | solution.py:123
  151.3 4.2 %collective-permute-done.11 = bf16[128,256]{1,0:T(8,128)(2,1)S(1)} collective-permute-done((bf16[128,256]{1,0:T(8,128)(2,1)S(1)}, bf16[128,256]{1,0:T(8,128)(2,1)S(1)}, u32[]{:S(2)}, u32[]{:S(2)}) %collective-permute-start.11) | collective-permute-done | bytes 65568 | tf_op jit(solution)/shard_map/ppermute | solution.py:123
  155.6 2.7 %fusion.5 = bf16[128,256]{1,0:T(8,128)(2,1)} fusion(bf16[16,128,256]{2,1,0:T(8,128)(2,1)S(1)} %bitcast_dynamic-update-slice_fusion, bf16[16,256,256]{2,1,0:T(8,128)(2,1)} %gather_fusion), kind=kOutput, calls=%fused_computation.18 | convolution fusion | flops 268468224 | bytes 3211264 | tf_op jit(solution)/shard_map/gtc,gcj->tj/dot_general | solution.py:151
  (69 shorter events, 6.0 us)
Async XLA Ops:
  0.0 75.5 %copy-start = (bf16[4096,256]{1,0:T(8,128)(2,1)S(1)}, bf16[4096,256]{1,0:T(8,128)(2,1)}, u32[]{:S(2)}) copy-start(bf16[4096,256]{1,0:T(8,128)(2,1)} %param.13) | copy-start | bytes 6291460
  0.0 9.1 %copy-start.2 = (f32[3,3,256]{2,1,0:T(4,128)S(1)}, f32[3,3,256]{2,1,0:T(4,128)}, u32[]{:S(2)}) copy-start(f32[3,3,256]{2,1,0:T(4,128)} %param.10) | copy-start | bytes 27652
  2.2 11.2 %collective-permute-start = (bf16[3,2,256]{2,1,0:T(2,128)(2,1)}, bf16[3,2,256]{2,1,0:T(2,128)(2,1)}, u32[]{:S(2)}, u32[]{:S(2)}) collective-permute-start(bf16[3,2,256]{2,1,0:T(2,128)(2,1)} %pad_maximum_fusion), channel_id=1, source_target_pairs={{0,16},{16,32},{32,48},{48,64},{64,80},{80,96},{96,112},{112,128},... | collective-permute-start | bytes 9224 | tf_op jit(solution)/shard_map/ppermute | solution.py:14
  9.7 4.8 %copy-start.5 = (f32[1,1,256]{2,1,0:T(1,128)S(1)}, f32[1,1,256]{2,1,0:T(1,128)}, u32[]{:S(2)}) copy-start(f32[1,1,256]{2,1,0:T(1,128)} %get-tuple-element.10) | copy-start | bytes 3076
  9.7 4.8 %copy-start.6 = (f32[1,1,256]{2,1,0:T(1,128)S(1)}, f32[1,1,256]{2,1,0:T(1,128)}, u32[]{:S(2)}) copy-start(f32[1,1,256]{2,1,0:T(1,128)} %get-tuple-element.11) | copy-start | bytes 3076
  9.8 4.8 %copy-start.7 = (f32[1,1,256]{2,1,0:T(1,128)S(1)}, f32[1,1,256]{2,1,0:T(1,128)}, u32[]{:S(2)}) copy-start(f32[1,1,256]{2,1,0:T(1,128)} %get-tuple-element.12) | copy-start | bytes 3076
  16.3 31.3 %all-to-all-start = ((bf16[64,4,128]{2,1,0:T(4,128)(2,1)}), bf16[64,4,128]{2,1,0:T(4,128)(2,1)S(1)}, u32[]{:S(2)}, u32[]{:S(2)}) async-start(bf16[64,4,128]{2,1,0:T(4,128)(2,1)} %bitcast.17), calls=%async_computation | async-start | bytes 131072 | tf_op jit(solution)/shard_map/all_to_all | solution.py:142
  51.8 3.1 %copy-start.8 = (f32[4]{0:T(128)S(1)}, f32[4]{0:T(128)}, u32[]{:S(2)}) copy-start(f32[4]{0:T(128)} %param.12) | copy-start | bytes 52
  52.5 8.2 %copy-start.1 = (bf16[128,256]{1,0:T(8,128)(2,1)S(1)}, bf16[128,256]{1,0:T(8,128)(2,1)}, u32[]{:S(2)}) copy-start(bf16[128,256]{1,0:T(8,128)(2,1)} %param.7) | copy-start | bytes 196612
  53.1 17.6 %copy-start.3 = (f32[1,1,256]{2,1,0:T(1,128)S(1)}, f32[1,1,256]{2,1,0:T(1,128)}, u32[]{:S(2)}) copy-start(f32[1,1,256]{2,1,0:T(1,128)} %get-tuple-element.14) | copy-start | bytes 3076
  53.2 17.6 %copy-start.4 = (f32[1,1,256]{2,1,0:T(1,128)S(1)}, f32[1,1,256]{2,1,0:T(1,128)}, u32[]{:S(2)}) copy-start(f32[1,1,256]{2,1,0:T(1,128)} %get-tuple-element.15) | copy-start | bytes 3076
  56.0 14.6 %all-to-all-start.1 = ((bf16[64,4,128]{2,1,0:T(4,128)(2,1)}), bf16[64,4,128]{2,1,0:T(4,128)(2,1)S(1)}, u32[]{:S(2)}, u32[]{:S(2)}) async-start(bf16[64,4,128]{2,1,0:T(4,128)(2,1)} %copy.76), calls=%async_computation.1 | async-start | bytes 131072 | tf_op jit(solution)/shard_map/all_to_all | solution.py:146
  70.8 22.4 %collective-permute-start.1 = (bf16[128,256]{1,0:T(8,128)(2,1)S(1)}, bf16[128,256]{1,0:T(8,128)(2,1)S(1)}, u32[]{:S(2)}, u32[]{:S(2)}) collective-permute-start(bf16[128,256]{1,0:T(8,128)(2,1)S(1)} %get-tuple-element.6), channel_id=1, source_target_pairs={{0,10},{1,11},{2,12},{3,13},{4,14},{5,15},{6,0},{7,1},{8,2},{9,3},... | collective-permute-start | bytes 196616 | tf_op jit(solution)/shard_map/ppermute | solution.py:122
  77.6 52.9 %collective-permute-start.7 = (bf16[128,256]{1,0:T(8,128)(2,1)S(1)}, bf16[128,256]{1,0:T(8,128)(2,1)S(1)}, u32[]{:S(2)}, u32[]{:S(2)}) collective-permute-start(bf16[128,256]{1,0:T(8,128)(2,1)S(1)} %get-tuple-element.6), channel_id=1, source_target_pairs={{0,8},{1,9},{2,10},{3,11},{4,12},{5,13},{6,14},{7,15},{8,0},{9,1},... | collective-permute-start | bytes 196616 | tf_op jit(solution)/shard_map/ppermute | solution.py:122
  82.6 43.2 %collective-permute-start.6 = (bf16[128,256]{1,0:T(8,128)(2,1)S(1)}, bf16[128,256]{1,0:T(8,128)(2,1)S(1)}, u32[]{:S(2)}, u32[]{:S(2)}) collective-permute-start(bf16[128,256]{1,0:T(8,128)(2,1)S(1)} %get-tuple-element.6), channel_id=1, source_target_pairs={{0,6},{1,7},{2,8},{3,9},{4,10},{5,11},{6,12},{7,13},{8,14},{9,15},... | collective-permute-start | bytes 196616 | tf_op jit(solution)/shard_map/ppermute | solution.py:122
  87.3 35.0 %collective-permute-start.5 = (bf16[128,256]{1,0:T(8,128)(2,1)S(1)}, bf16[128,256]{1,0:T(8,128)(2,1)S(1)}, u32[]{:S(2)}, u32[]{:S(2)}) collective-permute-start(bf16[128,256]{1,0:T(8,128)(2,1)S(1)} %get-tuple-element.6), channel_id=1, source_target_pairs={{0,4},{1,5},{2,6},{3,7},{4,8},{5,9},{6,10},{7,11},{8,12},{9,13},{1... | collective-permute-start | bytes 196616 | tf_op jit(solution)/shard_map/ppermute | solution.py:122
  89.2 20.8 %collective-permute-start.3 = (bf16[128,256]{1,0:T(8,128)(2,1)S(1)}, bf16[128,256]{1,0:T(8,128)(2,1)S(1)}, u32[]{:S(2)}, u32[]{:S(2)}) collective-permute-start(bf16[128,256]{1,0:T(8,128)(2,1)S(1)} %get-tuple-element.6), channel_id=1, source_target_pairs={{0,14},{1,15},{2,0},{3,1},{4,2},{5,3},{6,4},{7,5},{8,6},{9,7},{10,... | collective-permute-start | bytes 196616 | tf_op jit(solution)/shard_map/ppermute | solution.py:122
  93.2 8.6 %collective-permute-start.2 = (bf16[128,256]{1,0:T(8,128)(2,1)S(1)}, bf16[128,256]{1,0:T(8,128)(2,1)S(1)}, u32[]{:S(2)}, u32[]{:S(2)}) collective-permute-start(bf16[128,256]{1,0:T(8,128)(2,1)S(1)} %get-tuple-element.6), channel_id=1, source_target_pairs={{0,12},{1,13},{2,14},{3,15},{4,0},{5,1},{6,2},{7,3},{8,4},{9,5},{1... | collective-permute-start | bytes 196616 | tf_op jit(solution)/shard_map/ppermute | solution.py:122
  101.8 11.1 %collective-permute-start.8 = (bf16[128,256]{1,0:T(8,128)(2,1)S(1)}, bf16[128,256]{1,0:T(8,128)(2,1)S(1)}, u32[]{:S(2)}, u32[]{:S(2)}) collective-permute-start(bf16[128,256]{1,0:T(8,128)(2,1)S(1)} %get-tuple-element.6), channel_id=1, source_target_pairs={{0,1},{1,0},{2,3},{3,2},{4,5},{5,4},{6,7},{7,6},{8,9},{9,8},{10,11... | collective-permute-start | bytes 196616 | tf_op jit(solution)/shard_map/ppermute | solution.py:120
  110.0 8.2 %collective-permute-start.4 = (bf16[128,256]{1,0:T(8,128)(2,1)S(1)}, bf16[128,256]{1,0:T(8,128)(2,1)S(1)}, u32[]{:S(2)}, u32[]{:S(2)}) collective-permute-start(bf16[128,256]{1,0:T(8,128)(2,1)S(1)} %get-tuple-element.6), channel_id=1, source_target_pairs={{0,2},{1,3},{2,4},{3,5},{4,6},{5,7},{6,8},{7,9},{8,10},{9,11},{10,... | collective-permute-start | bytes 196616 | tf_op jit(solution)/shard_map/ppermute | solution.py:122
  112.9 42.6 %collective-permute-start.15 = (bf16[128,256]{1,0:T(8,128)(2,1)S(1)}, bf16[128,256]{1,0:T(8,128)(2,1)S(1)}, u32[]{:S(2)}, u32[]{:S(2)}) collective-permute-start(bf16[128,256]{1,0:T(8,128)(2,1)S(1)} %collective-permute-done.8), channel_id=1, source_target_pairs={{0,8},{1,9},{2,10},{3,11},{4,12},{5,13},{6,14},{7,15},{8,0},{9,1},... | collective-permute-start | bytes 196616 | tf_op jit(solution)/shard_map/ppermute | solution.py:123
  118.2 37.3 %collective-permute-start.14 = (bf16[128,256]{1,0:T(8,128)(2,1)S(1)}, bf16[128,256]{1,0:T(8,128)(2,1)S(1)}, u32[]{:S(2)}, u32[]{:S(2)}) collective-permute-start(bf16[128,256]{1,0:T(8,128)(2,1)S(1)} %collective-permute-done.8), channel_id=1, source_target_pairs={{0,6},{1,7},{2,8},{3,9},{4,10},{5,11},{6,12},{7,13},{8,14},{9,15},... | collective-permute-start | bytes 196616 | tf_op jit(solution)/shard_map/ppermute | solution.py:123
  122.3 33.2 %collective-permute-start.13 = (bf16[128,256]{1,0:T(8,128)(2,1)S(1)}, bf16[128,256]{1,0:T(8,128)(2,1)S(1)}, u32[]{:S(2)}, u32[]{:S(2)}) collective-permute-start(bf16[128,256]{1,0:T(8,128)(2,1)S(1)} %collective-permute-done.8), channel_id=1, source_target_pairs={{0,4},{1,5},{2,6},{3,7},{4,8},{5,9},{6,10},{7,11},{8,12},{9,13},{1... | collective-permute-start | bytes 196616 | tf_op jit(solution)/shard_map/ppermute | solution.py:123
  125.8 29.7 %collective-permute-start.12 = (bf16[128,256]{1,0:T(8,128)(2,1)S(1)}, bf16[128,256]{1,0:T(8,128)(2,1)S(1)}, u32[]{:S(2)}, u32[]{:S(2)}) collective-permute-start(bf16[128,256]{1,0:T(8,128)(2,1)S(1)} %collective-permute-done.8), channel_id=1, source_target_pairs={{0,2},{1,3},{2,4},{3,5},{4,6},{5,7},{6,8},{7,9},{8,10},{9,11},{10,... | collective-permute-start | bytes 196616 | tf_op jit(solution)/shard_map/ppermute | solution.py:123
  130.5 9.4 %collective-permute-start.9 = (bf16[128,256]{1,0:T(8,128)(2,1)S(1)}, bf16[128,256]{1,0:T(8,128)(2,1)S(1)}, u32[]{:S(2)}, u32[]{:S(2)}) collective-permute-start(bf16[128,256]{1,0:T(8,128)(2,1)S(1)} %collective-permute-done.8), channel_id=1, source_target_pairs={{0,10},{1,11},{2,12},{3,13},{4,14},{5,15},{6,0},{7,1},{8,2},{9,3},... | collective-permute-start | bytes 196616 | tf_op jit(solution)/shard_map/ppermute | solution.py:123
  139.9 9.4 %collective-permute-start.10 = (bf16[128,256]{1,0:T(8,128)(2,1)S(1)}, bf16[128,256]{1,0:T(8,128)(2,1)S(1)}, u32[]{:S(2)}, u32[]{:S(2)}) collective-permute-start(bf16[128,256]{1,0:T(8,128)(2,1)S(1)} %collective-permute-done.8), channel_id=1, source_target_pairs={{0,12},{1,13},{2,14},{3,15},{4,0},{5,1},{6,2},{7,3},{8,4},{9,5},{1... | collective-permute-start | bytes 196616 | tf_op jit(solution)/shard_map/ppermute | solution.py:123
  149.3 6.1 %collective-permute-start.11 = (bf16[128,256]{1,0:T(8,128)(2,1)S(1)}, bf16[128,256]{1,0:T(8,128)(2,1)S(1)}, u32[]{:S(2)}, u32[]{:S(2)}) collective-permute-start(bf16[128,256]{1,0:T(8,128)(2,1)S(1)} %collective-permute-done.8), channel_id=1, source_target_pairs={{0,14},{1,15},{2,0},{3,1},{4,2},{5,3},{6,4},{7,5},{8,6},{9,7},{10,... | collective-permute-start | bytes 196616 | tf_op jit(solution)/shard_map/ppermute | solution.py:123

commit v7 on v5

--- a/solution.py
+++ b/solution.py
@@ -6,12 +6,6 @@
 from jax.sharding import PartitionSpec as P
 
 HIGHEST_MODE = lax.Precision.HIGHEST
-
-
-def shifted(block, axis, distance):
-    devices = range(lax.axis_size(axis))
-    route = [(i - distance, i) for i in devices if i - distance in devices]
-    return lax.ppermute(block, axis, route)
 
 
 def tables(count):
@@ -96,16 +90,6 @@
     return result.reshape(channels, length) / total + gains[:, None] * signal
 
 
-def shifted_filter(current, tail, taps):
-    span = taps.shape[0]
-    rows = current.shape[0]
-    joined = jnp.concatenate([tail, current], 0).astype(jnp.float32)
-    total = taps[0] * joined[span - 1 :]
-    for offset in range(1, span):
-        total = total + taps[offset] * joined[span - 1 - offset : span - 1 - offset + rows]
-    return total
-
-
 def chan_route(size, step):
     pairs = size // 2
     return [(x * 2 + h, ((x + step) % pairs) * 2 + h) for x in range(pairs) for h in range(2)]
@@ -118,13 +102,19 @@
     mine_x = me // 2
     mine_h = me % 2
     partner = lax.ppermute(block, "chan", [(i, i ^ 1) for i in range(size)])
-    moving = jnp.stack([block, partner])
-    slots = [moving]
+    held = jnp.stack([block, partner])
+    slots = [held]
     places = [mine_x]
-    for step in range(1, pairs):
-        moving = lax.ppermute(moving, "chan", chan_route(size, 1))
-        slots.append(moving)
+    right = held
+    left = held
+    for step in range(1, pairs // 2 + 1):
+        right = lax.ppermute(right, "chan", chan_route(size, 1))
+        slots.append(right)
         places.append((mine_x - step) % pairs)
+        if step < pairs - step:
+            left = lax.ppermute(left, "chan", chan_route(size, -1))
+            slots.append(left)
+            places.append((mine_x + step) % pairs)
     place = jnp.stack(places)
     order = jnp.stack([place * 2 + mine_h, place * 2 + (1 - mine_h)], axis=1)
     return jnp.stack(slots), order
@@ -143,23 +133,20 @@
 
 def body(queries, keys, values, short_taps, long_filter, skip_gain, out_weight):
     rows, width = queries.shape
-    span = short_taps.shape[1]
-    edge = rows - (span - 1)
     groups = lax.axis_size("seq")
     per_group = width // groups
     seq_index = lax.axis_index("seq")
-    raw = jnp.stack([keys.T, values.T]).reshape(2, groups, per_group, rows).transpose(1, 0, 2, 3)
+    raw = jnp.stack([queries.T, keys.T, values.T]).reshape(3, groups, per_group, rows).transpose(1, 0, 2, 3)
     split_raw = lax.all_to_all(raw, "seq", split_axis=0, concat_axis=0, tiled=True)
-    whole = split_raw.transpose(1, 2, 0, 3).reshape(2, per_group, groups * rows).astype(jnp.float32)
+    whole = split_raw.transpose(1, 2, 0, 3).reshape(3, per_group, groups * rows).astype(jnp.float32)
     own_taps = lax.dynamic_slice_in_dim(short_taps, seq_index * per_group, per_group, axis=2)
-    signal = (causal_filter(whole[0], own_taps[1]) * causal_filter(whole[1], own_taps[2])).astype(jnp.bfloat16)
-    tail = shifted(queries[edge:], "seq", 1)
-    short_q = shifted_filter(queries, tail, short_taps[0]).astype(jnp.bfloat16)
+    short_q = causal_filter(whole[0], own_taps[0]).astype(jnp.bfloat16)
+    signal = (causal_filter(whole[1], own_taps[1]) * causal_filter(whole[2], own_taps[2])).astype(jnp.bfloat16)
     convolved = long_convolution(signal, long_filter, skip_gain).astype(jnp.bfloat16)
-    outgoing = convolved.reshape(per_group, groups, rows).transpose(1, 0, 2)
+    gated_t = (short_q.astype(jnp.float32) * convolved.astype(jnp.float32)).astype(jnp.bfloat16)
+    outgoing = gated_t.reshape(per_group, groups, rows).transpose(1, 0, 2)
     returned = lax.all_to_all(outgoing, "seq", split_axis=0, concat_axis=0, tiled=True)
-    long_out = returned.reshape(width, rows).T
-    gated = (short_q.astype(jnp.float32) * long_out.astype(jnp.float32)).astype(jnp.bfloat16)
+    gated = returned.reshape(width, rows).T
     pieces, order = gather_chan(gated)
     weight = out_weight.reshape(-1, width, out_weight.shape[1])[order]
     result = jnp.einsum("pqtc,pqcj->tj", pieces, weight, preferred_element_type=jnp.float32)

time: 142 us -> 113 us (0.80)
  the two profiles are of different devices: /device:TPU:112 before, /device:TPU:8 now
where the time goes in v7:
time: 113 us
  starting transfers between devices  58.9 us (52%)
  waiting for transfers between devices  24.7 us (22%)
  matrix products  13.7 us (12%)
  local copies, waits for them, and re-layouts  9.55 us (8%)
  other arithmetic  5.32 us (5%)
    all_to_all x1, starting transfers between devices, body(): lax.all_to_all(raw, 'seq', split_axis=0, concat_axis=0, tiled=True)  21.3 us
    ppermute x3, starting transfers between devices, gather_chan(): left = lax.ppermute(left, 'chan', chan_route(size, -1))  14 us
    all_to_all x1, waiting for transfers between devices, body(): lax.all_to_all(outgoing, 'seq', split_axis=0, concat_axis=0, tiled=True)  9.95 us
    ppermute x4, starting transfers between devices, gather_chan(): right = lax.ppermute(right, 'chan', chan_route(size, 1))  9.17 us
    all_to_all x1, starting transfers between devices, body(): lax.all_to_all(outgoing, 'seq', split_axis=0, concat_axis=0, tiled=True)  8.9 us
    ppermute x4, waiting for transfers between devices, gather_chan(): right = lax.ppermute(right, 'chan', chan_route(size, 1))  8.01 us
    ppermute x1, starting transfers between devices, gather_chan(): partner = lax.ppermute(block, 'chan', [(i, i ^ 1) for i in range(size)])  5.51 us
    ppermute x1, waiting for transfers between devices, gather_chan(): partner = lax.ppermute(block, 'chan', [(i, i ^ 1) for i in range(size)])  5.08 us
  transfers between devices with their start and end apart: 10, of which 6 were waited for; matrix products, arithmetic and copies ran while one was open for 11% of the time, Pallas kernels for 0%

profile of v7, /device:TPU:8, one launch (start us, length us, event | category | flops | bytes accessed | tf_op | source)
XLA Modules:
  0.0 112.7 jit_solution(7931687420230660032)
XLA Ops:
  0.0 1.1 copy.54
  1.1 1.0 copy.55
  2.1 1.0 copy.56
  3.2 0.7 copy.57
  3.9 21.3 %all-to-all-start = ((bf16[64,3,4,128]{3,2,1,0:T(4,128)(2,1)}), bf16[64,3,4,128]{3,2,1,0:T(4,128)(2,1)}, u32[]{:S(2)}, u32[]{:S(2)}) async-start(bf16[64,3,4,128]{3,2,1,0:T(4,128)(2,1)} %copy.57), calls=%async_computation | async-start | bytes 393216 | tf_op jit(solution)/shard_map/all_to_all | solution.py:140
  25.3 0.9 fusion.63
  26.7 0.9 pad_bitcast_fusion
  27.6 0.7 fusion
  28.3 0.7 convolution_bitcast_fusion
  29.3 0.8 fusion.42
  30.0 0.7 fusion.46
  30.8 0.8 convolution_subtract_fusion.1
  31.6 1.5 %fusion.97 = (f32[4]{0:T(128)}, f32[4]{0:T(128)S(1)}, f32[4]{0:T(128)S(1)}, f32[4]{0:T(128)S(1)}, f32[4]{0:T(128)S(1)}, /*index=5*/f32[4]{0:T(128)}, f32[4]{0:T(128)}, f32[4]{0:T(128)}, f32[4]{0:T(128)}) fusion(f32[3,3,256]{2,1,0:T(4,128)} %param.10, s32[]{:T(128)S(6)} %select_n.127, s32[]{:T(128)S(6)} %add.270, s32[]{:T(128)S(6)} %add.269), kind=kLoop, calls=%fused_computation.135 | loop fusion | bytes 300 | tf_op jit(solution)/shard_map/mul | solution.py:125
  33.1 0.7 stack.108
  33.7 0.9 fusion.62
  34.6 0.8 convolution_add_fusion.1
  35.4 1.6 %all-to-all-done = bf16[64,3,4,128]{3,2,1,0:T(4,128)(2,1)} async-done(((bf16[64,3,4,128]{3,2,1,0:T(4,128)(2,1)}), bf16[64,3,4,128]{3,2,1,0:T(4,128)(2,1)}, u32[]{:S(2)}, u32[]{:S(2)}) %all-to-all-start) | async-done | bytes 196640 | tf_op jit(solution)/shard_map/all_to_all | solution.py:140
  37.0 1.0 convert_bitcast_fusion
  38.1 1.0 fusion.59
  39.1 0.7 fusion.1
  39.9 0.7 convolution_bitcast_fusion.1
  40.6 0.8 fusion.44
  41.4 0.8 fusion.49
  42.1 0.8 convolution_add_fusion.2
  42.9 0.8 multiply_add_fusion
  43.7 0.7 fusion.30
  44.4 0.8 fusion.40
  45.2 0.6 convolution_add_fusion
  45.9 0.6 convolution_subtract_fusion
  46.6 0.5 fusion.12
  47.0 0.5 fusion.3
  47.5 0.8 fusion.29
  48.4 8.9 %all-to-all-start.1 = ((bf16[64,4,128]{2,1,0:T(4,128)(2,1)}), bf16[64,4,128]{2,1,0:T(4,128)(2,1)S(1)}, u32[]{:S(2)}, u32[]{:S(2)}) async-start(bf16[64,4,128]{2,1,0:T(4,128)(2,1)} %fusion.29), calls=%async_computation.1 | async-start | bytes 131072 | tf_op jit(solution)/shard_map/all_to_all | solution.py:148
  57.3 10.0 %all-to-all-done.1 = bf16[64,4,128]{2,1,0:T(4,128)(2,1)S(1)} async-done(((bf16[64,4,128]{2,1,0:T(4,128)(2,1)}), bf16[64,4,128]{2,1,0:T(4,128)(2,1)S(1)}, u32[]{:S(2)}, u32[]{:S(2)}) %all-to-all-start.1) | async-done | bytes 65568 | tf_op jit(solution)/shard_map/all_to_all | solution.py:148
  67.4 5.5 %collective-permute-start = (bf16[128,256]{1,0:T(8,128)(2,1)S(1)}, bf16[128,256]{1,0:T(8,128)(2,1)S(1)}, u32[]{:S(2)}, u32[]{:S(2)}) collective-permute-start(bf16[128,256]{1,0:T(8,128)(2,1)S(1)} %bitcast.183), channel_id=1, source_target_pairs={{0,1},{1,0},{2,3},{3,2},{4,5},{5,4},{6,7},{7,6},{8,9},{9,8},{10,11... | collective-permute-start | bytes 196616 | tf_op jit(solution)/shard_map/ppermute | solution.py:104
  73.0 5.1 %collective-permute-done = bf16[128,256]{1,0:T(8,128)(2,1)S(1)} collective-permute-done((bf16[128,256]{1,0:T(8,128)(2,1)S(1)}, bf16[128,256]{1,0:T(8,128)(2,1)S(1)}, u32[]{:S(2)}, u32[]{:S(2)}) %collective-permute-start) | collective-permute-done | bytes 65568 | tf_op jit(solution)/shard_map/ppermute | solution.py:104
  78.1 3.2 %collective-permute-start.1 = (bf16[2,128,256]{2,1,0:T(8,128)(2,1)S(1)}, bf16[2,128,256]{2,1,0:T(8,128)(2,1)S(1)}, u32[]{:S(2)}, u32[]{:S(2)}) collective-permute-start(bf16[2,128,256]{2,1,0:T(8,128)(2,1)S(1)} %pad_maximum_fusion), channel_id=1, source_target_pairs={{0,2},{1,3},{2,4},{3,5},{4,6},{5,7},{6,8},{7,9},{8,10},{9,11},{10,... | collective-permute-start | bytes 393224 | tf_op jit(solution)/shard_map/ppermute | solution.py:111
  81.4 3.8 %collective-permute-start.2 = (bf16[2,128,256]{2,1,0:T(8,128)(2,1)S(1)}, bf16[2,128,256]{2,1,0:T(8,128)(2,1)S(1)}, u32[]{:S(2)}, u32[]{:S(2)}) collective-permute-start(bf16[2,128,256]{2,1,0:T(8,128)(2,1)S(1)} %pad_maximum_fusion), channel_id=1, source_target_pairs={{0,14},{1,15},{2,0},{3,1},{4,2},{5,3},{6,4},{7,5},{8,6},{9,7},{10,... | collective-permute-start | bytes 393224 | tf_op jit(solution)/shard_map/ppermute | solution.py:115
  85.2 2.0 %gather_fusion = bf16[16,256,256]{2,1,0:T(8,128)(2,1)} fusion(bf16[16,256,256]{2,1,0:T(8,128)(2,1)S(1)} %bitcast.175, s32[1024]{0:T(1024)S(1)} %pad_clamp_fusion), kind=kCustom, calls=%fused_computation | custom fusion | bytes 4194368 | tf_op jit(solution)/shard_map/gather | solution.py:151
  87.3 2.1 %collective-permute-start.3 = (bf16[2,128,256]{2,1,0:T(8,128)(2,1)S(1)}, bf16[2,128,256]{2,1,0:T(8,128)(2,1)S(1)}, u32[]{:S(2)}, u32[]{:S(2)}) collective-permute-start(bf16[2,128,256]{2,1,0:T(8,128)(2,1)S(1)} %collective-permute-done.1), channel_id=1, source_target_pairs={{0,2},{1,3},{2,4},{3,5},{4,6},{5,7},{6,8},{7,9},{8,10},{9,11},{10,... | collective-permute-start | bytes 393224 | tf_op jit(solution)/shard_map/ppermute | solution.py:111
  89.4 5.0 %collective-permute-start.4 = (bf16[2,128,256]{2,1,0:T(8,128)(2,1)S(1)}, bf16[2,128,256]{2,1,0:T(8,128)(2,1)S(1)}, u32[]{:S(2)}, u32[]{:S(2)}) collective-permute-start(bf16[2,128,256]{2,1,0:T(8,128)(2,1)S(1)} %collective-permute-done.2), channel_id=1, source_target_pairs={{0,14},{1,15},{2,0},{3,1},{4,2},{5,3},{6,4},{7,5},{8,6},{9,7},{10,... | collective-permute-start | bytes 393224 | tf_op jit(solution)/shard_map/ppermute | solution.py:115
  94.5 1.0 collective-permute-done.3
  95.5 1.9 %collective-permute-start.5 = (bf16[2,128,256]{2,1,0:T(8,128)(2,1)S(1)}, bf16[2,128,256]{2,1,0:T(8,128)(2,1)S(1)}, u32[]{:S(2)}, u32[]{:S(2)}) collective-permute-start(bf16[2,128,256]{2,1,0:T(8,128)(2,1)S(1)} %collective-permute-done.3), channel_id=1, source_target_pairs={{0,2},{1,3},{2,4},{3,5},{4,6},{5,7},{6,8},{7,9},{8,10},{9,11},{10,... | collective-permute-start | bytes 393224 | tf_op jit(solution)/shard_map/ppermute | solution.py:111
  97.4 5.1 %collective-permute-start.6 = (bf16[2,128,256]{2,1,0:T(8,128)(2,1)S(1)}, bf16[2,128,256]{2,1,0:T(8,128)(2,1)S(1)}, u32[]{:S(2)}, u32[]{:S(2)}) collective-permute-start(bf16[2,128,256]{2,1,0:T(8,128)(2,1)S(1)} %collective-permute-done.4), channel_id=1, source_target_pairs={{0,14},{1,15},{2,0},{3,1},{4,2},{5,3},{6,4},{7,5},{8,6},{9,7},{10,... | collective-permute-start | bytes 393224 | tf_op jit(solution)/shard_map/ppermute | solution.py:115
  102.6 1.0 collective-permute-done.5
  103.5 1.9 %collective-permute-start.7 = (bf16[2,128,256]{2,1,0:T(8,128)(2,1)S(1)}, bf16[2,128,256]{2,1,0:T(8,128)(2,1)S(1)}, u32[]{:S(2)}, u32[]{:S(2)}) collective-permute-start(bf16[2,128,256]{2,1,0:T(8,128)(2,1)S(1)} %collective-permute-done.5), channel_id=1, source_target_pairs={{0,2},{1,3},{2,4},{3,5},{4,6},{5,7},{6,8},{7,9},{8,10},{9,11},{10,... | collective-permute-start | bytes 393224 | tf_op jit(solution)/shard_map/ppermute | solution.py:111
  105.5 6.1 %collective-permute-done.7 = bf16[2,128,256]{2,1,0:T(8,128)(2,1)S(1)} collective-permute-done((bf16[2,128,256]{2,1,0:T(8,128)(2,1)S(1)}, bf16[2,128,256]{2,1,0:T(8,128)(2,1)S(1)}, u32[]{:S(2)}, u32[]{:S(2)}) %collective-permute-start.7) | collective-permute-done | bytes 131104 | tf_op jit(solution)/shard_map/ppermute | solution.py:111
  111.6 1.1 fusion.4
  (44 shorter events, 1.4 us)
Async XLA Ops:
  0.0 85.2 %copy-start = (bf16[4096,256]{1,0:T(8,128)(2,1)S(1)}, bf16[4096,256]{1,0:T(8,128)(2,1)}, u32[]{:S(2)}) copy-start(bf16[4096,256]{1,0:T(8,128)(2,1)} %param.13) | copy-start | bytes 6291460
  3.9 33.1 %all-to-all-start = ((bf16[64,3,4,128]{3,2,1,0:T(4,128)(2,1)}), bf16[64,3,4,128]{3,2,1,0:T(4,128)(2,1)}, u32[]{:S(2)}, u32[]{:S(2)}) async-start(bf16[64,3,4,128]{3,2,1,0:T(4,128)(2,1)} %copy.57), calls=%async_computation | async-start | bytes 393216 | tf_op jit(solution)/shard_map/all_to_all | solution.py:140
  42.9 3.7 %copy-start.2 = (f32[128,128]{1,0:T(8,128)S(1)}, f32[128,128]{1,0:T(8,128)}, u32[]{:S(2)}) copy-start(f32[128,128]{1,0:T(8,128)} %fusion.63) | copy-start | bytes 196612
  43.7 3.3 %copy-start.3 = (f32[128,128]{1,0:T(8,128)S(1)}, f32[128,128]{1,0:T(8,128)}, u32[]{:S(2)}) copy-start(f32[128,128]{1,0:T(8,128)} %fusion.62) | copy-start | bytes 196612
  43.7 3.8 %copy-start.5 = (f32[4]{0:T(128)S(1)}, f32[4]{0:T(128)}, u32[]{:S(2)}) copy-start(f32[4]{0:T(128)} %get-tuple-element.10) | copy-start | bytes 52
  43.7 3.8 %copy-start.6 = (f32[4]{0:T(128)S(1)}, f32[4]{0:T(128)}, u32[]{:S(2)}) copy-start(f32[4]{0:T(128)} %get-tuple-element.16) | copy-start | bytes 52
  43.7 3.8 %copy-start.7 = (f32[4]{0:T(128)S(1)}, f32[4]{0:T(128)}, u32[]{:S(2)}) copy-start(f32[4]{0:T(128)} %get-tuple-element.17) | copy-start | bytes 52
  43.7 3.8 %copy-start.8 = (f32[4]{0:T(128)S(1)}, f32[4]{0:T(128)}, u32[]{:S(2)}) copy-start(f32[4]{0:T(128)} %param.12) | copy-start | bytes 52
  45.2 12.0 %copy-start.4 = (s32[8,1]{0,1:T(1,128)S(1)}, s32[8,1]{0,1:T(1,128)}, u32[]{:S(2)}) copy-start(s32[8,1]{0,1:T(1,128)} %stack.108) | copy-start | bytes 100
  48.4 18.9 %all-to-all-start.1 = ((bf16[64,4,128]{2,1,0:T(4,128)(2,1)}), bf16[64,4,128]{2,1,0:T(4,128)(2,1)S(1)}, u32[]{:S(2)}, u32[]{:S(2)}) async-start(bf16[64,4,128]{2,1,0:T(4,128)(2,1)} %fusion.29), calls=%async_computation.1 | async-start | bytes 131072 | tf_op jit(solution)/shard_map/all_to_all | solution.py:148
  67.4 10.8 %collective-permute-start = (bf16[128,256]{1,0:T(8,128)(2,1)S(1)}, bf16[128,256]{1,0:T(8,128)(2,1)S(1)}, u32[]{:S(2)}, u32[]{:S(2)}) collective-permute-start(bf16[128,256]{1,0:T(8,128)(2,1)S(1)} %bitcast.183), channel_id=1, source_target_pairs={{0,1},{1,0},{2,3},{3,2},{4,5},{5,4},{6,7},{7,6},{8,9},{9,8},{10,11... | collective-permute-start | bytes 196616 | tf_op jit(solution)/shard_map/ppermute | solution.py:104
  78.1 9.1 %collective-permute-start.1 = (bf16[2,128,256]{2,1,0:T(8,128)(2,1)S(1)}, bf16[2,128,256]{2,1,0:T(8,128)(2,1)S(1)}, u32[]{:S(2)}, u32[]{:S(2)}) collective-permute-start(bf16[2,128,256]{2,1,0:T(8,128)(2,1)S(1)} %pad_maximum_fusion), channel_id=1, source_target_pairs={{0,2},{1,3},{2,4},{3,5},{4,6},{5,7},{6,8},{7,9},{8,10},{9,11},{10,... | collective-permute-start | bytes 393224 | tf_op jit(solution)/shard_map/ppermute | solution.py:111
  81.4 8.1 %collective-permute-start.2 = (bf16[2,128,256]{2,1,0:T(8,128)(2,1)S(1)}, bf16[2,128,256]{2,1,0:T(8,128)(2,1)S(1)}, u32[]{:S(2)}, u32[]{:S(2)}) collective-permute-start(bf16[2,128,256]{2,1,0:T(8,128)(2,1)S(1)} %pad_maximum_fusion), channel_id=1, source_target_pairs={{0,14},{1,15},{2,0},{3,1},{4,2},{5,3},{6,4},{7,5},{8,6},{9,7},{10,... | collective-permute-start | bytes 393224 | tf_op jit(solution)/shard_map/ppermute | solution.py:115
  87.3 24.4 %copy-start.1 = (bf16[16,256,256]{2,1,0:T(8,128)(2,1)S(1)}, bf16[16,256,256]{2,1,0:T(8,128)(2,1)}, u32[]{:S(2)}) copy-start(bf16[16,256,256]{2,1,0:T(8,128)(2,1)} %gather_fusion) | copy-start | bytes 6291460
  87.3 8.2 %collective-permute-start.3 = (bf16[2,128,256]{2,1,0:T(8,128)(2,1)S(1)}, bf16[2,128,256]{2,1,0:T(8,128)(2,1)S(1)}, u32[]{:S(2)}, u32[]{:S(2)}) collective-permute-start(bf16[2,128,256]{2,1,0:T(8,128)(2,1)S(1)} %collective-permute-done.1), channel_id=1, source_target_pairs={{0,2},{1,3},{2,4},{3,5},{4,6},{5,7},{6,8},{7,9},{8,10},{9,11},{10,... | collective-permute-start | bytes 393224 | tf_op jit(solution)/shard_map/ppermute | solution.py:111
  89.4 8.0 %collective-permute-start.4 = (bf16[2,128,256]{2,1,0:T(8,128)(2,1)S(1)}, bf16[2,128,256]{2,1,0:T(8,128)(2,1)S(1)}, u32[]{:S(2)}, u32[]{:S(2)}) collective-permute-start(bf16[2,128,256]{2,1,0:T(8,128)(2,1)S(1)} %collective-permute-done.2), channel_id=1, source_target_pairs={{0,14},{1,15},{2,0},{3,1},{4,2},{5,3},{6,4},{7,5},{8,6},{9,7},{10,... | collective-permute-start | bytes 393224 | tf_op jit(solution)/shard_map/ppermute | solution.py:115
  95.5 8.1 %collective-permute-start.5 = (bf16[2,128,256]{2,1,0:T(8,128)(2,1)S(1)}, bf16[2,128,256]{2,1,0:T(8,128)(2,1)S(1)}, u32[]{:S(2)}, u32[]{:S(2)}) collective-permute-start(bf16[2,128,256]{2,1,0:T(8,128)(2,1)S(1)} %collective-permute-done.3), channel_id=1, source_target_pairs={{0,2},{1,3},{2,4},{3,5},{4,6},{5,7},{6,8},{7,9},{8,10},{9,11},{10,... | collective-permute-start | bytes 393224 | tf_op jit(solution)/shard_map/ppermute | solution.py:111
  97.4 8.1 %collective-permute-start.6 = (bf16[2,128,256]{2,1,0:T(8,128)(2,1)S(1)}, bf16[2,128,256]{2,1,0:T(8,128)(2,1)S(1)}, u32[]{:S(2)}, u32[]{:S(2)}) collective-permute-start(bf16[2,128,256]{2,1,0:T(8,128)(2,1)S(1)} %collective-permute-done.4), channel_id=1, source_target_pairs={{0,14},{1,15},{2,0},{3,1},{4,2},{5,3},{6,4},{7,5},{8,6},{9,7},{10,... | collective-permute-start | bytes 393224 | tf_op jit(solution)/shard_map/ppermute | solution.py:115
  103.5 8.1 %collective-permute-start.7 = (bf16[2,128,256]{2,1,0:T(8,128)(2,1)S(1)}, bf16[2,128,256]{2,1,0:T(8,128)(2,1)S(1)}, u32[]{:S(2)}, u32[]{:S(2)}) collective-permute-start(bf16[2,128,256]{2,1,0:T(8,128)(2,1)S(1)} %collective-permute-done.5), channel_id=1, source_target_pairs={{0,2},{1,3},{2,4},{3,5},{4,6},{5,7},{6,8},{7,9},{8,10},{9,11},{10,... | collective-permute-start | bytes 393224 | tf_op jit(solution)/shard_map/ppermute | solution.py:111

commit v8 on v7

--- a/solution.py
+++ b/solution.py
@@ -3,7 +3,7 @@
 import jax
 import jax.numpy as jnp
 from jax import lax
-from jax.sharding import PartitionSpec as P
+from jax.sharding import Mesh, PartitionSpec as P
 
 HIGHEST_MODE = lax.Precision.HIGHEST
 
@@ -90,33 +90,23 @@
     return result.reshape(channels, length) / total + gains[:, None] * signal
 
 
-def chan_route(size, step):
-    pairs = size // 2
-    return [(x * 2 + h, ((x + step) % pairs) * 2 + h) for x in range(pairs) for h in range(2)]
-
-
-def gather_chan(block):
-    size = lax.axis_size("chan")
-    pairs = size // 2
-    me = lax.axis_index("chan")
-    mine_x = me // 2
-    mine_h = me % 2
-    partner = lax.ppermute(block, "chan", [(i, i ^ 1) for i in range(size)])
-    held = jnp.stack([block, partner])
+def gather_pairs(held):
+    size = lax.axis_size("x")
+    mine = lax.axis_index("x")
     slots = [held]
-    places = [mine_x]
+    places = [mine]
     right = held
     left = held
-    for step in range(1, pairs // 2 + 1):
-        right = lax.ppermute(right, "chan", chan_route(size, 1))
+    for step in range(1, size // 2 + 1):
+        right = lax.ppermute(right, "x", [(i, (i + 1) % size) for i in range(size)])
         slots.append(right)
-        places.append((mine_x - step) % pairs)
-        if step < pairs - step:
-            left = lax.ppermute(left, "chan", chan_route(size, -1))
+        places.append((mine - step) % size)
+        if step < size - step:
+            left = lax.ppermute(left, "x", [(i, (i - 1) % size) for i in range(size)])
             slots.append(left)
-            places.append((mine_x + step) % pairs)
+            places.append((mine + step) % size)
     place = jnp.stack(places)
-    order = jnp.stack([place * 2 + mine_h, place * 2 + (1 - mine_h)], axis=1)
+    order = jnp.stack([place * 2, place * 2 + 1], axis=1)
     return jnp.stack(slots), order
 
 
@@ -133,11 +123,11 @@
 
 def body(queries, keys, values, short_taps, long_filter, skip_gain, out_weight):
     rows, width = queries.shape
-    groups = lax.axis_size("seq")
+    groups = lax.axis_size(SEQ)
     per_group = width // groups
-    seq_index = lax.axis_index("seq")
+    seq_index = lax.axis_index(SEQ)
     raw = jnp.stack([queries.T, keys.T, values.T]).reshape(3, groups, per_group, rows).transpose(1, 0, 2, 3)
-    split_raw = lax.all_to_all(raw, "seq", split_axis=0, concat_axis=0, tiled=True)
+    split_raw = lax.all_to_all(raw, SEQ, split_axis=0, concat_axis=0, tiled=True)
     whole = split_raw.transpose(1, 2, 0, 3).reshape(3, per_group, groups * rows).astype(jnp.float32)
     own_taps = lax.dynamic_slice_in_dim(short_taps, seq_index * per_group, per_group, axis=2)
     short_q = causal_filter(whole[0], own_taps[0]).astype(jnp.bfloat16)
@@ -145,23 +135,30 @@
     convolved = long_convolution(signal, long_filter, skip_gain).astype(jnp.bfloat16)
     gated_t = (short_q.astype(jnp.float32) * convolved.astype(jnp.float32)).astype(jnp.bfloat16)
     outgoing = gated_t.reshape(per_group, groups, rows).transpose(1, 0, 2)
-    returned = lax.all_to_all(outgoing, "seq", split_axis=0, concat_axis=0, tiled=True)
-    gated = returned.reshape(width, rows).T
-    pieces, order = gather_chan(gated)
+    both = jnp.broadcast_to(outgoing[None], (2,) + outgoing.shape).reshape((2 * groups,) + outgoing.shape[1:])
+    returned = lax.all_to_all(both, ("yh",) + SEQ, split_axis=0, concat_axis=0, tiled=True)
+    held = returned.reshape(2, width, rows).transpose(0, 2, 1)
+    pieces, order = gather_pairs(held)
     weight = out_weight.reshape(-1, width, out_weight.shape[1])[order]
     result = jnp.einsum("pqtc,pqcj->tj", pieces, weight, preferred_element_type=jnp.float32)
     return result.astype(jnp.bfloat16)
 
 
+SEQ = ("z", "ylo", "core")
+CHAN = ("x", "yh")
+
+
 def solution(mesh):
+    shape = mesh.devices.shape
+    fine = Mesh(mesh.devices.reshape(shape[0] // 8, 4, 2, shape[1] // 2, 2), SEQ + CHAN)
     in_specs = (
-        P("seq", "chan"),
-        P("seq", "chan"),
-        P("seq", "chan"),
-        P(None, None, "chan"),
-        P(("chan", "seq"), None),
-        P(("chan", "seq")),
-        P(None, "chan"),
+        P(SEQ, CHAN),
+        P(SEQ, CHAN),
+        P(SEQ, CHAN),
+        P(None, None, CHAN),
+        P(CHAN + SEQ, None),
+        P(CHAN + SEQ),
+        P(None, CHAN),
     )
-    out_specs = P("seq", "chan")
-    return jax.shard_map(body, mesh=mesh, in_specs=in_specs, out_specs=out_specs, check_vma=False)
+    out_specs = P(SEQ, CHAN)
+    return jax.shard_map(body, mesh=fine, in_specs=in_specs, out_specs=out_specs, check_vma=False)

time: 113 us -> 106 us (0.938)
  starting transfers between devices: 58.9 us -> 54.9 us
  waiting for transfers between devices: 24.7 us -> 21.1 us
    ppermute x8 -> x7, starting transfers between devices: 28.7 us -> 23.2 us  [the longest x3 14.8 us: gather_pairs(): left = lax.ppermute(left, 'x', [(i, (i - 1) % size) for i in range(size)])]
    ppermute x8 -> x7, waiting for transfers between devices: 13.1 us -> 9.55 us  [the longest x4 9.54 us: gather_pairs(): right = lax.ppermute(right, 'x', [(i, (i + 1) % size) for i in range(size)])]
    all_to_all x2, starting transfers between devices: 30.2 us -> 31.7 us  [the longest x1 21.3 us: body(): lax.all_to_all(raw, SEQ, split_axis=0, concat_axis=0, tiled=True)]
    unnamed x29 -> x31, local copies, waits for them, and re-layouts: 4.07 us -> 4.1 us
  transfers between devices with their start and end apart: 10 -> 9, of which waited for: 6 -> 6; matrix products, arithmetic and copies ran while one was open for 11% -> 12% of each run, Pallas kernels for 0% -> 0%
where the time goes in v8:
time: 106 us; the launch traced here: 105 us
  starting transfers between devices  54.9 us (52%)
  waiting for transfers between devices  21.1 us (20%)
  matrix products  13.7 us (13%)
  local copies, waits for them, and re-layouts  10.3 us (10%)
  other arithmetic  4.7 us (4%)
    all_to_all x1, starting transfers between devices, body(): lax.all_to_all(raw, SEQ, split_axis=0, concat_axis=0, tiled=True)  21.3 us
    ppermute x3, starting transfers between devices, gather_pairs(): left = lax.ppermute(left, 'x', [(i, (i - 1) % size) for i in range(size)])  14.8 us
    all_to_all x1, starting transfers between devices, body(): lax.all_to_all(both, ('yh',) + SEQ, split_axis=0, concat_axis=0, tiled=True)  10.4 us
    all_to_all x1, waiting for transfers between devices, body(): lax.all_to_all(both, ('yh',) + SEQ, split_axis=0, concat_axis=0, tiled=True)  9.88 us
    ppermute x4, waiting for transfers between devices, gather_pairs(): right = lax.ppermute(right, 'x', [(i, (i + 1) % size) for i in range(size)])  9.54 us
    ppermute x4, starting transfers between devices, gather_pairs(): right = lax.ppermute(right, 'x', [(i, (i + 1) % size) for i in range(size)])  8.36 us
    unnamed x31, local copies, waits for them, and re-layouts  4.1 us
  transfers between devices with their start and end apart: 9, of which 6 were waited for; matrix products, arithmetic and copies ran while one was open for 12% of the time, Pallas kernels for 0%

profile of v8, /device:TPU:8, one launch (start us, length us, event | category | flops | bytes accessed | tf_op | source)
XLA Modules:
  0.0 105.3 jit_solution(9038971222581191967)
XLA Ops:
  0.0 1.1 %copy.55 = bf16[128,256]{0,1:T(8,128)(2,1)S(1)} copy(bf16[128,256]{1,0:T(8,128)(2,1)} %param.7) | data formatting | bytes 131072 | tf_op args[0]
  1.1 1.0 copy.56
  2.1 1.0 copy.57
  3.2 0.7 copy.58
  3.9 21.3 %all-to-all-start = ((bf16[64,3,4,128]{3,2,1,0:T(4,128)(2,1)}), bf16[64,3,4,128]{3,2,1,0:T(4,128)(2,1)}, u32[]{:S(2)}, u32[]{:S(2)}) async-start(bf16[64,3,4,128]{3,2,1,0:T(4,128)(2,1)} %copy.58), calls=%async_computation | async-start | bytes 393216 | tf_op jit(solution)/shard_map/all_to_all | solution.py:130
  25.3 0.9 fusion.63
  26.7 0.9 pad_bitcast_fusion
  27.6 0.7 fusion
  28.3 0.7 convolution_bitcast_fusion
  29.3 0.8 fusion.42
  30.0 0.7 fusion.46
  30.8 0.8 convolution_subtract_fusion.1
  31.6 1.5 %fusion.97 = (f32[4]{0:T(128)}, f32[4]{0:T(128)S(1)}, f32[4]{0:T(128)S(1)}, f32[4]{0:T(128)S(1)}, f32[4]{0:T(128)S(1)}, /*index=5*/f32[4]{0:T(128)}, f32[4]{0:T(128)}, f32[4]{0:T(128)}, f32[4]{0:T(128)}) fusion(f32[3,3,256]{2,1,0:T(4,128)} %param.10, s32[]{:T(128)S(6)} %select_n.119, s32[]{:T(128)S(6)} %add.242, s32[]{:T(128)S(6)} %add.241), kind=kLoop, calls=%fused_computation.135 | loop fusion | bytes 300 | tf_op jit(solution)/shard_map/mul | solution.py:115
  33.1 0.7 stack.96
  33.7 0.9 fusion.62
  34.6 0.8 convolution_add_fusion.1
  35.4 1.7 %all-to-all-done = bf16[64,3,4,128]{3,2,1,0:T(4,128)(2,1)} async-done(((bf16[64,3,4,128]{3,2,1,0:T(4,128)(2,1)}), bf16[64,3,4,128]{3,2,1,0:T(4,128)(2,1)}, u32[]{:S(2)}, u32[]{:S(2)}) %all-to-all-start) | async-done | bytes 196640 | tf_op jit(solution)/shard_map/all_to_all | solution.py:130
  37.0 1.0 convert_bitcast_fusion
  38.1 1.0 fusion.59
  39.1 0.7 fusion.1
  39.9 0.7 convolution_bitcast_fusion.1
  40.6 0.8 fusion.44
  41.4 0.8 fusion.49
  42.1 0.8 convolution_add_fusion.2
  42.9 0.8 multiply_add_fusion
  43.7 0.7 fusion.30
  44.4 0.8 fusion.40
  45.2 0.6 convolution_add_fusion
  45.9 0.6 convolution_subtract_fusion
  46.5 0.5 fusion.12
  47.0 0.5 fusion.3
  47.5 0.3 fusion.29
  47.9 0.7 broadcast_in_dim.2
  48.5 10.4 %all-to-all-start.1 = ((bf16[128,4,128]{2,1,0:T(4,128)(2,1)}), bf16[128,4,128]{2,1,0:T(4,128)(2,1)S(1)}, u32[]{:S(2)}, u32[]{:S(2)}) async-start(bf16[128,4,128]{2,1,0:T(4,128)(2,1)} %bitcast.30), calls=%async_computation.1 | async-start | bytes 262144 | tf_op jit(solution)/shard_map/all_to_all | solution.py:139
  59.2 2.0 %gather_fusion = bf16[16,256,256]{2,1,0:T(8,128)(2,1)} fusion(bf16[16,256,256]{2,1,0:T(8,128)(2,1)S(1)} %bitcast.178, s32[1024]{0:T(1024)S(1)} %pad_clamp_fusion), kind=kCustom, calls=%fused_computation | custom fusion | bytes 4194368 | tf_op jit(solution)/shard_map/gather | solution.py:142
  61.2 9.9 %all-to-all-done.1 = bf16[128,4,128]{2,1,0:T(4,128)(2,1)S(1)} async-done(((bf16[128,4,128]{2,1,0:T(4,128)(2,1)}), bf16[128,4,128]{2,1,0:T(4,128)(2,1)S(1)}, u32[]{:S(2)}, u32[]{:S(2)}) %all-to-all-start.1) | async-done | bytes 131104 | tf_op jit(solution)/shard_map/all_to_all | solution.py:139
  71.2 2.6 %collective-permute-start = (bf16[2,128,256]{2,1,0:T(8,128)(2,1)S(1)}, bf16[2,128,256]{2,1,0:T(8,128)(2,1)S(1)}, u32[]{:S(2)}, u32[]{:S(2)}) collective-permute-start(bf16[2,128,256]{2,1,0:T(8,128)(2,1)S(1)} %bitcast.187), channel_id=1, source_target_pairs={{0,2},{2,4},{4,6},{6,8},{8,10},{10,12},{12,14},{14,0},{1,3},{3,5},... | collective-permute-start | bytes 393224 | tf_op jit(solution)/shard_map/ppermute | solution.py:101
  73.9 4.5 %collective-permute-start.1 = (bf16[2,128,256]{2,1,0:T(8,128)(2,1)S(1)}, bf16[2,128,256]{2,1,0:T(8,128)(2,1)S(1)}, u32[]{:S(2)}, u32[]{:S(2)}) collective-permute-start(bf16[2,128,256]{2,1,0:T(8,128)(2,1)S(1)} %bitcast.188), channel_id=1, source_target_pairs={{0,14},{2,0},{4,2},{6,4},{8,6},{10,8},{12,10},{14,12},{1,15},{3,1}... | collective-permute-start | bytes 393224 | tf_op jit(solution)/shard_map/ppermute | solution.py:105
  78.4 1.5 %collective-permute-done = bf16[2,128,256]{2,1,0:T(8,128)(2,1)S(1)} collective-permute-done((bf16[2,128,256]{2,1,0:T(8,128)(2,1)S(1)}, bf16[2,128,256]{2,1,0:T(8,128)(2,1)S(1)}, u32[]{:S(2)}, u32[]{:S(2)}) %collective-permute-start) | collective-permute-done | bytes 131104 | tf_op jit(solution)/shard_map/ppermute | solution.py:101
  80.0 1.9 %collective-permute-start.2 = (bf16[2,128,256]{2,1,0:T(8,128)(2,1)S(1)}, bf16[2,128,256]{2,1,0:T(8,128)(2,1)S(1)}, u32[]{:S(2)}, u32[]{:S(2)}) collective-permute-start(bf16[2,128,256]{2,1,0:T(8,128)(2,1)S(1)} %collective-permute-done), channel_id=1, source_target_pairs={{0,2},{2,4},{4,6},{6,8},{8,10},{10,12},{12,14},{14,0},{1,3},{3,5},... | collective-permute-start | bytes 393224 | tf_op jit(solution)/shard_map/ppermute | solution.py:101
  81.9 5.1 %collective-permute-start.3 = (bf16[2,128,256]{2,1,0:T(8,128)(2,1)S(1)}, bf16[2,128,256]{2,1,0:T(8,128)(2,1)S(1)}, u32[]{:S(2)}, u32[]{:S(2)}) collective-permute-start(bf16[2,128,256]{2,1,0:T(8,128)(2,1)S(1)} %collective-permute-done.1), channel_id=1, source_target_pairs={{0,14},{2,0},{4,2},{6,4},{8,6},{10,8},{12,10},{14,12},{1,15},{3,1}... | collective-permute-start | bytes 393224 | tf_op jit(solution)/shard_map/ppermute | solution.py:105
  87.1 1.0 collective-permute-done.2
  88.0 1.9 %collective-permute-start.4 = (bf16[2,128,256]{2,1,0:T(8,128)(2,1)S(1)}, bf16[2,128,256]{2,1,0:T(8,128)(2,1)S(1)}, u32[]{:S(2)}, u32[]{:S(2)}) collective-permute-start(bf16[2,128,256]{2,1,0:T(8,128)(2,1)S(1)} %collective-permute-done.2), channel_id=1, source_target_pairs={{0,2},{2,4},{4,6},{6,8},{8,10},{10,12},{12,14},{14,0},{1,3},{3,5},... | collective-permute-start | bytes 393224 | tf_op jit(solution)/shard_map/ppermute | solution.py:101
  90.0 5.1 %collective-permute-start.5 = (bf16[2,128,256]{2,1,0:T(8,128)(2,1)S(1)}, bf16[2,128,256]{2,1,0:T(8,128)(2,1)S(1)}, u32[]{:S(2)}, u32[]{:S(2)}) collective-permute-start(bf16[2,128,256]{2,1,0:T(8,128)(2,1)S(1)} %collective-permute-done.3), channel_id=1, source_target_pairs={{0,14},{2,0},{4,2},{6,4},{8,6},{10,8},{12,10},{14,12},{1,15},{3,1}... | collective-permute-start | bytes 393224 | tf_op jit(solution)/shard_map/ppermute | solution.py:105
  95.1 1.0 collective-permute-done.4
  96.1 1.9 %collective-permute-start.6 = (bf16[2,128,256]{2,1,0:T(8,128)(2,1)S(1)}, bf16[2,128,256]{2,1,0:T(8,128)(2,1)S(1)}, u32[]{:S(2)}, u32[]{:S(2)}) collective-permute-start(bf16[2,128,256]{2,1,0:T(8,128)(2,1)S(1)} %collective-permute-done.4), channel_id=1, source_target_pairs={{0,2},{2,4},{4,6},{6,8},{8,10},{10,12},{12,14},{14,0},{1,3},{3,5},... | collective-permute-start | bytes 393224 | tf_op jit(solution)/shard_map/ppermute | solution.py:101
  98.1 6.1 %collective-permute-done.6 = bf16[2,128,256]{2,1,0:T(8,128)(2,1)S(1)} collective-permute-done((bf16[2,128,256]{2,1,0:T(8,128)(2,1)S(1)}, bf16[2,128,256]{2,1,0:T(8,128)(2,1)S(1)}, u32[]{:S(2)}, u32[]{:S(2)}) %collective-permute-start.6) | collective-permute-done | bytes 131104 | tf_op jit(solution)/shard_map/ppermute | solution.py:101
  104.2 1.1 %fusion.4 = bf16[128,256]{1,0:T(8,128)(2,1)} fusion(bf16[8,2,128,256]{3,2,1,0:T(8,128)(2,1)S(1)} %bitcast_dynamic-update-slice_fusion.1, bf16[8,2,256,256]{3,2,1,0:T(8,128)(2,1)S(1)} %bitcast.179), kind=kOutput, calls=%fused_computation.17 | convolution fusion | flops 268468224 | bytes 3211264 | tf_op jit(solution)/shard_map/pqtc,pqcj->tj/dot_general | solution.py:143
  (44 shorter events, 1.5 us)
Async XLA Ops:
  0.0 59.2 %copy-start = (bf16[4096,256]{1,0:T(8,128)(2,1)S(1)}, bf16[4096,256]{1,0:T(8,128)(2,1)}, u32[]{:S(2)}) copy-start(bf16[4096,256]{1,0:T(8,128)(2,1)} %param.13) | copy-start | bytes 6291460
  3.9 33.1 %all-to-all-start = ((bf16[64,3,4,128]{3,2,1,0:T(4,128)(2,1)}), bf16[64,3,4,128]{3,2,1,0:T(4,128)(2,1)}, u32[]{:S(2)}, u32[]{:S(2)}) async-start(bf16[64,3,4,128]{3,2,1,0:T(4,128)(2,1)} %copy.58), calls=%async_computation | async-start | bytes 393216 | tf_op jit(solution)/shard_map/all_to_all | solution.py:130
  42.9 3.6 %copy-start.2 = (f32[128,128]{1,0:T(8,128)S(1)}, f32[128,128]{1,0:T(8,128)}, u32[]{:S(2)}) copy-start(f32[128,128]{1,0:T(8,128)} %fusion.63) | copy-start | bytes 196612
  43.7 3.3 %copy-start.3 = (f32[128,128]{1,0:T(8,128)S(1)}, f32[128,128]{1,0:T(8,128)}, u32[]{:S(2)}) copy-start(f32[128,128]{1,0:T(8,128)} %fusion.62) | copy-start | bytes 196612
  43.7 3.8 %copy-start.4 = (f32[4]{0:T(128)S(1)}, f32[4]{0:T(128)}, u32[]{:S(2)}) copy-start(f32[4]{0:T(128)} %get-tuple-element.10) | copy-start | bytes 52
  43.7 3.8 %copy-start.5 = (f32[4]{0:T(128)S(1)}, f32[4]{0:T(128)}, u32[]{:S(2)}) copy-start(f32[4]{0:T(128)} %get-tuple-element.16) | copy-start | bytes 52
  43.7 3.8 %copy-start.6 = (f32[4]{0:T(128)S(1)}, f32[4]{0:T(128)}, u32[]{:S(2)}) copy-start(f32[4]{0:T(128)} %get-tuple-element.17) | copy-start | bytes 52
  43.7 3.8 %copy-start.8 = (f32[4]{0:T(128)S(1)}, f32[4]{0:T(128)}, u32[]{:S(2)}) copy-start(f32[4]{0:T(128)} %param.12) | copy-start | bytes 52
  45.9 13.1 %copy-start.7 = (s32[8,1]{0,1:T(1,128)S(1)}, s32[8,1]{0,1:T(1,128)}, u32[]{:S(2)}) copy-start(s32[8,1]{0,1:T(1,128)} %stack.96) | copy-start | bytes 100
  48.5 22.6 %all-to-all-start.1 = ((bf16[128,4,128]{2,1,0:T(4,128)(2,1)}), bf16[128,4,128]{2,1,0:T(4,128)(2,1)S(1)}, u32[]{:S(2)}, u32[]{:S(2)}) async-start(bf16[128,4,128]{2,1,0:T(4,128)(2,1)} %bitcast.30), calls=%async_computation.1 | async-start | bytes 262144 | tf_op jit(solution)/shard_map/all_to_all | solution.py:139
  71.2 33.0 %copy-start.1 = (bf16[16,256,256]{2,1,0:T(8,128)(2,1)S(1)}, bf16[16,256,256]{2,1,0:T(8,128)(2,1)}, u32[]{:S(2)}) copy-start(bf16[16,256,256]{2,1,0:T(8,128)(2,1)} %gather_fusion) | copy-start | bytes 6291460
  71.2 8.8 %collective-permute-start = (bf16[2,128,256]{2,1,0:T(8,128)(2,1)S(1)}, bf16[2,128,256]{2,1,0:T(8,128)(2,1)S(1)}, u32[]{:S(2)}, u32[]{:S(2)}) collective-permute-start(bf16[2,128,256]{2,1,0:T(8,128)(2,1)S(1)} %bitcast.187), channel_id=1, source_target_pairs={{0,2},{2,4},{4,6},{6,8},{8,10},{10,12},{12,14},{14,0},{1,3},{3,5},... | collective-permute-start | bytes 393224 | tf_op jit(solution)/shard_map/ppermute | solution.py:101
  73.9 8.0 %collective-permute-start.1 = (bf16[2,128,256]{2,1,0:T(8,128)(2,1)S(1)}, bf16[2,128,256]{2,1,0:T(8,128)(2,1)S(1)}, u32[]{:S(2)}, u32[]{:S(2)}) collective-permute-start(bf16[2,128,256]{2,1,0:T(8,128)(2,1)S(1)} %bitcast.188), channel_id=1, source_target_pairs={{0,14},{2,0},{4,2},{6,4},{8,6},{10,8},{12,10},{14,12},{1,15},{3,1}... | collective-permute-start | bytes 393224 | tf_op jit(solution)/shard_map/ppermute | solution.py:105
  80.0 8.1 %collective-permute-start.2 = (bf16[2,128,256]{2,1,0:T(8,128)(2,1)S(1)}, bf16[2,128,256]{2,1,0:T(8,128)(2,1)S(1)}, u32[]{:S(2)}, u32[]{:S(2)}) collective-permute-start(bf16[2,128,256]{2,1,0:T(8,128)(2,1)S(1)} %collective-permute-done), channel_id=1, source_target_pairs={{0,2},{2,4},{4,6},{6,8},{8,10},{10,12},{12,14},{14,0},{1,3},{3,5},... | collective-permute-start | bytes 393224 | tf_op jit(solution)/shard_map/ppermute | solution.py:101
  81.9 8.1 %collective-permute-start.3 = (bf16[2,128,256]{2,1,0:T(8,128)(2,1)S(1)}, bf16[2,128,256]{2,1,0:T(8,128)(2,1)S(1)}, u32[]{:S(2)}, u32[]{:S(2)}) collective-permute-start(bf16[2,128,256]{2,1,0:T(8,128)(2,1)S(1)} %collective-permute-done.1), channel_id=1, source_target_pairs={{0,14},{2,0},{4,2},{6,4},{8,6},{10,8},{12,10},{14,12},{1,15},{3,1}... | collective-permute-start | bytes 393224 | tf_op jit(solution)/shard_map/ppermute | solution.py:105
  88.0 8.1 %collective-permute-start.4 = (bf16[2,128,256]{2,1,0:T(8,128)(2,1)S(1)}, bf16[2,128,256]{2,1,0:T(8,128)(2,1)S(1)}, u32[]{:S(2)}, u32[]{:S(2)}) collective-permute-start(bf16[2,128,256]{2,1,0:T(8,128)(2,1)S(1)} %collective-permute-done.2), channel_id=1, source_target_pairs={{0,2},{2,4},{4,6},{6,8},{8,10},{10,12},{12,14},{14,0},{1,3},{3,5},... | collective-permute-start | bytes 393224 | tf_op jit(solution)/shard_map/ppermute | solution.py:101
  90.0 8.1 %collective-permute-start.5 = (bf16[2,128,256]{2,1,0:T(8,128)(2,1)S(1)}, bf16[2,128,256]{2,1,0:T(8,128)(2,1)S(1)}, u32[]{:S(2)}, u32[]{:S(2)}) collective-permute-start(bf16[2,128,256]{2,1,0:T(8,128)(2,1)S(1)} %collective-permute-done.3), channel_id=1, source_target_pairs={{0,14},{2,0},{4,2},{6,4},{8,6},{10,8},{12,10},{14,12},{1,15},{3,1}... | collective-permute-start | bytes 393224 | tf_op jit(solution)/shard_map/ppermute | solution.py:105
  96.1 8.1 %collective-permute-start.6 = (bf16[2,128,256]{2,1,0:T(8,128)(2,1)S(1)}, bf16[2,128,256]{2,1,0:T(8,128)(2,1)S(1)}, u32[]{:S(2)}, u32[]{:S(2)}) collective-permute-start(bf16[2,128,256]{2,1,0:T(8,128)(2,1)S(1)} %collective-permute-done.4), channel_id=1, source_target_pairs={{0,2},{2,4},{4,6},{6,8},{8,10},{10,12},{12,14},{14,0},{1,3},{3,5},... | collective-permute-start | bytes 393224 | tf_op jit(solution)/shard_map/ppermute | solution.py:101

commit v9 on v8

--- a/solution.py
+++ b/solution.py
@@ -32,22 +32,26 @@
     return (best, total // best)
 
 
+def rotation(cos_t, sin_t, sign):
+    return jnp.concatenate(
+        [jnp.concatenate([cos_t, sign * sin_t], 1), jnp.concatenate([-sign * sin_t, cos_t], 1)], 0
+    )
+
+
 def spectrum(signal, inner, outer, outer_tables, inner_tables, turn_tables):
     cos_out, sin_out = outer_tables
     cos_in, sin_in = inner_tables
     turn_cos, turn_sin = turn_tables
-    blocks = signal.reshape(signal.shape[0], outer, inner)
-    first_re = jnp.einsum("kn,cnm->ckm", cos_out, blocks, precision=HIGHEST_MODE)
-    first_im = -jnp.einsum("kn,cnm->ckm", sin_out, blocks, precision=HIGHEST_MODE)
+    used = signal.shape[1] // inner
+    blocks = signal.reshape(signal.shape[0], used, inner)
+    stacked = jnp.concatenate([cos_out[:, :used], -sin_out[:, :used]], 0)
+    first = jnp.einsum("kn,cnm->ckm", stacked, blocks, precision=HIGHEST_MODE)
+    first_re, first_im = first[:, :outer], first[:, outer:]
     turned_re = first_re * turn_cos + first_im * turn_sin
     turned_im = first_im * turn_cos - first_re * turn_sin
-    real_part = jnp.einsum("ckm,mj->ckj", turned_re, cos_in, precision=HIGHEST_MODE) + jnp.einsum(
-        "ckm,mj->ckj", turned_im, sin_in, precision=HIGHEST_MODE
-    )
-    imag_part = jnp.einsum("ckm,mj->ckj", turned_im, cos_in, precision=HIGHEST_MODE) - jnp.einsum(
-        "ckm,mj->ckj", turned_re, sin_in, precision=HIGHEST_MODE
-    )
-    return (real_part, imag_part)
+    turned = jnp.concatenate([turned_re, turned_im], 2)
+    second = jnp.einsum("ckm,mj->ckj", turned, rotation(cos_in, sin_in, -1.0), precision=HIGHEST_MODE)
+    return (second[..., :inner], second[..., inner:])
 
 
 def long_convolution(mixed, filters, gains):
@@ -58,35 +62,21 @@
     inner_tables = tables(inner)
     turn_tables = twiddle(outer, inner, total)
     signal = mixed.astype(jnp.float32)
-    padding = jnp.zeros((channels, length), jnp.float32)
-    sig_re, sig_im = spectrum(
-        jnp.concatenate([signal, padding], 1), inner, outer, outer_tables, inner_tables, turn_tables
-    )
-    fil_re, fil_im = spectrum(
-        jnp.concatenate([filters, padding], 1),
-        inner,
-        outer,
-        outer_tables,
-        inner_tables,
-        turn_tables,
-    )
+    sig_re, sig_im = spectrum(signal, inner, outer, outer_tables, inner_tables, turn_tables)
+    fil_re, fil_im = spectrum(filters, inner, outer, outer_tables, inner_tables, turn_tables)
     prod_re = sig_re * fil_re - sig_im * fil_im
     prod_im = sig_re * fil_im + sig_im * fil_re
     cos_in, sin_in = inner_tables
-    back_re = jnp.einsum("ckj,jm->ckm", prod_re, cos_in, precision=HIGHEST_MODE) - jnp.einsum(
-        "ckj,jm->ckm", prod_im, sin_in, precision=HIGHEST_MODE
-    )
-    back_im = jnp.einsum("ckj,jm->ckm", prod_re, sin_in, precision=HIGHEST_MODE) + jnp.einsum(
-        "ckj,jm->ckm", prod_im, cos_in, precision=HIGHEST_MODE
-    )
+    product = jnp.concatenate([prod_re, prod_im], 2)
+    back = jnp.einsum("ckj,jm->ckm", product, rotation(cos_in, sin_in, 1.0), precision=HIGHEST_MODE)
+    back_re, back_im = back[..., :inner], back[..., inner:]
     turn_cos, turn_sin = turn_tables
     rot_re = back_re * turn_cos - back_im * turn_sin
     rot_im = back_re * turn_sin + back_im * turn_cos
     cos_out, sin_out = outer_tables
     half = outer // 2
-    result = jnp.einsum("nk,ckm->cnm", cos_out[:half], rot_re, precision=HIGHEST_MODE) - jnp.einsum(
-        "nk,ckm->cnm", sin_out[:half], rot_im, precision=HIGHEST_MODE
-    )
+    stacked = jnp.concatenate([cos_out[:half], -sin_out[:half]], 1)
+    result = jnp.einsum("nk,ckm->cnm", stacked, jnp.concatenate([rot_re, rot_im], 1), precision=HIGHEST_MODE)
     return result.reshape(channels, length) / total + gains[:, None] * signal
 
 

time: 106 us -> 97 us (0.915)
  matrix products: 13.7 us -> 5.41 us
  waiting for transfers between devices: 21.1 us -> 28.7 us
  starting transfers between devices: 54.9 us -> 52 us
  other arithmetic: 4.7 us -> 1.9 us
  local copies, waits for them, and re-layouts: 10.3 us -> 8.01 us
    dot_general x18 -> x6, matrix products: 12.6 us -> 4.34 us  [the longest x2 1.99 us: spectrum(): jnp.einsum('ckm,mj->ckj', turned, rotation(cos_in, sin_in, -1.0), precisi...]
    all_to_all x1, waiting for transfers between devices: 1.65 us -> 9.25 us  [body(): lax.all_to_all(raw, SEQ, split_axis=0, concat_axis=0, tiled=True)]
    all_to_all x1, starting transfers between devices: 10.4 us -> 7.76 us  [body(): lax.all_to_all(both, ('yh',) + SEQ, split_axis=0, concat_axis=0, tiled=True)]
    cos x2 -> x0, other arithmetic: 1.14 us -> none  [the longest x1 0.89 us: tables(): return (jnp.cos(phase), jnp.sin(phase))]
    unnamed x31 -> x19, local copies, waits for them, and re-layouts: 4.1 us -> 3.12 us
  transfers between devices with their start and end apart: 9 -> 9, of which waited for: 6 -> 6; matrix products, arithmetic and copies ran while one was open for 12% -> 5% of each run, Pallas kernels for 0% -> 0%
where the time goes in v9:
time: 97 us; the launch traced here: 96.5 us
  starting transfers between devices  52 us (54%)
  waiting for transfers between devices  28.7 us (30%)
  local copies, waits for them, and re-layouts  8.01 us (8%)
  matrix products  5.41 us (6%)
  other arithmetic  1.9 us (2%)
    all_to_all x1, starting transfers between devices, body(): lax.all_to_all(raw, SEQ, split_axis=0, concat_axis=0, tiled=True)  21.1 us
    ppermute x3, starting transfers between devices, gather_pairs(): left = lax.ppermute(left, 'x', [(i, (i - 1) % size) for i in range(size)])  14.8 us
    all_to_all x1, waiting for transfers between devices, body(): lax.all_to_all(both, ('yh',) + SEQ, split_axis=0, concat_axis=0, tiled=True)  9.89 us
    ppermute x4, waiting for transfers between devices, gather_pairs(): right = lax.ppermute(right, 'x', [(i, (i + 1) % size) for i in range(size)])  9.54 us
    all_to_all x1, waiting for transfers between devices, body(): lax.all_to_all(raw, SEQ, split_axis=0, concat_axis=0, tiled=True)  9.25 us
    ppermute x4, starting transfers between devices, gather_pairs(): right = lax.ppermute(right, 'x', [(i, (i + 1) % size) for i in range(size)])  8.36 us
    all_to_all x1, starting transfers between devices, body(): lax.all_to_all(both, ('yh',) + SEQ, split_axis=0, concat_axis=0, tiled=True)  7.76 us
    unnamed x19, local copies, waits for them, and re-layouts  3.12 us
  transfers between devices with their start and end apart: 9, of which 6 were waited for; matrix products, arithmetic and copies ran while one was open for 5% of the time, Pallas kernels for 0%

profile of v9, /device:TPU:8, one launch (start us, length us, event | category | flops | bytes accessed | tf_op | source)
XLA Modules:
  0.0 96.5 jit_solution(14705159138980693513)
XLA Ops:
  0.0 1.1 %copy.37 = bf16[128,256]{0,1:T(8,128)(2,1)S(1)} copy(bf16[128,256]{1,0:T(8,128)(2,1)} %param.7) | data formatting | bytes 131072 | tf_op args[0]
  1.1 1.0 copy.38
  2.1 1.0 copy.39
  3.0 0.2 maximum_bitcast_fusion
  3.2 0.7 copy.40
  3.9 21.1 %all-to-all-start = ((bf16[64,3,4,128]{3,2,1,0:T(4,128)(2,1)}), bf16[64,3,4,128]{3,2,1,0:T(4,128)(2,1)S(1)}, u32[]{:S(2)}, u32[]{:S(2)}) async-start(bf16[64,3,4,128]{3,2,1,0:T(4,128)(2,1)} %copy.40), calls=%async_computation | async-start | bytes 393216 | tf_op jit(solution)/shard_map/all_to_all | solution.py:120
  25.0 0.3 broadcast_multiply_fusion
  25.3 0.3 fusion.47
  25.6 0.9 fusion.50
  26.6 0.1 stack.96
  26.8 0.3 fusion.45
  27.0 0.6 convolution_bitcast_fusion
  27.7 9.3 %all-to-all-done = bf16[64,3,4,128]{3,2,1,0:T(4,128)(2,1)S(1)} async-done(((bf16[64,3,4,128]{3,2,1,0:T(4,128)(2,1)}), bf16[64,3,4,128]{3,2,1,0:T(4,128)(2,1)S(1)}, u32[]{:S(2)}, u32[]{:S(2)}) %all-to-all-start) | async-done | bytes 196640 | tf_op jit(solution)/shard_map/all_to_all | solution.py:120
  37.0 0.1 slice_bitcast_fusion.2
  37.0 0.3 multiply_convert_fusion.1
  37.4 0.4 convolution_bitcast_fusion.1
  37.8 0.1 multiply_add_fusion.3
  38.0 1.0 %fusion.2 = f32[4,128,256]{2,1,0:T(8,128)S(1)} fusion(f32[4,128,128]{1,2,0:T(8,128)S(1)} %get-tuple-element.10, f32[4,128,128]{1,2,0:T(8,128)S(1)} %get-tuple-element.9, f32[128,128]{0,1:T(8,128)S(1)} %get-tuple-element.32, f32[128,128]{0,1:T(8,128)S(1)} %get-tuple-element.31, f32[128,128]{0,1:T(8,128)S(1)} %broadcast_multiply_fusion), kind=kOutput, calls=%fused_computation.7 | convolution fusion | flops 402980864 | bytes 1245184 | tf_op jit(solution)/shard_map/ckm,mj->ckj/dot_general | solution.py:53
  39.0 1.0 %fusion.6 = f32[4,128,256]{2,1,0:T(8,128)S(1)} fusion(f32[4,128,128]{1,2,0:T(8,128)S(1)} %get-tuple-element.16, f32[4,128,128]{1,2,0:T(8,128)S(1)} %get-tuple-element.17, f32[128,128]{0,1:T(8,128)S(1)} %get-tuple-element.32, f32[128,128]{0,1:T(8,128)S(1)} %get-tuple-element.31, f32[128,128]{0,1:T(8,128)S(1)} %broadcast_multiply_fusion), kind=kOutput, calls=%fused_computation.11 | convolution fusion | flops 402980864 | bytes 1245184 | tf_op jit(solution)/shard_map/ckm,mj->ckj/dot_general | solution.py:53
  40.0 0.0 copy-start.3
  40.0 0.1 multiply_subtract_fusion.1
  40.1 0.6 fusion.10
  40.7 0.1 multiply_subtract_fusion
  40.8 0.6 fusion
  41.4 0.2 fusion.35
  41.7 0.1 copy.50
  41.8 0.7 broadcast_in_dim.2
  42.5 7.8 %all-to-all-start.1 = ((bf16[128,4,128]{2,1,0:T(4,128)(2,1)}), bf16[128,4,128]{2,1,0:T(4,128)(2,1)S(1)}, u32[]{:S(2)}, u32[]{:S(2)}) async-start(bf16[128,4,128]{2,1,0:T(4,128)(2,1)} %bitcast.30), calls=%async_computation.1 | async-start | bytes 262144 | tf_op jit(solution)/shard_map/all_to_all | solution.py:129
  50.3 0.1 copy.52
  50.3 0.1 reshape.722
  50.4 2.0 %gather_fusion = bf16[16,256,256]{2,1,0:T(8,128)(2,1)} fusion(bf16[16,256,256]{2,1,0:T(8,128)(2,1)S(1)} %bitcast.139, s32[1024]{0:T(1024)S(1)} %pad_clamp_fusion), kind=kCustom, calls=%fused_computation | custom fusion | bytes 4194368 | tf_op jit(solution)/shard_map/gather | solution.py:132
  52.5 9.9 %all-to-all-done.1 = bf16[128,4,128]{2,1,0:T(4,128)(2,1)S(1)} async-done(((bf16[128,4,128]{2,1,0:T(4,128)(2,1)}), bf16[128,4,128]{2,1,0:T(4,128)(2,1)S(1)}, u32[]{:S(2)}, u32[]{:S(2)}) %all-to-all-start.1) | async-done | bytes 131104 | tf_op jit(solution)/shard_map/all_to_all | solution.py:129
  62.3 0.1 copy.51
  62.5 2.6 %collective-permute-start = (bf16[2,128,256]{2,1,0:T(8,128)(2,1)S(1)}, bf16[2,128,256]{2,1,0:T(8,128)(2,1)S(1)}, u32[]{:S(2)}, u32[]{:S(2)}) collective-permute-start(bf16[2,128,256]{2,1,0:T(8,128)(2,1)S(1)} %bitcast.150), channel_id=1, source_target_pairs={{0,2},{2,4},{4,6},{6,8},{8,10},{10,12},{12,14},{14,0},{1,3},{3,5},... | collective-permute-start | bytes 393224 | tf_op jit(solution)/shard_map/ppermute | solution.py:91
  65.1 4.6 %collective-permute-start.1 = (bf16[2,128,256]{2,1,0:T(8,128)(2,1)S(1)}, bf16[2,128,256]{2,1,0:T(8,128)(2,1)S(1)}, u32[]{:S(2)}, u32[]{:S(2)}) collective-permute-start(bf16[2,128,256]{2,1,0:T(8,128)(2,1)S(1)} %bitcast.151), channel_id=1, source_target_pairs={{0,14},{2,0},{4,2},{6,4},{8,6},{10,8},{12,10},{14,12},{1,15},{3,1}... | collective-permute-start | bytes 393224 | tf_op jit(solution)/shard_map/ppermute | solution.py:95
  69.7 1.5 %collective-permute-done = bf16[2,128,256]{2,1,0:T(8,128)(2,1)S(1)} collective-permute-done((bf16[2,128,256]{2,1,0:T(8,128)(2,1)S(1)}, bf16[2,128,256]{2,1,0:T(8,128)(2,1)S(1)}, u32[]{:S(2)}, u32[]{:S(2)}) %collective-permute-start) | collective-permute-done | bytes 131104 | tf_op jit(solution)/shard_map/ppermute | solution.py:91
  71.2 1.9 %collective-permute-start.2 = (bf16[2,128,256]{2,1,0:T(8,128)(2,1)S(1)}, bf16[2,128,256]{2,1,0:T(8,128)(2,1)S(1)}, u32[]{:S(2)}, u32[]{:S(2)}) collective-permute-start(bf16[2,128,256]{2,1,0:T(8,128)(2,1)S(1)} %collective-permute-done), channel_id=1, source_target_pairs={{0,2},{2,4},{4,6},{6,8},{8,10},{10,12},{12,14},{14,0},{1,3},{3,5},... | collective-permute-start | bytes 393224 | tf_op jit(solution)/shard_map/ppermute | solution.py:91
  73.1 0.0 collective-permute-done.1
  73.1 5.1 %collective-permute-start.3 = (bf16[2,128,256]{2,1,0:T(8,128)(2,1)S(1)}, bf16[2,128,256]{2,1,0:T(8,128)(2,1)S(1)}, u32[]{:S(2)}, u32[]{:S(2)}) collective-permute-start(bf16[2,128,256]{2,1,0:T(8,128)(2,1)S(1)} %collective-permute-done.1), channel_id=1, source_target_pairs={{0,14},{2,0},{4,2},{6,4},{8,6},{10,8},{12,10},{14,12},{1,15},{3,1}... | collective-permute-start | bytes 393224 | tf_op jit(solution)/shard_map/ppermute | solution.py:95
  78.3 1.0 collective-permute-done.2
  79.3 1.9 %collective-permute-start.4 = (bf16[2,128,256]{2,1,0:T(8,128)(2,1)S(1)}, bf16[2,128,256]{2,1,0:T(8,128)(2,1)S(1)}, u32[]{:S(2)}, u32[]{:S(2)}) collective-permute-start(bf16[2,128,256]{2,1,0:T(8,128)(2,1)S(1)} %collective-permute-done.2), channel_id=1, source_target_pairs={{0,2},{2,4},{4,6},{6,8},{8,10},{10,12},{12,14},{14,0},{1,3},{3,5},... | collective-permute-start | bytes 393224 | tf_op jit(solution)/shard_map/ppermute | solution.py:91
  81.2 0.0 collective-permute-done.3
  81.2 5.1 %collective-permute-start.5 = (bf16[2,128,256]{2,1,0:T(8,128)(2,1)S(1)}, bf16[2,128,256]{2,1,0:T(8,128)(2,1)S(1)}, u32[]{:S(2)}, u32[]{:S(2)}) collective-permute-start(bf16[2,128,256]{2,1,0:T(8,128)(2,1)S(1)} %collective-permute-done.3), channel_id=1, source_target_pairs={{0,14},{2,0},{4,2},{6,4},{8,6},{10,8},{12,10},{14,12},{1,15},{3,1}... | collective-permute-start | bytes 393224 | tf_op jit(solution)/shard_map/ppermute | solution.py:95
  86.4 1.0 collective-permute-done.4
  87.3 1.9 %collective-permute-start.6 = (bf16[2,128,256]{2,1,0:T(8,128)(2,1)S(1)}, bf16[2,128,256]{2,1,0:T(8,128)(2,1)S(1)}, u32[]{:S(2)}, u32[]{:S(2)}) collective-permute-start(bf16[2,128,256]{2,1,0:T(8,128)(2,1)S(1)} %collective-permute-done.4), channel_id=1, source_target_pairs={{0,2},{2,4},{4,6},{6,8},{8,10},{10,12},{12,14},{14,0},{1,3},{3,5},... | collective-permute-start | bytes 393224 | tf_op jit(solution)/shard_map/ppermute | solution.py:91
  89.3 0.0 collective-permute-done.5
  89.3 6.1 %collective-permute-done.6 = bf16[2,128,256]{2,1,0:T(8,128)(2,1)S(1)} collective-permute-done((bf16[2,128,256]{2,1,0:T(8,128)(2,1)S(1)}, bf16[2,128,256]{2,1,0:T(8,128)(2,1)S(1)}, u32[]{:S(2)}, u32[]{:S(2)}) %collective-permute-start.6) | collective-permute-done | bytes 131104 | tf_op jit(solution)/shard_map/ppermute | solution.py:91
  95.4 1.1 %fusion.1 = bf16[128,256]{1,0:T(8,128)(2,1)} fusion(bf16[8,2,128,256]{3,2,1,0:T(8,128)(2,1)S(1)} %bitcast_dynamic-update-slice_fusion.1, bf16[8,2,256,256]{3,2,1,0:T(8,128)(2,1)S(1)} %bitcast.140), kind=kOutput, calls=%fused_computation.6 | convolution fusion | flops 268468224 | bytes 3211264 | tf_op jit(solution)/shard_map/pqtc,pqcj->tj/dot_general | solution.py:133
  (23 shorter events, 0.2 us)
Async XLA Ops:
  0.0 50.4 %copy-start = (bf16[4096,256]{1,0:T(8,128)(2,1)S(1)}, bf16[4096,256]{1,0:T(8,128)(2,1)}, u32[]{:S(2)}) copy-start(bf16[4096,256]{1,0:T(8,128)(2,1)} %param.13) | copy-start | bytes 6291460
  0.0 27.0 %copy-start.2 = (f32[4,8192]{1,0:T(4,128)S(1)}, f32[4,8192]{1,0:T(4,128)}, u32[]{:S(2)}) copy-start(f32[4,8192]{1,0:T(4,128)} %param.11) | copy-start | bytes 393220
  3.9 33.0 %all-to-all-start = ((bf16[64,3,4,128]{3,2,1,0:T(4,128)(2,1)}), bf16[64,3,4,128]{3,2,1,0:T(4,128)(2,1)S(1)}, u32[]{:S(2)}, u32[]{:S(2)}) async-start(bf16[64,3,4,128]{3,2,1,0:T(4,128)(2,1)} %copy.40), calls=%async_computation | async-start | bytes 393216 | tf_op jit(solution)/shard_map/all_to_all | solution.py:120
  40.0 1.5 %copy-start.3 = (f32[4]{0:T(128)S(1)}, f32[4]{0:T(128)}, u32[]{:S(2)}) copy-start(f32[4]{0:T(128)} %param.12) | copy-start | bytes 52
  42.5 19.9 %all-to-all-start.1 = ((bf16[128,4,128]{2,1,0:T(4,128)(2,1)}), bf16[128,4,128]{2,1,0:T(4,128)(2,1)S(1)}, u32[]{:S(2)}, u32[]{:S(2)}) async-start(bf16[128,4,128]{2,1,0:T(4,128)(2,1)} %bitcast.30), calls=%async_computation.1 | async-start | bytes 262144 | tf_op jit(solution)/shard_map/all_to_all | solution.py:129
  62.5 33.0 %copy-start.1 = (bf16[16,256,256]{2,1,0:T(8,128)(2,1)S(1)}, bf16[16,256,256]{2,1,0:T(8,128)(2,1)}, u32[]{:S(2)}) copy-start(bf16[16,256,256]{2,1,0:T(8,128)(2,1)} %gather_fusion) | copy-start | bytes 6291460
  62.5 8.8 %collective-permute-start = (bf16[2,128,256]{2,1,0:T(8,128)(2,1)S(1)}, bf16[2,128,256]{2,1,0:T(8,128)(2,1)S(1)}, u32[]{:S(2)}, u32[]{:S(2)}) collective-permute-start(bf16[2,128,256]{2,1,0:T(8,128)(2,1)S(1)} %bitcast.150), channel_id=1, source_target_pairs={{0,2},{2,4},{4,6},{6,8},{8,10},{10,12},{12,14},{14,0},{1,3},{3,5},... | collective-permute-start | bytes 393224 | tf_op jit(solution)/shard_map/ppermute | solution.py:91
  65.1 8.0 %collective-permute-start.1 = (bf16[2,128,256]{2,1,0:T(8,128)(2,1)S(1)}, bf16[2,128,256]{2,1,0:T(8,128)(2,1)S(1)}, u32[]{:S(2)}, u32[]{:S(2)}) collective-permute-start(bf16[2,128,256]{2,1,0:T(8,128)(2,1)S(1)} %bitcast.151), channel_id=1, source_target_pairs={{0,14},{2,0},{4,2},{6,4},{8,6},{10,8},{12,10},{14,12},{1,15},{3,1}... | collective-permute-start | bytes 393224 | tf_op jit(solution)/shard_map/ppermute | solution.py:95
  71.2 8.1 %collective-permute-start.2 = (bf16[2,128,256]{2,1,0:T(8,128)(2,1)S(1)}, bf16[2,128,256]{2,1,0:T(8,128)(2,1)S(1)}, u32[]{:S(2)}, u32[]{:S(2)}) collective-permute-start(bf16[2,128,256]{2,1,0:T(8,128)(2,1)S(1)} %collective-permute-done), channel_id=1, source_target_pairs={{0,2},{2,4},{4,6},{6,8},{8,10},{10,12},{12,14},{14,0},{1,3},{3,5},... | collective-permute-start | bytes 393224 | tf_op jit(solution)/shard_map/ppermute | solution.py:91
  73.1 8.1 %collective-permute-start.3 = (bf16[2,128,256]{2,1,0:T(8,128)(2,1)S(1)}, bf16[2,128,256]{2,1,0:T(8,128)(2,1)S(1)}, u32[]{:S(2)}, u32[]{:S(2)}) collective-permute-start(bf16[2,128,256]{2,1,0:T(8,128)(2,1)S(1)} %collective-permute-done.1), channel_id=1, source_target_pairs={{0,14},{2,0},{4,2},{6,4},{8,6},{10,8},{12,10},{14,12},{1,15},{3,1}... | collective-permute-start | bytes 393224 | tf_op jit(solution)/shard_map/ppermute | solution.py:95
  79.3 8.1 %collective-permute-start.4 = (bf16[2,128,256]{2,1,0:T(8,128)(2,1)S(1)}, bf16[2,128,256]{2,1,0:T(8,128)(2,1)S(1)}, u32[]{:S(2)}, u32[]{:S(2)}) collective-permute-start(bf16[2,128,256]{2,1,0:T(8,128)(2,1)S(1)} %collective-permute-done.2), channel_id=1, source_target_pairs={{0,2},{2,4},{4,6},{6,8},{8,10},{10,12},{12,14},{14,0},{1,3},{3,5},... | collective-permute-start | bytes 393224 | tf_op jit(solution)/shard_map/ppermute | solution.py:91
  81.2 8.1 %collective-permute-start.5 = (bf16[2,128,256]{2,1,0:T(8,128)(2,1)S(1)}, bf16[2,128,256]{2,1,0:T(8,128)(2,1)S(1)}, u32[]{:S(2)}, u32[]{:S(2)}) collective-permute-start(bf16[2,128,256]{2,1,0:T(8,128)(2,1)S(1)} %collective-permute-done.3), channel_id=1, source_target_pairs={{0,14},{2,0},{4,2},{6,4},{8,6},{10,8},{12,10},{14,12},{1,15},{3,1}... | collective-permute-start | bytes 393224 | tf_op jit(solution)/shard_map/ppermute | solution.py:95
  87.3 8.1 %collective-permute-start.6 = (bf16[2,128,256]{2,1,0:T(8,128)(2,1)S(1)}, bf16[2,128,256]{2,1,0:T(8,128)(2,1)S(1)}, u32[]{:S(2)}, u32[]{:S(2)}) collective-permute-start(bf16[2,128,256]{2,1,0:T(8,128)(2,1)S(1)} %collective-permute-done.4), channel_id=1, source_target_pairs={{0,2},{2,4},{4,6},{6,8},{8,10},{10,12},{12,14},{14,0},{1,3},{3,5},... | collective-permute-start | bytes 393224 | tf_op jit(solution)/shard_map/ppermute | solution.py:91

commit v10 on v9

--- a/solution.py
+++ b/solution.py
@@ -80,24 +80,17 @@
     return result.reshape(channels, length) / total + gains[:, None] * signal
 
 
-def gather_pairs(held):
-    size = lax.axis_size("x")
-    mine = lax.axis_index("x")
-    slots = [held]
-    places = [mine]
-    right = held
-    left = held
-    for step in range(1, size // 2 + 1):
-        right = lax.ppermute(right, "x", [(i, (i + 1) % size) for i in range(size)])
-        slots.append(right)
-        places.append((mine - step) % size)
-        if step < size - step:
-            left = lax.ppermute(left, "x", [(i, (i - 1) % size) for i in range(size)])
-            slots.append(left)
-            places.append((mine + step) % size)
-    place = jnp.stack(places)
-    order = jnp.stack([place * 2, place * 2 + 1], axis=1)
-    return jnp.stack(slots), order
+def gather_quads(held):
+    size = lax.axis_size(X)
+    half = size // 2
+    mine = lax.axis_index(X)
+    right = lax.ppermute(held, X, [(i, (i + 1) % size) for i in range(size)])
+    left = lax.ppermute(held, X, [(i, (i - 1) % size) for i in range(size)])
+    farther = lax.ppermute(right, X, [(i, (i + 1) % size) for i in range(size)])
+    origins = jnp.stack([mine, (mine - 1) % size, (mine + 1) % size, (mine - 2) % size])
+    places = (origins % half)[:, None] + half * jnp.arange(2)[None, :]
+    order = places[:, :, None] * 2 + jnp.arange(2)[None, None, :]
+    return jnp.stack([held, right, left, farther]), order
 
 
 def causal_filter(signal, taps):
@@ -125,22 +118,23 @@
     convolved = long_convolution(signal, long_filter, skip_gain).astype(jnp.bfloat16)
     gated_t = (short_q.astype(jnp.float32) * convolved.astype(jnp.float32)).astype(jnp.bfloat16)
     outgoing = gated_t.reshape(per_group, groups, rows).transpose(1, 0, 2)
-    both = jnp.broadcast_to(outgoing[None], (2,) + outgoing.shape).reshape((2 * groups,) + outgoing.shape[1:])
-    returned = lax.all_to_all(both, ("yh",) + SEQ, split_axis=0, concat_axis=0, tiled=True)
-    held = returned.reshape(2, width, rows).transpose(0, 2, 1)
-    pieces, order = gather_pairs(held)
+    copies = jnp.broadcast_to(outgoing[None], (4,) + outgoing.shape).reshape((4 * groups,) + outgoing.shape[1:])
+    returned = lax.all_to_all(copies, ("xhi", "yh") + SEQ, split_axis=0, concat_axis=0, tiled=True)
+    held = returned.reshape(2, 2, width, rows).transpose(0, 1, 3, 2)
+    pieces, order = gather_quads(held)
     weight = out_weight.reshape(-1, width, out_weight.shape[1])[order]
-    result = jnp.einsum("pqtc,pqcj->tj", pieces, weight, preferred_element_type=jnp.float32)
+    result = jnp.einsum("sahtc,sahcj->tj", pieces, weight, preferred_element_type=jnp.float32)
     return result.astype(jnp.bfloat16)
 
 
 SEQ = ("z", "ylo", "core")
-CHAN = ("x", "yh")
+X = ("xhi", "xlo")
+CHAN = X + ("yh",)
 
 
 def solution(mesh):
     shape = mesh.devices.shape
-    fine = Mesh(mesh.devices.reshape(shape[0] // 8, 4, 2, shape[1] // 2, 2), SEQ + CHAN)
+    fine = Mesh(mesh.devices.reshape(shape[0] // 8, 4, 2, 2, shape[1] // 4, 2), SEQ + CHAN)
     in_specs = (
         P(SEQ, CHAN),
         P(SEQ, CHAN),

time: 97 us -> 101 us (1.041)
  the two profiles are of different devices: /device:TPU:8 before, /device:TPU:1 now
where the time goes in v10:
time: 101 us; the launch traced here: 100 us
  starting transfers between devices  44.5 us (44%)
  waiting for transfers between devices  38.5 us (38%)
  local copies, waits for them, and re-layouts  7.84 us (8%)
  matrix products  7.01 us (7%)
  other arithmetic  2.13 us (2%)
    all_to_all x1, starting transfers between devices, body(): lax.all_to_all(raw, SEQ, split_axis=0, concat_axis=0, tiled=True)  22.1 us
    all_to_all x1, waiting for transfers between devices, body(): lax.all_to_all(copies, ('xhi', 'yh') + SEQ, split_axis=0, concat_axis=0,...  19.4 us
    all_to_all x1, starting transfers between devices, body(): lax.all_to_all(copies, ('xhi', 'yh') + SEQ, split_axis=0, concat_axis=0,...  13.7 us
    all_to_all x1, waiting for transfers between devices, body(): lax.all_to_all(raw, SEQ, split_axis=0, concat_axis=0, tiled=True)  9.52 us
    ppermute x1, waiting for transfers between devices, gather_quads(): farther = lax.ppermute(right, X, [(i, (i + 1) % size) for i in range(size)])  5.42 us
    ppermute x1, waiting for transfers between devices, gather_quads(): right = lax.ppermute(held, X, [(i, (i + 1) % size) for i in range(size)])  4.14 us
    ppermute x1, starting transfers between devices, gather_quads(): left = lax.ppermute(held, X, [(i, (i - 1) % size) for i in range(size)])  3.33 us
    ppermute x1, starting transfers between devices, gather_quads(): right = lax.ppermute(held, X, [(i, (i + 1) % size) for i in range(size)])  3.15 us
  transfers between devices with their start and end apart: 5, of which 4 were waited for; matrix products, arithmetic and copies ran while one was open for 5% of the time, Pallas kernels for 0%

profile of v10, /device:TPU:1, one launch (start us, length us, event | category | flops | bytes accessed | tf_op | source)
XLA Modules:
  0.0 100.4 jit_solution(5272566188836151671)
XLA Ops:
  0.0 0.0 copy-start
  0.0 0.0 copy-start.1
  0.0 1.1 %copy.42 = bf16[128,256]{0,1:T(8,128)(2,1)S(1)} copy(bf16[128,256]{1,0:T(8,128)(2,1)} %param.7) | data formatting | bytes 131072 | tf_op args[0]
  1.1 1.0 copy.43
  2.1 1.0 copy.44
  3.0 0.2 maximum_bitcast_fusion
  3.2 0.7 copy.45
  4.0 22.1 %all-to-all-start = ((bf16[64,3,4,128]{3,2,1,0:T(4,128)(2,1)}), bf16[64,3,4,128]{3,2,1,0:T(4,128)(2,1)S(1)}, u32[]{:S(2)}, u32[]{:S(2)}) async-start(bf16[64,3,4,128]{3,2,1,0:T(4,128)(2,1)} %copy.45), calls=%async_computation | async-start | bytes 393216 | tf_op jit(solution)/shard_map/all_to_all | solution.py:113
  26.1 0.3 broadcast_multiply_fusion
  26.3 0.3 fusion.61
  26.7 0.9 fusion.64
  27.6 0.3 fusion.59
  27.9 0.0 copy-done.1
  27.9 0.6 convolution_bitcast_fusion
  28.5 9.5 %all-to-all-done = bf16[64,3,4,128]{3,2,1,0:T(4,128)(2,1)S(1)} async-done(((bf16[64,3,4,128]{3,2,1,0:T(4,128)(2,1)}), bf16[64,3,4,128]{3,2,1,0:T(4,128)(2,1)S(1)}, u32[]{:S(2)}, u32[]{:S(2)}) %all-to-all-start) | async-done | bytes 196640 | tf_op jit(solution)/shard_map/all_to_all | solution.py:113
  38.1 0.1 slice_bitcast_fusion.2
  38.2 0.3 multiply_convert_fusion.1
  38.5 0.4 convolution_bitcast_fusion.1
  38.9 0.1 multiply_add_fusion.3
  39.1 1.0 fusion.16
  40.1 1.0 fusion.20
  41.1 0.0 copy-start.2
  41.1 0.1 multiply_subtract_fusion.1
  41.2 0.6 fusion.24
  41.8 0.1 multiply_subtract_fusion
  41.9 0.6 fusion.2
  42.5 0.0 copy-done.2
  42.6 0.2 fusion.49
  42.8 0.1 copy.55
  42.9 0.8 broadcast_in_dim.2
  43.7 13.7 %all-to-all-start.1 = ((bf16[256,4,128]{2,1,0:T(4,128)(2,1)}), bf16[256,4,128]{2,1,0:T(4,128)(2,1)S(1)}, u32[]{:S(2)}, u32[]{:S(2)}) async-start(bf16[256,4,128]{2,1,0:T(4,128)(2,1)} %bitcast.30), calls=%async_computation.1 | async-start | bytes 524288 | tf_op jit(solution)/shard_map/all_to_all | solution.py:122
  57.4 19.4 %all-to-all-done.1 = bf16[256,4,128]{2,1,0:T(4,128)(2,1)S(1)} async-done(((bf16[256,4,128]{2,1,0:T(4,128)(2,1)}), bf16[256,4,128]{2,1,0:T(4,128)(2,1)S(1)}, u32[]{:S(2)}, u32[]{:S(2)}) %all-to-all-start.1) | async-done | bytes 262176 | tf_op jit(solution)/shard_map/all_to_all | solution.py:122
  76.9 0.1 copy.56
  77.0 3.2 %collective-permute-start = (bf16[2,2,128,256]{3,2,1,0:T(8,128)(2,1)S(1)}, bf16[2,2,128,256]{3,2,1,0:T(8,128)(2,1)S(1)}, u32[]{:S(2)}, u32[]{:S(2)}) collective-permute-start(bf16[2,2,128,256]{3,2,1,0:T(8,128)(2,1)S(1)} %bitcast.134), channel_id=1, source_target_pairs={{0,2},{2,4},{4,6},{6,8},{8,10},{10,12},{12,14},{14,0},{1,3},{3,5},... | collective-permute-start | bytes 786440 | tf_op jit(solution)/shard_map/ppermute | solution.py:87
  80.2 0.1 and_select_fusion
  80.2 0.1 add_multiply_fusion
  80.3 3.3 %collective-permute-start.1 = (bf16[2,2,128,256]{3,2,1,0:T(8,128)(2,1)S(1)}, bf16[2,2,128,256]{3,2,1,0:T(8,128)(2,1)S(1)}, u32[]{:S(2)}, u32[]{:S(2)}) collective-permute-start(bf16[2,2,128,256]{3,2,1,0:T(8,128)(2,1)S(1)} %bitcast.135), channel_id=1, source_target_pairs={{0,14},{2,0},{4,2},{6,4},{8,6},{10,8},{12,10},{14,12},{1,15},{3,1}... | collective-permute-start | bytes 786440 | tf_op jit(solution)/shard_map/ppermute | solution.py:88
  83.7 4.1 %collective-permute-done = bf16[2,2,128,256]{3,2,1,0:T(8,128)(2,1)S(1)} collective-permute-done((bf16[2,2,128,256]{3,2,1,0:T(8,128)(2,1)S(1)}, bf16[2,2,128,256]{3,2,1,0:T(8,128)(2,1)S(1)}, u32[]{:S(2)}, u32[]{:S(2)}) %collective-permute-start) | collective-permute-done | bytes 262176 | tf_op jit(solution)/shard_map/ppermute | solution.py:87
  87.8 2.3 %collective-permute-start.2 = (bf16[2,2,128,256]{3,2,1,0:T(8,128)(2,1)S(1)}, bf16[2,2,128,256]{3,2,1,0:T(8,128)(2,1)S(1)}, u32[]{:S(2)}, u32[]{:S(2)}) collective-permute-start(bf16[2,2,128,256]{3,2,1,0:T(8,128)(2,1)S(1)} %collective-permute-done), channel_id=1, source_target_pairs={{0,2},{2,4},{4,6},{6,8},{8,10},{10,12},{12,14},{14,0},{1,3},{3,5},... | collective-permute-start | bytes 786440 | tf_op jit(solution)/shard_map/ppermute | solution.py:89
  90.1 0.1 compare_select_fusion
  90.1 0.1 reshape.249
  90.2 0.0 copy-done
  90.2 2.0 %gather_fusion = bf16[16,256,256]{2,1,0:T(8,128)(2,1)} fusion(bf16[16,256,256]{2,1,0:T(8,128)(2,1)S(1)} %bitcast.123, s32[1024]{0:T(1024)S(1)} %pad_clamp_fusion), kind=kCustom, calls=%fused_computation | custom fusion | bytes 4194368 | tf_op jit(solution)/shard_map/gather | solution.py:125
  92.3 0.0 collective-permute-done.1
  92.3 5.4 %collective-permute-done.2 = bf16[2,2,128,256]{3,2,1,0:T(8,128)(2,1)S(1)} collective-permute-done((bf16[2,2,128,256]{3,2,1,0:T(8,128)(2,1)S(1)}, bf16[2,2,128,256]{3,2,1,0:T(8,128)(2,1)S(1)}, u32[]{:S(2)}, u32[]{:S(2)}) %collective-permute-start.2) | collective-permute-done | bytes 262176 | tf_op jit(solution)/shard_map/ppermute | solution.py:89
  97.7 2.7 %fusion.6 = bf16[128,256]{1,0:T(8,128)(2,1)} fusion(bf16[4,2,2,256,256]{4,3,2,1,0:T(8,128)(2,1)} %bitcast.124, bf16[1,2,2,128,256]{4,3,0,2,1:T(8,128)(2,1)S(1)} %bitcast.144, bf16[1,2,2,128,256]{4,3,0,2,1:T(8,128)(2,1)S(1)} %bitcast.143, bf16[1,2,2,128,256]{4,3,0,2,1:T(8,128)(2,1)S(1)} %bitcast.142, bf16[1,2,2,128,256]{4,3,0,2,1:T(8,128)(2,1)S(1)} %bitcast.136), kind=kOutput, calls=%fused_computation.8 | convolution fusion | flops 270041088 | bytes 3211264 | tf_op jit(solution)/shard_map/sahtc,sahcj->tj/dot_general | solution.py:126
  (7 shorter events, 0.1 us)
Async XLA Ops:
  0.0 90.2 %copy-start = (bf16[4096,256]{1,0:T(8,128)(2,1)S(1)}, bf16[4096,256]{1,0:T(8,128)(2,1)}, u32[]{:S(2)}) copy-start(bf16[4096,256]{1,0:T(8,128)(2,1)} %param.13) | copy-start | bytes 6291460
  0.0 27.9 %copy-start.1 = (f32[4,8192]{1,0:T(4,128)S(1)}, f32[4,8192]{1,0:T(4,128)}, u32[]{:S(2)}) copy-start(f32[4,8192]{1,0:T(4,128)} %param.11) | copy-start | bytes 393220
  4.0 34.1 %all-to-all-start = ((bf16[64,3,4,128]{3,2,1,0:T(4,128)(2,1)}), bf16[64,3,4,128]{3,2,1,0:T(4,128)(2,1)S(1)}, u32[]{:S(2)}, u32[]{:S(2)}) async-start(bf16[64,3,4,128]{3,2,1,0:T(4,128)(2,1)} %copy.45), calls=%async_computation | async-start | bytes 393216 | tf_op jit(solution)/shard_map/all_to_all | solution.py:113
  41.1 1.5 %copy-start.2 = (f32[4]{0:T(128)S(1)}, f32[4]{0:T(128)}, u32[]{:S(2)}) copy-start(f32[4]{0:T(128)} %param.12) | copy-start | bytes 52
  43.7 33.2 %all-to-all-start.1 = ((bf16[256,4,128]{2,1,0:T(4,128)(2,1)}), bf16[256,4,128]{2,1,0:T(4,128)(2,1)S(1)}, u32[]{:S(2)}, u32[]{:S(2)}) async-start(bf16[256,4,128]{2,1,0:T(4,128)(2,1)} %bitcast.30), calls=%async_computation.1 | async-start | bytes 524288 | tf_op jit(solution)/shard_map/all_to_all | solution.py:122
  77.0 10.8 %collective-permute-start = (bf16[2,2,128,256]{3,2,1,0:T(8,128)(2,1)S(1)}, bf16[2,2,128,256]{3,2,1,0:T(8,128)(2,1)S(1)}, u32[]{:S(2)}, u32[]{:S(2)}) collective-permute-start(bf16[2,2,128,256]{3,2,1,0:T(8,128)(2,1)S(1)} %bitcast.134), channel_id=1, source_target_pairs={{0,2},{2,4},{4,6},{6,8},{8,10},{10,12},{12,14},{14,0},{1,3},{3,5},... | collective-permute-start | bytes 786440 | tf_op jit(solution)/shard_map/ppermute | solution.py:87
  80.3 11.9 %collective-permute-start.1 = (bf16[2,2,128,256]{3,2,1,0:T(8,128)(2,1)S(1)}, bf16[2,2,128,256]{3,2,1,0:T(8,128)(2,1)S(1)}, u32[]{:S(2)}, u32[]{:S(2)}) collective-permute-start(bf16[2,2,128,256]{3,2,1,0:T(8,128)(2,1)S(1)} %bitcast.135), channel_id=1, source_target_pairs={{0,14},{2,0},{4,2},{6,4},{8,6},{10,8},{12,10},{14,12},{1,15},{3,1}... | collective-permute-start | bytes 786440 | tf_op jit(solution)/shard_map/ppermute | solution.py:88
  87.8 9.9 %collective-permute-start.2 = (bf16[2,2,128,256]{3,2,1,0:T(8,128)(2,1)S(1)}, bf16[2,2,128,256]{3,2,1,0:T(8,128)(2,1)S(1)}, u32[]{:S(2)}, u32[]{:S(2)}) collective-permute-start(bf16[2,2,128,256]{3,2,1,0:T(8,128)(2,1)S(1)} %collective-permute-done), channel_id=1, source_target_pairs={{0,2},{2,4},{4,6},{6,8},{8,10},{10,12},{12,14},{14,0},{1,3},{3,5},... | collective-permute-start | bytes 786440 | tf_op jit(solution)/shard_map/ppermute | solution.py:89

commit v11 on v9

--- a/solution.py
+++ b/solution.py
@@ -83,21 +83,20 @@
 def gather_pairs(held):
     size = lax.axis_size("x")
     mine = lax.axis_index("x")
-    slots = [held]
-    places = [mine]
-    right = held
-    left = held
-    for step in range(1, size // 2 + 1):
-        right = lax.ppermute(right, "x", [(i, (i + 1) % size) for i in range(size)])
-        slots.append(right)
-        places.append((mine - step) % size)
-        if step < size - step:
-            left = lax.ppermute(left, "x", [(i, (i - 1) % size) for i in range(size)])
-            slots.append(left)
-            places.append((mine + step) % size)
-    place = jnp.stack(places)
+
+    def moved(block, step):
+        return lax.ppermute(block, "x", [(i, (i + step) % size) for i in range(size)])
+
+    right = moved(held, 1)
+    left = moved(held, -1)
+    across = moved(held, size // 2)
+    right_two = moved(jnp.stack([right, held]), 2)
+    left_two = moved(jnp.stack([left, held]), -2)
+    pieces = jnp.concatenate([jnp.stack([held, right, left, across]), right_two, left_two])
+    offsets = jnp.array([0, -1, 1, -(size // 2), -3, -2, 3, 2], jnp.int32)
+    place = (mine + offsets) % size
     order = jnp.stack([place * 2, place * 2 + 1], axis=1)
-    return jnp.stack(slots), order
+    return pieces, order
 
 
 def causal_filter(signal, taps):

time: 97 us -> 98 us (1.010)
  the two profiles are of different devices: /device:TPU:8 before, /device:TPU:3 now
where the time goes in v11:
time: 98 us; the launch traced here: 97.5 us
  starting transfers between devices  46.4 us (47%)
  waiting for transfers between devices  35.4 us (36%)
  local copies, waits for them, and re-layouts  7.9 us (8%)
  matrix products  5.41 us (6%)
  other arithmetic  1.95 us (2%)
    all_to_all x1, starting transfers between devices, body(): lax.all_to_all(raw, SEQ, split_axis=0, concat_axis=0, tiled=True)  21.3 us
    ppermute x5, starting transfers between devices, moved(): lax.ppermute(block, 'x', [(i, (i + step) % size) for i in range(size)])  17.8 us
    ppermute x5, waiting for transfers between devices, moved(): lax.ppermute(block, 'x', [(i, (i + step) % size) for i in range(size)])  15.6 us
    all_to_all x1, waiting for transfers between devices, body(): lax.all_to_all(both, ('yh',) + SEQ, split_axis=0, concat_axis=0, tiled=True)  10.4 us
    all_to_all x1, waiting for transfers between devices, body(): lax.all_to_all(raw, SEQ, split_axis=0, concat_axis=0, tiled=True)  9.51 us
    all_to_all x1, starting transfers between devices, body(): lax.all_to_all(both, ('yh',) + SEQ, split_axis=0, concat_axis=0, tiled=True)  7.26 us
    unnamed x19, local copies, waits for them, and re-layouts  3.11 us
    gather x1, local copies, waits for them, and re-layouts, body(): weight = out_weight.reshape(-1, width, out_weight.shape[1])[order]  2.01 us
  transfers between devices with their start and end apart: 7, of which 3 were waited for; matrix products, arithmetic and copies ran while one was open for 5% of the time, Pallas kernels for 0%

profile of v11, /device:TPU:3, one launch (start us, length us, event | category | flops | bytes accessed | tf_op | source)
XLA Modules:
  0.0 97.5 jit_solution(12792036939552469297)
XLA Ops:
  0.0 0.0 copy-start
  0.0 1.1 %copy.38 = bf16[128,256]{0,1:T(8,128)(2,1)S(1)} copy(bf16[128,256]{1,0:T(8,128)(2,1)} %param.8) | data formatting | bytes 131072 | tf_op args[0]
  1.1 1.0 copy.39
  2.1 1.0 copy.40
  3.0 0.2 maximum_bitcast_fusion
  3.2 0.7 copy.41
  3.9 21.3 %all-to-all-start = ((bf16[64,3,4,128]{3,2,1,0:T(4,128)(2,1)}), bf16[64,3,4,128]{3,2,1,0:T(4,128)(2,1)S(1)}, u32[]{:S(2)}, u32[]{:S(2)}) async-start(bf16[64,3,4,128]{3,2,1,0:T(4,128)(2,1)} %copy.41), calls=%async_computation | async-start | bytes 393216 | tf_op jit(solution)/shard_map/all_to_all | solution.py:119
  25.3 0.3 broadcast_multiply_fusion
  25.5 0.3 fusion.47
  25.8 0.9 fusion.52
  26.8 0.3 fusion.45
  27.0 0.0 copy-done.2
  27.1 0.6 convolution_bitcast_fusion
  27.7 9.5 %all-to-all-done = bf16[64,3,4,128]{3,2,1,0:T(4,128)(2,1)S(1)} async-done(((bf16[64,3,4,128]{3,2,1,0:T(4,128)(2,1)}), bf16[64,3,4,128]{3,2,1,0:T(4,128)(2,1)S(1)}, u32[]{:S(2)}, u32[]{:S(2)}) %all-to-all-start) | async-done | bytes 196640 | tf_op jit(solution)/shard_map/all_to_all | solution.py:119
  37.2 0.1 slice_bitcast_fusion.2
  37.3 0.3 multiply_convert_fusion.1
  37.7 0.4 convolution_bitcast_fusion.1
  38.1 0.1 multiply_add_fusion.3
  38.2 1.0 %fusion.2 = f32[4,128,256]{2,1,0:T(8,128)S(1)} fusion(f32[4,128,128]{1,2,0:T(8,128)S(1)} %get-tuple-element.12, f32[4,128,128]{1,2,0:T(8,128)S(1)} %get-tuple-element.11, f32[128,128]{0,1:T(8,128)S(1)} %get-tuple-element.34, f32[128,128]{0,1:T(8,128)S(1)} %get-tuple-element.33, f32[128,128]{0,1:T(8,128)S(1)} %broadcast_multiply_fusion), kind=kOutput, calls=%fused_computation.7 | convolution fusion | flops 402980864 | bytes 1245184 | tf_op jit(solution)/shard_map/ckm,mj->ckj/dot_general | solution.py:53
  39.3 1.0 %fusion.6 = f32[4,128,256]{2,1,0:T(8,128)S(1)} fusion(f32[4,128,128]{1,2,0:T(8,128)S(1)} %get-tuple-element.20, f32[4,128,128]{1,2,0:T(8,128)S(1)} %get-tuple-element.21, f32[128,128]{0,1:T(8,128)S(1)} %get-tuple-element.34, f32[128,128]{0,1:T(8,128)S(1)} %get-tuple-element.33, f32[128,128]{0,1:T(8,128)S(1)} %broadcast_multiply_fusion), kind=kOutput, calls=%fused_computation.11 | convolution fusion | flops 402980864 | bytes 1245184 | tf_op jit(solution)/shard_map/ckm,mj->ckj/dot_general | solution.py:53
  40.3 0.0 copy-start.3
  40.3 0.1 multiply_subtract_fusion.1
  40.3 0.0 copy-start.4
  40.3 0.6 fusion.10
  41.0 0.1 multiply_subtract_fusion
  41.1 0.6 fusion
  41.7 0.0 copy-done.3
  41.7 0.2 fusion.35
  42.0 0.1 copy.51
  42.1 0.7 broadcast_in_dim.2
  42.8 7.3 %all-to-all-start.1 = ((bf16[128,4,128]{2,1,0:T(4,128)(2,1)}), bf16[128,4,128]{2,1,0:T(4,128)(2,1)S(1)}, u32[]{:S(2)}, u32[]{:S(2)}) async-start(bf16[128,4,128]{2,1,0:T(4,128)(2,1)} %bitcast.30), calls=%async_computation.1 | async-start | bytes 262144 | tf_op jit(solution)/shard_map/all_to_all | solution.py:128
  50.1 0.1 copy.53
  50.2 0.1 reshape.194
  50.3 2.0 %gather_fusion = bf16[16,256,256]{2,1,0:T(8,128)(2,1)} fusion(bf16[16,256,256]{2,1,0:T(8,128)(2,1)S(1)} %bitcast.122, s32[1024]{0:T(1024)S(1)} %pad_clamp_fusion), kind=kCustom, calls=%fused_computation | custom fusion | bytes 4194368 | tf_op jit(solution)/shard_map/gather | solution.py:131
  52.3 10.4 %all-to-all-done.1 = bf16[128,4,128]{2,1,0:T(4,128)(2,1)S(1)} async-done(((bf16[128,4,128]{2,1,0:T(4,128)(2,1)}), bf16[128,4,128]{2,1,0:T(4,128)(2,1)S(1)}, u32[]{:S(2)}, u32[]{:S(2)}) %all-to-all-start.1) | async-done | bytes 131104 | tf_op jit(solution)/shard_map/all_to_all | solution.py:128
  62.6 0.1 copy.52
  62.8 0.0 copy-start.1
  62.8 2.3 %collective-permute-start.1 = (bf16[2,128,256]{2,1,0:T(8,128)(2,1)S(1)}, bf16[2,128,256]{2,1,0:T(8,128)(2,1)S(1)}, u32[]{:S(2)}, u32[]{:S(2)}) collective-permute-start(bf16[2,128,256]{2,1,0:T(8,128)(2,1)S(1)} %bitcast.127), channel_id=1, source_target_pairs={{0,14},{2,0},{4,2},{6,4},{8,6},{10,8},{12,10},{14,12},{1,15},{3,1}... | collective-permute-start | bytes 393224 | tf_op jit(solution)/shard_map/ppermute | solution.py:88
  65.1 3.1 %collective-permute-start = (bf16[2,128,256]{2,1,0:T(8,128)(2,1)S(1)}, bf16[2,128,256]{2,1,0:T(8,128)(2,1)S(1)}, u32[]{:S(2)}, u32[]{:S(2)}) collective-permute-start(bf16[2,128,256]{2,1,0:T(8,128)(2,1)S(1)} %bitcast.128), channel_id=1, source_target_pairs={{0,2},{2,4},{4,6},{6,8},{8,10},{10,12},{12,14},{14,0},{1,3},{3,5},... | collective-permute-start | bytes 393224 | tf_op jit(solution)/shard_map/ppermute | solution.py:88
  68.2 6.2 %collective-permute-start.2 = (bf16[2,128,256]{2,1,0:T(8,128)(2,1)S(1)}, bf16[2,128,256]{2,1,0:T(8,128)(2,1)S(1)}, u32[]{:S(2)}, u32[]{:S(2)}) collective-permute-start(bf16[2,128,256]{2,1,0:T(8,128)(2,1)S(1)} %bitcast.129), channel_id=1, source_target_pairs={{0,8},{2,10},{4,12},{6,14},{8,0},{10,2},{12,4},{14,6},{1,9},{3,11}... | collective-permute-start | bytes 393224 | tf_op jit(solution)/shard_map/ppermute | solution.py:88
  74.4 0.0 collective-permute-done.1
  74.4 0.0 collective-permute-done
  74.5 4.2 %collective-permute-start.4 = (bf16[2,2,128,256]{3,2,1,0:T(8,128)(2,1)S(1)}, bf16[2,2,128,256]{3,2,1,0:T(8,128)(2,1)S(1)}, u32[]{:S(2)}, u32[]{:S(2)}) collective-permute-start(bf16[2,2,128,256]{3,2,1,0:T(8,128)(2,1)S(1)} %get-tuple-element.18), channel_id=1, source_target_pairs={{0,12},{2,14},{4,0},{6,2},{8,4},{10,6},{12,8},{14,10},{1,13},{3,15... | collective-permute-start | bytes 786440 | tf_op jit(solution)/shard_map/ppermute | solution.py:88
  78.8 1.9 %collective-permute-start.3 = (bf16[2,2,128,256]{3,2,1,0:T(8,128)(2,1)S(1)}, bf16[2,2,128,256]{3,2,1,0:T(8,128)(2,1)S(1)}, u32[]{:S(2)}, u32[]{:S(2)}) collective-permute-start(bf16[2,2,128,256]{3,2,1,0:T(8,128)(2,1)S(1)} %get-tuple-element.19), channel_id=1, source_target_pairs={{0,4},{2,6},{4,8},{6,10},{8,12},{10,14},{12,0},{14,2},{1,5},{3,7},... | collective-permute-start | bytes 786440 | tf_op jit(solution)/shard_map/ppermute | solution.py:88
  80.7 0.0 collective-permute-done.2
  80.8 15.6 %collective-permute-done.3 = bf16[2,2,128,256]{3,2,1,0:T(8,128)(2,1)S(1)} collective-permute-done((bf16[2,2,128,256]{3,2,1,0:T(8,128)(2,1)S(1)}, bf16[2,2,128,256]{3,2,1,0:T(8,128)(2,1)S(1)}, u32[]{:S(2)}, u32[]{:S(2)}) %collective-permute-start.3) | collective-permute-done | bytes 262176 | tf_op jit(solution)/shard_map/ppermute | solution.py:88
  96.3 0.0 collective-permute-done.4
  96.4 1.1 %fusion.1 = bf16[128,256]{1,0:T(8,128)(2,1)} fusion(bf16[8,2,128,256]{3,2,1,0:T(8,128)(2,1)S(1)} %constant_dynamic-update-slice_fusion, bf16[8,2,256,256]{3,2,1,0:T(8,128)(2,1)S(1)} %bitcast.123), kind=kOutput, calls=%fused_computation.6 | convolution fusion | flops 268468224 | bytes 3211264 | tf_op jit(solution)/shard_map/pqtc,pqcj->tj/dot_general | solution.py:132
  (19 shorter events, 0.2 us)
Async XLA Ops:
  0.0 50.2 %copy-start = (bf16[4096,256]{1,0:T(8,128)(2,1)S(1)}, bf16[4096,256]{1,0:T(8,128)(2,1)}, u32[]{:S(2)}) copy-start(bf16[4096,256]{1,0:T(8,128)(2,1)} %param.14) | copy-start | bytes 6291460
  0.0 27.0 %copy-start.2 = (f32[4,8192]{1,0:T(4,128)S(1)}, f32[4,8192]{1,0:T(4,128)}, u32[]{:S(2)}) copy-start(f32[4,8192]{1,0:T(4,128)} %param.12) | copy-start | bytes 393220
  3.9 33.3 %all-to-all-start = ((bf16[64,3,4,128]{3,2,1,0:T(4,128)(2,1)}), bf16[64,3,4,128]{3,2,1,0:T(4,128)(2,1)S(1)}, u32[]{:S(2)}, u32[]{:S(2)}) async-start(bf16[64,3,4,128]{3,2,1,0:T(4,128)(2,1)} %copy.41), calls=%async_computation | async-start | bytes 393216 | tf_op jit(solution)/shard_map/all_to_all | solution.py:119
  40.3 1.5 %copy-start.3 = (f32[4]{0:T(128)S(1)}, f32[4]{0:T(128)}, u32[]{:S(2)}) copy-start(f32[4]{0:T(128)} %param.13) | copy-start | bytes 52
  40.3 9.7 %copy-start.4 = (s32[8]{0:T(128)S(1)}, s32[8]{0:T(128)}, u32[]{:S(2)}) copy-start(s32[8]{0:T(128)} %constant.89.clone) | copy-start | bytes 100
  42.8 19.9 %all-to-all-start.1 = ((bf16[128,4,128]{2,1,0:T(4,128)(2,1)}), bf16[128,4,128]{2,1,0:T(4,128)(2,1)S(1)}, u32[]{:S(2)}, u32[]{:S(2)}) async-start(bf16[128,4,128]{2,1,0:T(4,128)(2,1)} %bitcast.30), calls=%async_computation.1 | async-start | bytes 262144 | tf_op jit(solution)/shard_map/all_to_all | solution.py:128
  62.8 33.6 %copy-start.1 = (bf16[16,256,256]{2,1,0:T(8,128)(2,1)S(1)}, bf16[16,256,256]{2,1,0:T(8,128)(2,1)}, u32[]{:S(2)}) copy-start(bf16[16,256,256]{2,1,0:T(8,128)(2,1)} %gather_fusion) | copy-start | bytes 6291460
  62.8 11.7 %collective-permute-start.1 = (bf16[2,128,256]{2,1,0:T(8,128)(2,1)S(1)}, bf16[2,128,256]{2,1,0:T(8,128)(2,1)S(1)}, u32[]{:S(2)}, u32[]{:S(2)}) collective-permute-start(bf16[2,128,256]{2,1,0:T(8,128)(2,1)S(1)} %bitcast.127), channel_id=1, source_target_pairs={{0,14},{2,0},{4,2},{6,4},{8,6},{10,8},{12,10},{14,12},{1,15},{3,1}... | collective-permute-start | bytes 393224 | tf_op jit(solution)/shard_map/ppermute | solution.py:88
  65.1 9.4 %collective-permute-start = (bf16[2,128,256]{2,1,0:T(8,128)(2,1)S(1)}, bf16[2,128,256]{2,1,0:T(8,128)(2,1)S(1)}, u32[]{:S(2)}, u32[]{:S(2)}) collective-permute-start(bf16[2,128,256]{2,1,0:T(8,128)(2,1)S(1)} %bitcast.128), channel_id=1, source_target_pairs={{0,2},{2,4},{4,6},{6,8},{8,10},{10,12},{12,14},{14,0},{1,3},{3,5},... | collective-permute-start | bytes 393224 | tf_op jit(solution)/shard_map/ppermute | solution.py:88
  68.2 12.6 %collective-permute-start.2 = (bf16[2,128,256]{2,1,0:T(8,128)(2,1)S(1)}, bf16[2,128,256]{2,1,0:T(8,128)(2,1)S(1)}, u32[]{:S(2)}, u32[]{:S(2)}) collective-permute-start(bf16[2,128,256]{2,1,0:T(8,128)(2,1)S(1)} %bitcast.129), channel_id=1, source_target_pairs={{0,8},{2,10},{4,12},{6,14},{8,0},{10,2},{12,4},{14,6},{1,9},{3,11}... | collective-permute-start | bytes 393224 | tf_op jit(solution)/shard_map/ppermute | solution.py:88
  74.5 21.8 %collective-permute-start.4 = (bf16[2,2,128,256]{3,2,1,0:T(8,128)(2,1)S(1)}, bf16[2,2,128,256]{3,2,1,0:T(8,128)(2,1)S(1)}, u32[]{:S(2)}, u32[]{:S(2)}) collective-permute-start(bf16[2,2,128,256]{3,2,1,0:T(8,128)(2,1)S(1)} %get-tuple-element.18), channel_id=1, source_target_pairs={{0,12},{2,14},{4,0},{6,2},{8,4},{10,6},{12,8},{14,10},{1,13},{3,15... | collective-permute-start | bytes 786440 | tf_op jit(solution)/shard_map/ppermute | solution.py:88
  78.8 17.6 %collective-permute-start.3 = (bf16[2,2,128,256]{3,2,1,0:T(8,128)(2,1)S(1)}, bf16[2,2,128,256]{3,2,1,0:T(8,128)(2,1)S(1)}, u32[]{:S(2)}, u32[]{:S(2)}) collective-permute-start(bf16[2,2,128,256]{3,2,1,0:T(8,128)(2,1)S(1)} %get-tuple-element.19), channel_id=1, source_target_pairs={{0,4},{2,6},{4,8},{6,10},{8,12},{10,14},{12,0},{14,2},{1,5},{3,7},... | collective-permute-start | bytes 786440 | tf_op jit(solution)/shard_map/ppermute | solution.py:88

commit v12 on v9

--- a/solution.py
+++ b/solution.py
@@ -5,7 +5,7 @@
 from jax import lax
 from jax.sharding import Mesh, PartitionSpec as P
 
-HIGHEST_MODE = lax.Precision.HIGHEST
+DFT_PRECISION = lax.Precision.HIGH
 
 
 def tables(count):
@@ -45,12 +45,12 @@
     used = signal.shape[1] // inner
     blocks = signal.reshape(signal.shape[0], used, inner)
     stacked = jnp.concatenate([cos_out[:, :used], -sin_out[:, :used]], 0)
-    first = jnp.einsum("kn,cnm->ckm", stacked, blocks, precision=HIGHEST_MODE)
+    first = jnp.einsum("kn,cnm->ckm", stacked, blocks, precision=DFT_PRECISION)
     first_re, first_im = first[:, :outer], first[:, outer:]
     turned_re = first_re * turn_cos + first_im * turn_sin
     turned_im = first_im * turn_cos - first_re * turn_sin
     turned = jnp.concatenate([turned_re, turned_im], 2)
-    second = jnp.einsum("ckm,mj->ckj", turned, rotation(cos_in, sin_in, -1.0), precision=HIGHEST_MODE)
+    second = jnp.einsum("ckm,mj->ckj", turned, rotation(cos_in, sin_in, -1.0), precision=DFT_PRECISION)
     return (second[..., :inner], second[..., inner:])
 
 
@@ -68,7 +68,7 @@
     prod_im = sig_re * fil_im + sig_im * fil_re
     cos_in, sin_in = inner_tables
     product = jnp.concatenate([prod_re, prod_im], 2)
-    back = jnp.einsum("ckj,jm->ckm", product, rotation(cos_in, sin_in, 1.0), precision=HIGHEST_MODE)
+    back = jnp.einsum("ckj,jm->ckm", product, rotation(cos_in, sin_in, 1.0), precision=DFT_PRECISION)
     back_re, back_im = back[..., :inner], back[..., inner:]
     turn_cos, turn_sin = turn_tables
     rot_re = back_re * turn_cos - back_im * turn_sin
@@ -76,7 +76,7 @@
     cos_out, sin_out = outer_tables
     half = outer // 2
     stacked = jnp.concatenate([cos_out[:half], -sin_out[:half]], 1)
-    result = jnp.einsum("nk,ckm->cnm", stacked, jnp.concatenate([rot_re, rot_im], 1), precision=HIGHEST_MODE)
+    result = jnp.einsum("nk,ckm->cnm", stacked, jnp.concatenate([rot_re, rot_im], 1), precision=DFT_PRECISION)
     return result.reshape(channels, length) / total + gains[:, None] * signal
 
 

time: 97 us -> 95.7 us (0.987)
  matrix products: 5.41 us -> 3.85 us
where the time goes in v12:
time: 95.7 us; the launch traced here: 95.2 us
  starting transfers between devices  52 us (54%)
  waiting for transfers between devices  28.9 us (30%)
  local copies, waits for them, and re-layouts  8.01 us (8%)
  matrix products  3.85 us (4%)
  other arithmetic  1.9 us (2%)
    all_to_all x1, starting transfers between devices, body(): lax.all_to_all(raw, SEQ, split_axis=0, concat_axis=0, tiled=True)  21.1 us
    ppermute x3, starting transfers between devices, gather_pairs(): left = lax.ppermute(left, 'x', [(i, (i - 1) % size) for i in range(size)])  14.8 us
    all_to_all x1, waiting for transfers between devices, body(): lax.all_to_all(both, ('yh',) + SEQ, split_axis=0, concat_axis=0, tiled=True)  9.89 us
    ppermute x4, waiting for transfers between devices, gather_pairs(): right = lax.ppermute(right, 'x', [(i, (i + 1) % size) for i in range(size)])  9.54 us
    all_to_all x1, waiting for transfers between devices, body(): lax.all_to_all(raw, SEQ, split_axis=0, concat_axis=0, tiled=True)  9.46 us
    ppermute x4, starting transfers between devices, gather_pairs(): right = lax.ppermute(right, 'x', [(i, (i + 1) % size) for i in range(size)])  8.35 us
    all_to_all x1, starting transfers between devices, body(): lax.all_to_all(both, ('yh',) + SEQ, split_axis=0, concat_axis=0, tiled=True)  7.77 us
    unnamed x19, local copies, waits for them, and re-layouts  3.12 us
  transfers between devices with their start and end apart: 9, of which 6 were waited for; matrix products, arithmetic and copies ran while one was open for 5% of the time, Pallas kernels for 0%

profile of v12, /device:TPU:8, one launch (start us, length us, event | category | flops | bytes accessed | tf_op | source)
XLA Modules:
  0.0 95.2 jit_solution(4338291030424558453)
XLA Ops:
  0.0 1.1 %copy.37 = bf16[128,256]{0,1:T(8,128)(2,1)S(1)} copy(bf16[128,256]{1,0:T(8,128)(2,1)} %param.7) | data formatting | bytes 131072 | tf_op args[0]
  1.1 1.0 %copy.38 = bf16[128,256]{0,1:T(8,128)(2,1)S(1)} copy(bf16[128,256]{1,0:T(8,128)(2,1)} %param.8) | data formatting | bytes 131072 | tf_op args[1]
  2.1 1.0 %copy.39 = bf16[128,256]{0,1:T(8,128)(2,1)S(1)} copy(bf16[128,256]{1,0:T(8,128)(2,1)} %param.9) | data formatting | bytes 131072 | tf_op args[2]
  3.0 0.2 maximum_bitcast_fusion
  3.2 0.7 copy.40
  3.9 21.1 %all-to-all-start = ((bf16[64,3,4,128]{3,2,1,0:T(4,128)(2,1)}), bf16[64,3,4,128]{3,2,1,0:T(4,128)(2,1)S(1)}, u32[]{:S(2)}, u32[]{:S(2)}) async-start(bf16[64,3,4,128]{3,2,1,0:T(4,128)(2,1)} %copy.40), calls=%async_computation | async-start | bytes 393216 | tf_op jit(solution)/shard_map/all_to_all | solution.py:120
  25.0 0.3 broadcast_multiply_fusion
  25.3 0.3 fusion.47
  25.6 0.9 fusion.50
  26.6 0.1 stack.96
  26.8 0.3 fusion.45
  27.0 0.4 convolution_bitcast_fusion
  27.5 9.5 %all-to-all-done = bf16[64,3,4,128]{3,2,1,0:T(4,128)(2,1)S(1)} async-done(((bf16[64,3,4,128]{3,2,1,0:T(4,128)(2,1)}), bf16[64,3,4,128]{3,2,1,0:T(4,128)(2,1)S(1)}, u32[]{:S(2)}, u32[]{:S(2)}) %all-to-all-start) | async-done | bytes 196640 | tf_op jit(solution)/shard_map/all_to_all | solution.py:120
  37.0 0.1 slice_bitcast_fusion.2
  37.0 0.3 multiply_convert_fusion.1
  37.4 0.3 convolution_bitcast_fusion.1
  37.7 0.1 multiply_add_fusion.3
  37.9 0.6 fusion.2
  38.5 0.6 fusion.6
  39.1 0.0 copy-start.3
  39.1 0.1 multiply_subtract_fusion.1
  39.2 0.4 fusion.10
  39.6 0.1 multiply_subtract_fusion
  39.7 0.4 fusion
  40.1 0.2 fusion.35
  40.4 0.1 copy.50
  40.4 0.7 broadcast_in_dim.2
  41.1 7.8 %all-to-all-start.1 = ((bf16[128,4,128]{2,1,0:T(4,128)(2,1)}), bf16[128,4,128]{2,1,0:T(4,128)(2,1)S(1)}, u32[]{:S(2)}, u32[]{:S(2)}) async-start(bf16[128,4,128]{2,1,0:T(4,128)(2,1)} %bitcast.30), calls=%async_computation.1 | async-start | bytes 262144 | tf_op jit(solution)/shard_map/all_to_all | solution.py:129
  48.9 0.1 copy.52
  49.0 0.1 reshape.722
  49.1 2.0 %gather_fusion = bf16[16,256,256]{2,1,0:T(8,128)(2,1)} fusion(bf16[16,256,256]{2,1,0:T(8,128)(2,1)S(1)} %bitcast.139, s32[1024]{0:T(1024)S(1)} %pad_clamp_fusion), kind=kCustom, calls=%fused_computation | custom fusion | bytes 4194368 | tf_op jit(solution)/shard_map/gather | solution.py:132
  51.1 9.9 %all-to-all-done.1 = bf16[128,4,128]{2,1,0:T(4,128)(2,1)S(1)} async-done(((bf16[128,4,128]{2,1,0:T(4,128)(2,1)}), bf16[128,4,128]{2,1,0:T(4,128)(2,1)S(1)}, u32[]{:S(2)}, u32[]{:S(2)}) %all-to-all-start.1) | async-done | bytes 131104 | tf_op jit(solution)/shard_map/all_to_all | solution.py:129
  61.0 0.1 copy.51
  61.1 2.6 %collective-permute-start = (bf16[2,128,256]{2,1,0:T(8,128)(2,1)S(1)}, bf16[2,128,256]{2,1,0:T(8,128)(2,1)S(1)}, u32[]{:S(2)}, u32[]{:S(2)}) collective-permute-start(bf16[2,128,256]{2,1,0:T(8,128)(2,1)S(1)} %bitcast.150), channel_id=1, source_target_pairs={{0,2},{2,4},{4,6},{6,8},{8,10},{10,12},{12,14},{14,0},{1,3},{3,5},... | collective-permute-start | bytes 393224 | tf_op jit(solution)/shard_map/ppermute | solution.py:91
  63.8 4.6 %collective-permute-start.1 = (bf16[2,128,256]{2,1,0:T(8,128)(2,1)S(1)}, bf16[2,128,256]{2,1,0:T(8,128)(2,1)S(1)}, u32[]{:S(2)}, u32[]{:S(2)}) collective-permute-start(bf16[2,128,256]{2,1,0:T(8,128)(2,1)S(1)} %bitcast.151), channel_id=1, source_target_pairs={{0,14},{2,0},{4,2},{6,4},{8,6},{10,8},{12,10},{14,12},{1,15},{3,1}... | collective-permute-start | bytes 393224 | tf_op jit(solution)/shard_map/ppermute | solution.py:95
  68.3 1.5 %collective-permute-done = bf16[2,128,256]{2,1,0:T(8,128)(2,1)S(1)} collective-permute-done((bf16[2,128,256]{2,1,0:T(8,128)(2,1)S(1)}, bf16[2,128,256]{2,1,0:T(8,128)(2,1)S(1)}, u32[]{:S(2)}, u32[]{:S(2)}) %collective-permute-start) | collective-permute-done | bytes 131104 | tf_op jit(solution)/shard_map/ppermute | solution.py:91
  69.9 1.9 %collective-permute-start.2 = (bf16[2,128,256]{2,1,0:T(8,128)(2,1)S(1)}, bf16[2,128,256]{2,1,0:T(8,128)(2,1)S(1)}, u32[]{:S(2)}, u32[]{:S(2)}) collective-permute-start(bf16[2,128,256]{2,1,0:T(8,128)(2,1)S(1)} %collective-permute-done), channel_id=1, source_target_pairs={{0,2},{2,4},{4,6},{6,8},{8,10},{10,12},{12,14},{14,0},{1,3},{3,5},... | collective-permute-start | bytes 393224 | tf_op jit(solution)/shard_map/ppermute | solution.py:91
  71.8 0.0 collective-permute-done.1
  71.8 5.1 %collective-permute-start.3 = (bf16[2,128,256]{2,1,0:T(8,128)(2,1)S(1)}, bf16[2,128,256]{2,1,0:T(8,128)(2,1)S(1)}, u32[]{:S(2)}, u32[]{:S(2)}) collective-permute-start(bf16[2,128,256]{2,1,0:T(8,128)(2,1)S(1)} %collective-permute-done.1), channel_id=1, source_target_pairs={{0,14},{2,0},{4,2},{6,4},{8,6},{10,8},{12,10},{14,12},{1,15},{3,1}... | collective-permute-start | bytes 393224 | tf_op jit(solution)/shard_map/ppermute | solution.py:95
  77.0 1.0 %collective-permute-done.2 = bf16[2,128,256]{2,1,0:T(8,128)(2,1)S(1)} collective-permute-done((bf16[2,128,256]{2,1,0:T(8,128)(2,1)S(1)}, bf16[2,128,256]{2,1,0:T(8,128)(2,1)S(1)}, u32[]{:S(2)}, u32[]{:S(2)}) %collective-permute-start.2) | collective-permute-done | bytes 131104 | tf_op jit(solution)/shard_map/ppermute | solution.py:91
  77.9 1.9 %collective-permute-start.4 = (bf16[2,128,256]{2,1,0:T(8,128)(2,1)S(1)}, bf16[2,128,256]{2,1,0:T(8,128)(2,1)S(1)}, u32[]{:S(2)}, u32[]{:S(2)}) collective-permute-start(bf16[2,128,256]{2,1,0:T(8,128)(2,1)S(1)} %collective-permute-done.2), channel_id=1, source_target_pairs={{0,2},{2,4},{4,6},{6,8},{8,10},{10,12},{12,14},{14,0},{1,3},{3,5},... | collective-permute-start | bytes 393224 | tf_op jit(solution)/shard_map/ppermute | solution.py:91
  79.9 0.0 collective-permute-done.3
  79.9 5.1 %collective-permute-start.5 = (bf16[2,128,256]{2,1,0:T(8,128)(2,1)S(1)}, bf16[2,128,256]{2,1,0:T(8,128)(2,1)S(1)}, u32[]{:S(2)}, u32[]{:S(2)}) collective-permute-start(bf16[2,128,256]{2,1,0:T(8,128)(2,1)S(1)} %collective-permute-done.3), channel_id=1, source_target_pairs={{0,14},{2,0},{4,2},{6,4},{8,6},{10,8},{12,10},{14,12},{1,15},{3,1}... | collective-permute-start | bytes 393224 | tf_op jit(solution)/shard_map/ppermute | solution.py:95
  85.0 1.0 %collective-permute-done.4 = bf16[2,128,256]{2,1,0:T(8,128)(2,1)S(1)} collective-permute-done((bf16[2,128,256]{2,1,0:T(8,128)(2,1)S(1)}, bf16[2,128,256]{2,1,0:T(8,128)(2,1)S(1)}, u32[]{:S(2)}, u32[]{:S(2)}) %collective-permute-start.4) | collective-permute-done | bytes 131104 | tf_op jit(solution)/shard_map/ppermute | solution.py:91
  86.0 1.9 %collective-permute-start.6 = (bf16[2,128,256]{2,1,0:T(8,128)(2,1)S(1)}, bf16[2,128,256]{2,1,0:T(8,128)(2,1)S(1)}, u32[]{:S(2)}, u32[]{:S(2)}) collective-permute-start(bf16[2,128,256]{2,1,0:T(8,128)(2,1)S(1)} %collective-permute-done.4), channel_id=1, source_target_pairs={{0,2},{2,4},{4,6},{6,8},{8,10},{10,12},{12,14},{14,0},{1,3},{3,5},... | collective-permute-start | bytes 393224 | tf_op jit(solution)/shard_map/ppermute | solution.py:91
  87.9 0.0 collective-permute-done.5
  88.0 6.1 %collective-permute-done.6 = bf16[2,128,256]{2,1,0:T(8,128)(2,1)S(1)} collective-permute-done((bf16[2,128,256]{2,1,0:T(8,128)(2,1)S(1)}, bf16[2,128,256]{2,1,0:T(8,128)(2,1)S(1)}, u32[]{:S(2)}, u32[]{:S(2)}) %collective-permute-start.6) | collective-permute-done | bytes 131104 | tf_op jit(solution)/shard_map/ppermute | solution.py:91
  94.1 1.1 %fusion.1 = bf16[128,256]{1,0:T(8,128)(2,1)} fusion(bf16[8,2,128,256]{3,2,1,0:T(8,128)(2,1)S(1)} %bitcast_dynamic-update-slice_fusion.1, bf16[8,2,256,256]{3,2,1,0:T(8,128)(2,1)S(1)} %bitcast.140), kind=kOutput, calls=%fused_computation.6 | convolution fusion | flops 268468224 | bytes 3211264 | tf_op jit(solution)/shard_map/pqtc,pqcj->tj/dot_general | solution.py:133
  (23 shorter events, 0.2 us)
Async XLA Ops:
  0.0 49.1 %copy-start = (bf16[4096,256]{1,0:T(8,128)(2,1)S(1)}, bf16[4096,256]{1,0:T(8,128)(2,1)}, u32[]{:S(2)}) copy-start(bf16[4096,256]{1,0:T(8,128)(2,1)} %param.13) | copy-start | bytes 6291460
  0.0 27.0 %copy-start.2 = (f32[4,8192]{1,0:T(4,128)S(1)}, f32[4,8192]{1,0:T(4,128)}, u32[]{:S(2)}) copy-start(f32[4,8192]{1,0:T(4,128)} %param.11) | copy-start | bytes 393220
  3.9 33.0 %all-to-all-start = ((bf16[64,3,4,128]{3,2,1,0:T(4,128)(2,1)}), bf16[64,3,4,128]{3,2,1,0:T(4,128)(2,1)S(1)}, u32[]{:S(2)}, u32[]{:S(2)}) async-start(bf16[64,3,4,128]{3,2,1,0:T(4,128)(2,1)} %copy.40), calls=%async_computation | async-start | bytes 393216 | tf_op jit(solution)/shard_map/all_to_all | solution.py:120
  39.1 1.0 %copy-start.3 = (f32[4]{0:T(128)S(1)}, f32[4]{0:T(128)}, u32[]{:S(2)}) copy-start(f32[4]{0:T(128)} %param.12) | copy-start | bytes 52
  41.1 19.9 %all-to-all-start.1 = ((bf16[128,4,128]{2,1,0:T(4,128)(2,1)}), bf16[128,4,128]{2,1,0:T(4,128)(2,1)S(1)}, u32[]{:S(2)}, u32[]{:S(2)}) async-start(bf16[128,4,128]{2,1,0:T(4,128)(2,1)} %bitcast.30), calls=%async_computation.1 | async-start | bytes 262144 | tf_op jit(solution)/shard_map/all_to_all | solution.py:129
  61.1 33.0 %copy-start.1 = (bf16[16,256,256]{2,1,0:T(8,128)(2,1)S(1)}, bf16[16,256,256]{2,1,0:T(8,128)(2,1)}, u32[]{:S(2)}) copy-start(bf16[16,256,256]{2,1,0:T(8,128)(2,1)} %gather_fusion) | copy-start | bytes 6291460
  61.1 8.8 %collective-permute-start = (bf16[2,128,256]{2,1,0:T(8,128)(2,1)S(1)}, bf16[2,128,256]{2,1,0:T(8,128)(2,1)S(1)}, u32[]{:S(2)}, u32[]{:S(2)}) collective-permute-start(bf16[2,128,256]{2,1,0:T(8,128)(2,1)S(1)} %bitcast.150), channel_id=1, source_target_pairs={{0,2},{2,4},{4,6},{6,8},{8,10},{10,12},{12,14},{14,0},{1,3},{3,5},... | collective-permute-start | bytes 393224 | tf_op jit(solution)/shard_map/ppermute | solution.py:91
  63.8 8.0 %collective-permute-start.1 = (bf16[2,128,256]{2,1,0:T(8,128)(2,1)S(1)}, bf16[2,128,256]{2,1,0:T(8,128)(2,1)S(1)}, u32[]{:S(2)}, u32[]{:S(2)}) collective-permute-start(bf16[2,128,256]{2,1,0:T(8,128)(2,1)S(1)} %bitcast.151), channel_id=1, source_target_pairs={{0,14},{2,0},{4,2},{6,4},{8,6},{10,8},{12,10},{14,12},{1,15},{3,1}... | collective-permute-start | bytes 393224 | tf_op jit(solution)/shard_map/ppermute | solution.py:95
  69.9 8.1 %collective-permute-start.2 = (bf16[2,128,256]{2,1,0:T(8,128)(2,1)S(1)}, bf16[2,128,256]{2,1,0:T(8,128)(2,1)S(1)}, u32[]{:S(2)}, u32[]{:S(2)}) collective-permute-start(bf16[2,128,256]{2,1,0:T(8,128)(2,1)S(1)} %collective-permute-done), channel_id=1, source_target_pairs={{0,2},{2,4},{4,6},{6,8},{8,10},{10,12},{12,14},{14,0},{1,3},{3,5},... | collective-permute-start | bytes 393224 | tf_op jit(solution)/shard_map/ppermute | solution.py:91
  71.8 8.1 %collective-permute-start.3 = (bf16[2,128,256]{2,1,0:T(8,128)(2,1)S(1)}, bf16[2,128,256]{2,1,0:T(8,128)(2,1)S(1)}, u32[]{:S(2)}, u32[]{:S(2)}) collective-permute-start(bf16[2,128,256]{2,1,0:T(8,128)(2,1)S(1)} %collective-permute-done.1), channel_id=1, source_target_pairs={{0,14},{2,0},{4,2},{6,4},{8,6},{10,8},{12,10},{14,12},{1,15},{3,1}... | collective-permute-start | bytes 393224 | tf_op jit(solution)/shard_map/ppermute | solution.py:95
  77.9 8.1 %collective-permute-start.4 = (bf16[2,128,256]{2,1,0:T(8,128)(2,1)S(1)}, bf16[2,128,256]{2,1,0:T(8,128)(2,1)S(1)}, u32[]{:S(2)}, u32[]{:S(2)}) collective-permute-start(bf16[2,128,256]{2,1,0:T(8,128)(2,1)S(1)} %collective-permute-done.2), channel_id=1, source_target_pairs={{0,2},{2,4},{4,6},{6,8},{8,10},{10,12},{12,14},{14,0},{1,3},{3,5},... | collective-permute-start | bytes 393224 | tf_op jit(solution)/shard_map/ppermute | solution.py:91
  79.9 8.1 %collective-permute-start.5 = (bf16[2,128,256]{2,1,0:T(8,128)(2,1)S(1)}, bf16[2,128,256]{2,1,0:T(8,128)(2,1)S(1)}, u32[]{:S(2)}, u32[]{:S(2)}) collective-permute-start(bf16[2,128,256]{2,1,0:T(8,128)(2,1)S(1)} %collective-permute-done.3), channel_id=1, source_target_pairs={{0,14},{2,0},{4,2},{6,4},{8,6},{10,8},{12,10},{14,12},{1,15},{3,1}... | collective-permute-start | bytes 393224 | tf_op jit(solution)/shard_map/ppermute | solution.py:95
  86.0 8.1 %collective-permute-start.6 = (bf16[2,128,256]{2,1,0:T(8,128)(2,1)S(1)}, bf16[2,128,256]{2,1,0:T(8,128)(2,1)S(1)}, u32[]{:S(2)}, u32[]{:S(2)}) collective-permute-start(bf16[2,128,256]{2,1,0:T(8,128)(2,1)S(1)} %collective-permute-done.4), channel_id=1, source_target_pairs={{0,2},{2,4},{4,6},{6,8},{8,10},{10,12},{12,14},{14,0},{1,3},{3,5},... | collective-permute-start | bytes 393224 | tf_op jit(solution)/shard_map/ppermute | solution.py:91

commit v13 on v12

--- a/solution.py
+++ b/solution.py
@@ -83,18 +83,20 @@
 def gather_pairs(held):
     size = lax.axis_size("x")
     mine = lax.axis_index("x")
-    slots = [held]
-    places = [mine]
+
+    def moved(block, step):
+        return lax.ppermute(block, "x", [(i, (i + step) % size) for i in range(size)])
+
+    across = moved(held, size // 2)
+    slots = [held, across]
+    places = [mine, (mine + size // 2) % size]
     right = held
     left = held
-    for step in range(1, size // 2 + 1):
-        right = lax.ppermute(right, "x", [(i, (i + 1) % size) for i in range(size)])
-        slots.append(right)
-        places.append((mine - step) % size)
-        if step < size - step:
-            left = lax.ppermute(left, "x", [(i, (i - 1) % size) for i in range(size)])
-            slots.append(left)
-            places.append((mine + step) % size)
+    for step in range(1, size // 2):
+        right = moved(right, 1)
+        left = moved(left, -1)
+        slots += [right, left]
+        places += [(mine - step) % size, (mine + step) % size]
     place = jnp.stack(places)
     order = jnp.stack([place * 2, place * 2 + 1], axis=1)
     return jnp.stack(slots), order

time: 95.7 us -> 98.1 us (1.025)
  the two profiles are of different devices: /device:TPU:8 before, /device:TPU:14 now
where the time goes in v13:
time: 98.1 us; the launch traced here: 97.5 us
  starting transfers between devices  54.9 us (56%)
  waiting for transfers between devices  28.4 us (29%)
  local copies, waits for them, and re-layouts  8.01 us (8%)
  matrix products  3.85 us (4%)
  other arithmetic  1.9 us (2%)
    ppermute x7, starting transfers between devices, moved(): lax.ppermute(block, 'x', [(i, (i + step) % size) for i in range(size)])  26.1 us
    all_to_all x1, starting transfers between devices, body(): lax.all_to_all(raw, SEQ, split_axis=0, concat_axis=0, tiled=True)  21.1 us
    all_to_all x1, waiting for transfers between devices, body(): lax.all_to_all(both, ('yh',) + SEQ, split_axis=0, concat_axis=0, tiled=True)  9.89 us
    all_to_all x1, waiting for transfers between devices, body(): lax.all_to_all(raw, SEQ, split_axis=0, concat_axis=0, tiled=True)  9.48 us
    ppermute x7, waiting for transfers between devices, moved(): lax.ppermute(block, 'x', [(i, (i + step) % size) for i in range(size)])  9.03 us
    all_to_all x1, starting transfers between devices, body(): lax.all_to_all(both, ('yh',) + SEQ, split_axis=0, concat_axis=0, tiled=True)  7.76 us
    unnamed x19, local copies, waits for them, and re-layouts  3.12 us
    gather x1, local copies, waits for them, and re-layouts, body(): weight = out_weight.reshape(-1, width, out_weight.shape[1])[order]  2.01 us
  transfers between devices with their start and end apart: 9, of which 6 were waited for; matrix products, arithmetic and copies ran while one was open for 5% of the time, Pallas kernels for 0%

profile of v13, /device:TPU:14, one launch (start us, length us, event | category | flops | bytes accessed | tf_op | source)
XLA Modules:
  0.0 97.5 jit_solution(99825304085801831)
XLA Ops:
  0.0 1.1 %copy.37 = bf16[128,256]{0,1:T(8,128)(2,1)S(1)} copy(bf16[128,256]{1,0:T(8,128)(2,1)} %param.7) | data formatting | bytes 131072 | tf_op args[0]
  1.1 1.0 copy.38
  2.1 1.0 copy.39
  3.0 0.2 maximum_bitcast_fusion
  3.2 0.7 copy.40
  3.9 21.1 %all-to-all-start = ((bf16[64,3,4,128]{3,2,1,0:T(4,128)(2,1)}), bf16[64,3,4,128]{3,2,1,0:T(4,128)(2,1)S(1)}, u32[]{:S(2)}, u32[]{:S(2)}) async-start(bf16[64,3,4,128]{3,2,1,0:T(4,128)(2,1)} %copy.40), calls=%async_computation | async-start | bytes 393216 | tf_op jit(solution)/shard_map/all_to_all | solution.py:122
  25.0 0.3 broadcast_multiply_fusion
  25.3 0.3 fusion.47
  25.6 0.9 fusion.50
  26.6 0.1 stack.96
  26.7 0.3 fusion.45
  27.0 0.4 convolution_bitcast_fusion
  27.4 9.5 %all-to-all-done = bf16[64,3,4,128]{3,2,1,0:T(4,128)(2,1)S(1)} async-done(((bf16[64,3,4,128]{3,2,1,0:T(4,128)(2,1)}), bf16[64,3,4,128]{3,2,1,0:T(4,128)(2,1)S(1)}, u32[]{:S(2)}, u32[]{:S(2)}) %all-to-all-start) | async-done | bytes 196640 | tf_op jit(solution)/shard_map/all_to_all | solution.py:122
  37.0 0.1 slice_bitcast_fusion.2
  37.0 0.3 multiply_convert_fusion.1
  37.4 0.3 convolution_bitcast_fusion.1
  37.7 0.1 multiply_add_fusion.3
  37.9 0.6 fusion.2
  38.5 0.6 fusion.6
  39.1 0.0 copy-start.3
  39.1 0.1 multiply_subtract_fusion.1
  39.2 0.4 fusion.10
  39.6 0.1 multiply_subtract_fusion
  39.7 0.4 fusion
  40.1 0.2 fusion.35
  40.4 0.1 copy.50
  40.4 0.7 broadcast_in_dim.2
  41.1 7.8 %all-to-all-start.1 = ((bf16[128,4,128]{2,1,0:T(4,128)(2,1)}), bf16[128,4,128]{2,1,0:T(4,128)(2,1)S(1)}, u32[]{:S(2)}, u32[]{:S(2)}) async-start(bf16[128,4,128]{2,1,0:T(4,128)(2,1)} %bitcast.30), calls=%async_computation.1 | async-start | bytes 262144 | tf_op jit(solution)/shard_map/all_to_all | solution.py:131
  48.9 0.1 copy.52
  49.0 0.1 reshape.722
  49.1 2.0 %gather_fusion = bf16[16,256,256]{2,1,0:T(8,128)(2,1)} fusion(bf16[16,256,256]{2,1,0:T(8,128)(2,1)S(1)} %bitcast.139, s32[1024]{0:T(1024)S(1)} %pad_clamp_fusion), kind=kCustom, calls=%fused_computation | custom fusion | bytes 4194368 | tf_op jit(solution)/shard_map/gather | solution.py:134
  51.1 9.9 %all-to-all-done.1 = bf16[128,4,128]{2,1,0:T(4,128)(2,1)S(1)} async-done(((bf16[128,4,128]{2,1,0:T(4,128)(2,1)}), bf16[128,4,128]{2,1,0:T(4,128)(2,1)S(1)}, u32[]{:S(2)}, u32[]{:S(2)}) %all-to-all-start.1) | async-done | bytes 131104 | tf_op jit(solution)/shard_map/all_to_all | solution.py:131
  61.0 0.1 copy.51
  61.1 2.4 %collective-permute-start.1 = (bf16[2,128,256]{2,1,0:T(8,128)(2,1)S(1)}, bf16[2,128,256]{2,1,0:T(8,128)(2,1)S(1)}, u32[]{:S(2)}, u32[]{:S(2)}) collective-permute-start(bf16[2,128,256]{2,1,0:T(8,128)(2,1)S(1)} %bitcast.149), channel_id=1, source_target_pairs={{0,2},{2,4},{4,6},{6,8},{8,10},{10,12},{12,14},{14,0},{1,3},{3,5},... | collective-permute-start | bytes 393224 | tf_op jit(solution)/shard_map/ppermute | solution.py:88
  63.5 7.4 %collective-permute-start = (bf16[2,128,256]{2,1,0:T(8,128)(2,1)S(1)}, bf16[2,128,256]{2,1,0:T(8,128)(2,1)S(1)}, u32[]{:S(2)}, u32[]{:S(2)}) collective-permute-start(bf16[2,128,256]{2,1,0:T(8,128)(2,1)S(1)} %bitcast.150), channel_id=1, source_target_pairs={{0,8},{2,10},{4,12},{6,14},{8,0},{10,2},{12,4},{14,6},{1,9},{3,11}... | collective-permute-start | bytes 393224 | tf_op jit(solution)/shard_map/ppermute | solution.py:88
  70.9 1.9 %collective-permute-start.2 = (bf16[2,128,256]{2,1,0:T(8,128)(2,1)S(1)}, bf16[2,128,256]{2,1,0:T(8,128)(2,1)S(1)}, u32[]{:S(2)}, u32[]{:S(2)}) collective-permute-start(bf16[2,128,256]{2,1,0:T(8,128)(2,1)S(1)} %bitcast.151), channel_id=1, source_target_pairs={{0,14},{2,0},{4,2},{6,4},{8,6},{10,8},{12,10},{14,12},{1,15},{3,1}... | collective-permute-start | bytes 393224 | tf_op jit(solution)/shard_map/ppermute | solution.py:88
  72.9 0.0 collective-permute-done.1
  72.9 5.1 %collective-permute-start.3 = (bf16[2,128,256]{2,1,0:T(8,128)(2,1)S(1)}, bf16[2,128,256]{2,1,0:T(8,128)(2,1)S(1)}, u32[]{:S(2)}, u32[]{:S(2)}) collective-permute-start(bf16[2,128,256]{2,1,0:T(8,128)(2,1)S(1)} %collective-permute-done.1), channel_id=1, source_target_pairs={{0,2},{2,4},{4,6},{6,8},{8,10},{10,12},{12,14},{14,0},{1,3},{3,5},... | collective-permute-start | bytes 393224 | tf_op jit(solution)/shard_map/ppermute | solution.py:88
  78.0 2.2 %collective-permute-done.2 = bf16[2,128,256]{2,1,0:T(8,128)(2,1)S(1)} collective-permute-done((bf16[2,128,256]{2,1,0:T(8,128)(2,1)S(1)}, bf16[2,128,256]{2,1,0:T(8,128)(2,1)S(1)}, u32[]{:S(2)}, u32[]{:S(2)}) %collective-permute-start.2) | collective-permute-done | bytes 131104 | tf_op jit(solution)/shard_map/ppermute | solution.py:88
  80.2 3.5 %collective-permute-start.4 = (bf16[2,128,256]{2,1,0:T(8,128)(2,1)S(1)}, bf16[2,128,256]{2,1,0:T(8,128)(2,1)S(1)}, u32[]{:S(2)}, u32[]{:S(2)}) collective-permute-start(bf16[2,128,256]{2,1,0:T(8,128)(2,1)S(1)} %collective-permute-done.2), channel_id=1, source_target_pairs={{0,14},{2,0},{4,2},{6,4},{8,6},{10,8},{12,10},{14,12},{1,15},{3,1}... | collective-permute-start | bytes 393224 | tf_op jit(solution)/shard_map/ppermute | solution.py:88
  83.7 0.0 collective-permute-done
  83.8 0.0 collective-permute-done.3
  83.8 3.6 %collective-permute-start.5 = (bf16[2,128,256]{2,1,0:T(8,128)(2,1)S(1)}, bf16[2,128,256]{2,1,0:T(8,128)(2,1)S(1)}, u32[]{:S(2)}, u32[]{:S(2)}) collective-permute-start(bf16[2,128,256]{2,1,0:T(8,128)(2,1)S(1)} %collective-permute-done.3), channel_id=1, source_target_pairs={{0,2},{2,4},{4,6},{6,8},{8,10},{10,12},{12,14},{14,0},{1,3},{3,5},... | collective-permute-start | bytes 393224 | tf_op jit(solution)/shard_map/ppermute | solution.py:88
  87.4 1.0 %collective-permute-done.4 = bf16[2,128,256]{2,1,0:T(8,128)(2,1)S(1)} collective-permute-done((bf16[2,128,256]{2,1,0:T(8,128)(2,1)S(1)}, bf16[2,128,256]{2,1,0:T(8,128)(2,1)S(1)}, u32[]{:S(2)}, u32[]{:S(2)}) %collective-permute-start.4) | collective-permute-done | bytes 131104 | tf_op jit(solution)/shard_map/ppermute | solution.py:88
  88.4 2.2 %collective-permute-start.6 = (bf16[2,128,256]{2,1,0:T(8,128)(2,1)S(1)}, bf16[2,128,256]{2,1,0:T(8,128)(2,1)S(1)}, u32[]{:S(2)}, u32[]{:S(2)}) collective-permute-start(bf16[2,128,256]{2,1,0:T(8,128)(2,1)S(1)} %collective-permute-done.4), channel_id=1, source_target_pairs={{0,14},{2,0},{4,2},{6,4},{8,6},{10,8},{12,10},{14,12},{1,15},{3,1}... | collective-permute-start | bytes 393224 | tf_op jit(solution)/shard_map/ppermute | solution.py:88
  90.6 0.1 collective-permute-done.5
  90.7 5.8 %collective-permute-done.6 = bf16[2,128,256]{2,1,0:T(8,128)(2,1)S(1)} collective-permute-done((bf16[2,128,256]{2,1,0:T(8,128)(2,1)S(1)}, bf16[2,128,256]{2,1,0:T(8,128)(2,1)S(1)}, u32[]{:S(2)}, u32[]{:S(2)}) %collective-permute-start.6) | collective-permute-done | bytes 131104 | tf_op jit(solution)/shard_map/ppermute | solution.py:88
  96.5 1.1 %fusion.1 = bf16[128,256]{1,0:T(8,128)(2,1)} fusion(bf16[8,2,128,256]{3,2,1,0:T(8,128)(2,1)S(1)} %bitcast_dynamic-update-slice_fusion.1, bf16[8,2,256,256]{3,2,1,0:T(8,128)(2,1)S(1)} %bitcast.140), kind=kOutput, calls=%fused_computation.6 | convolution fusion | flops 268468224 | bytes 3211264 | tf_op jit(solution)/shard_map/pqtc,pqcj->tj/dot_general | solution.py:135
  (23 shorter events, 0.2 us)
Async XLA Ops:
  0.0 49.1 %copy-start = (bf16[4096,256]{1,0:T(8,128)(2,1)S(1)}, bf16[4096,256]{1,0:T(8,128)(2,1)}, u32[]{:S(2)}) copy-start(bf16[4096,256]{1,0:T(8,128)(2,1)} %param.13) | copy-start | bytes 6291460
  0.0 27.0 %copy-start.2 = (f32[4,8192]{1,0:T(4,128)S(1)}, f32[4,8192]{1,0:T(4,128)}, u32[]{:S(2)}) copy-start(f32[4,8192]{1,0:T(4,128)} %param.11) | copy-start | bytes 393220
  3.9 33.0 %all-to-all-start = ((bf16[64,3,4,128]{3,2,1,0:T(4,128)(2,1)}), bf16[64,3,4,128]{3,2,1,0:T(4,128)(2,1)S(1)}, u32[]{:S(2)}, u32[]{:S(2)}) async-start(bf16[64,3,4,128]{3,2,1,0:T(4,128)(2,1)} %copy.40), calls=%async_computation | async-start | bytes 393216 | tf_op jit(solution)/shard_map/all_to_all | solution.py:122
  39.1 1.0 copy-start.3
  41.1 19.9 %all-to-all-start.1 = ((bf16[128,4,128]{2,1,0:T(4,128)(2,1)}), bf16[128,4,128]{2,1,0:T(4,128)(2,1)S(1)}, u32[]{:S(2)}, u32[]{:S(2)}) async-start(bf16[128,4,128]{2,1,0:T(4,128)(2,1)} %bitcast.30), calls=%async_computation.1 | async-start | bytes 262144 | tf_op jit(solution)/shard_map/all_to_all | solution.py:131
  61.1 35.3 %copy-start.1 = (bf16[16,256,256]{2,1,0:T(8,128)(2,1)S(1)}, bf16[16,256,256]{2,1,0:T(8,128)(2,1)}, u32[]{:S(2)}) copy-start(bf16[16,256,256]{2,1,0:T(8,128)(2,1)} %gather_fusion) | copy-start | bytes 6291460
  61.1 11.8 %collective-permute-start.1 = (bf16[2,128,256]{2,1,0:T(8,128)(2,1)S(1)}, bf16[2,128,256]{2,1,0:T(8,128)(2,1)S(1)}, u32[]{:S(2)}, u32[]{:S(2)}) collective-permute-start(bf16[2,128,256]{2,1,0:T(8,128)(2,1)S(1)} %bitcast.149), channel_id=1, source_target_pairs={{0,2},{2,4},{4,6},{6,8},{8,10},{10,12},{12,14},{14,0},{1,3},{3,5},... | collective-permute-start | bytes 393224 | tf_op jit(solution)/shard_map/ppermute | solution.py:88
  63.5 20.2 %collective-permute-start = (bf16[2,128,256]{2,1,0:T(8,128)(2,1)S(1)}, bf16[2,128,256]{2,1,0:T(8,128)(2,1)S(1)}, u32[]{:S(2)}, u32[]{:S(2)}) collective-permute-start(bf16[2,128,256]{2,1,0:T(8,128)(2,1)S(1)} %bitcast.150), channel_id=1, source_target_pairs={{0,8},{2,10},{4,12},{6,14},{8,0},{10,2},{12,4},{14,6},{1,9},{3,11}... | collective-permute-start | bytes 393224 | tf_op jit(solution)/shard_map/ppermute | solution.py:88
  70.9 9.3 %collective-permute-start.2 = (bf16[2,128,256]{2,1,0:T(8,128)(2,1)S(1)}, bf16[2,128,256]{2,1,0:T(8,128)(2,1)S(1)}, u32[]{:S(2)}, u32[]{:S(2)}) collective-permute-start(bf16[2,128,256]{2,1,0:T(8,128)(2,1)S(1)} %bitcast.151), channel_id=1, source_target_pairs={{0,14},{2,0},{4,2},{6,4},{8,6},{10,8},{12,10},{14,12},{1,15},{3,1}... | collective-permute-start | bytes 393224 | tf_op jit(solution)/shard_map/ppermute | solution.py:88
  72.9 10.9 %collective-permute-start.3 = (bf16[2,128,256]{2,1,0:T(8,128)(2,1)S(1)}, bf16[2,128,256]{2,1,0:T(8,128)(2,1)S(1)}, u32[]{:S(2)}, u32[]{:S(2)}) collective-permute-start(bf16[2,128,256]{2,1,0:T(8,128)(2,1)S(1)} %collective-permute-done.1), channel_id=1, source_target_pairs={{0,2},{2,4},{4,6},{6,8},{8,10},{10,12},{12,14},{14,0},{1,3},{3,5},... | collective-permute-start | bytes 393224 | tf_op jit(solution)/shard_map/ppermute | solution.py:88
  80.2 8.1 %collective-permute-start.4 = (bf16[2,128,256]{2,1,0:T(8,128)(2,1)S(1)}, bf16[2,128,256]{2,1,0:T(8,128)(2,1)S(1)}, u32[]{:S(2)}, u32[]{:S(2)}) collective-permute-start(bf16[2,128,256]{2,1,0:T(8,128)(2,1)S(1)} %collective-permute-done.2), channel_id=1, source_target_pairs={{0,14},{2,0},{4,2},{6,4},{8,6},{10,8},{12,10},{14,12},{1,15},{3,1}... | collective-permute-start | bytes 393224 | tf_op jit(solution)/shard_map/ppermute | solution.py:88
  83.8 6.9 %collective-permute-start.5 = (bf16[2,128,256]{2,1,0:T(8,128)(2,1)S(1)}, bf16[2,128,256]{2,1,0:T(8,128)(2,1)S(1)}, u32[]{:S(2)}, u32[]{:S(2)}) collective-permute-start(bf16[2,128,256]{2,1,0:T(8,128)(2,1)S(1)} %collective-permute-done.3), channel_id=1, source_target_pairs={{0,2},{2,4},{4,6},{6,8},{8,10},{10,12},{12,14},{14,0},{1,3},{3,5},... | collective-permute-start | bytes 393224 | tf_op jit(solution)/shard_map/ppermute | solution.py:88
  88.4 8.1 %collective-permute-start.6 = (bf16[2,128,256]{2,1,0:T(8,128)(2,1)S(1)}, bf16[2,128,256]{2,1,0:T(8,128)(2,1)S(1)}, u32[]{:S(2)}, u32[]{:S(2)}) collective-permute-start(bf16[2,128,256]{2,1,0:T(8,128)(2,1)S(1)} %collective-permute-done.4), channel_id=1, source_target_pairs={{0,14},{2,0},{4,2},{6,4},{8,6},{10,8},{12,10},{14,12},{1,15},{3,1}... | collective-permute-start | bytes 393224 | tf_op jit(solution)/shard_map/ppermute | solution.py:88

commit v14 on v12

--- a/solution.py
+++ b/solution.py
@@ -123,14 +123,17 @@
     short_q = causal_filter(whole[0], own_taps[0]).astype(jnp.bfloat16)
     signal = (causal_filter(whole[1], own_taps[1]) * causal_filter(whole[2], own_taps[2])).astype(jnp.bfloat16)
     convolved = long_convolution(signal, long_filter, skip_gain).astype(jnp.bfloat16)
-    gated_t = (short_q.astype(jnp.float32) * convolved.astype(jnp.float32)).astype(jnp.bfloat16)
-    outgoing = gated_t.reshape(per_group, groups, rows).transpose(1, 0, 2)
-    both = jnp.broadcast_to(outgoing[None], (2,) + outgoing.shape).reshape((2 * groups,) + outgoing.shape[1:])
+    product = short_q.astype(jnp.float32) * convolved.astype(jnp.float32)
+    gated_t = jnp.broadcast_to(product[None], (2,) + product.shape).astype(jnp.bfloat16)
+    both = gated_t.reshape(2, per_group, groups, rows).transpose(0, 2, 1, 3).reshape(2 * groups, per_group, rows)
     returned = lax.all_to_all(both, ("yh",) + SEQ, split_axis=0, concat_axis=0, tiled=True)
     held = returned.reshape(2, width, rows).transpose(0, 2, 1)
     pieces, order = gather_pairs(held)
     weight = out_weight.reshape(-1, width, out_weight.shape[1])[order]
-    result = jnp.einsum("pqtc,pqcj->tj", pieces, weight, preferred_element_type=jnp.float32)
+    result = sum(
+        jnp.einsum("qtc,qcj->tj", pieces[p], weight[p], preferred_element_type=jnp.float32)
+        for p in range(pieces.shape[0])
+    )
     return result.astype(jnp.bfloat16)
 
 

time: 95.7 us -> 102 us (1.066)
  the two profiles are of different devices: /device:TPU:8 before, /device:TPU:16 now
where the time goes in v14:
time: 102 us; the launch traced here: 101 us
  starting transfers between devices  52.1 us (51%)
  waiting for transfers between devices  30.1 us (30%)
  matrix products  8.74 us (9%)
  local copies, waits for them, and re-layouts  7.95 us (8%)
  other arithmetic  1.9 us (2%)
    all_to_all x1, starting transfers between devices, body(): lax.all_to_all(raw, SEQ, split_axis=0, concat_axis=0, tiled=True)  21 us
    ppermute x3, starting transfers between devices, gather_pairs(): left = lax.ppermute(left, 'x', [(i, (i - 1) % size) for i in range(size)])  15.6 us
    ppermute x4, waiting for transfers between devices, gather_pairs(): right = lax.ppermute(right, 'x', [(i, (i + 1) % size) for i in range(size)])  11.7 us
    all_to_all x1, waiting for transfers between devices, body(): lax.all_to_all(both, ('yh',) + SEQ, split_axis=0, concat_axis=0, tiled=True)  9.55 us
    all_to_all x1, waiting for transfers between devices, body(): lax.all_to_all(raw, SEQ, split_axis=0, concat_axis=0, tiled=True)  8.88 us
    all_to_all x1, starting transfers between devices, body(): lax.all_to_all(both, ('yh',) + SEQ, split_axis=0, concat_axis=0, tiled=True)  7.91 us
    ppermute x4, starting transfers between devices, gather_pairs(): right = lax.ppermute(right, 'x', [(i, (i + 1) % size) for i in range(size)])  7.67 us
    dot_general x8, matrix products, body(): jnp.einsum('qtc,qcj->tj', pieces[p], weight[p], preferred_element_type=jn...  5.96 us
  transfers between devices with their start and end apart: 9, of which 4 were waited for; matrix products, arithmetic and copies ran while one was open for 9% of the time, Pallas kernels for 0%

profile of v14, /device:TPU:16, one launch (start us, length us, event | category | flops | bytes accessed | tf_op | source)
XLA Modules:
  0.0 101.3 jit_solution(14322010392485764909)
XLA Ops:
  0.0 1.1 %copy.36 = bf16[128,256]{0,1:T(8,128)(2,1)S(1)} copy(bf16[128,256]{1,0:T(8,128)(2,1)} %param.7) | data formatting | bytes 131072 | tf_op args[0]
  1.1 1.0 copy.37
  2.1 1.0 copy.38
  3.0 0.2 maximum_bitcast_fusion
  3.2 0.7 copy.39
  3.9 21.0 %all-to-all-start = ((bf16[64,3,4,128]{3,2,1,0:T(4,128)(2,1)}), bf16[64,3,4,128]{3,2,1,0:T(4,128)(2,1)S(1)}, u32[]{:S(2)}, u32[]{:S(2)}) async-start(bf16[64,3,4,128]{3,2,1,0:T(4,128)(2,1)} %copy.39), calls=%async_computation | async-start | bytes 393216 | tf_op jit(solution)/shard_map/all_to_all | solution.py:120
  24.9 0.3 fusion.62
  25.2 0.3 broadcast_multiply_fusion
  25.5 0.9 fusion.65
  26.5 0.1 stack.60
  26.6 0.3 fusion.60
  26.9 0.4 convolution_bitcast_fusion
  27.3 8.9 %all-to-all-done = bf16[64,3,4,128]{3,2,1,0:T(4,128)(2,1)S(1)} async-done(((bf16[64,3,4,128]{3,2,1,0:T(4,128)(2,1)}), bf16[64,3,4,128]{3,2,1,0:T(4,128)(2,1)S(1)}, u32[]{:S(2)}, u32[]{:S(2)}) %all-to-all-start) | async-done | bytes 196640 | tf_op jit(solution)/shard_map/all_to_all | solution.py:120
  36.3 0.1 slice_bitcast_fusion.2
  36.3 0.3 multiply_convert_fusion.1
  36.7 0.3 convolution_bitcast_fusion.1
  37.0 0.1 multiply_add_fusion.3
  37.2 0.6 fusion.9
  37.8 0.6 fusion.13
  38.4 0.1 multiply_subtract_fusion.1
  38.5 0.4 fusion.17
  38.9 0.1 multiply_subtract_fusion
  39.0 0.4 fusion
  39.4 0.2 fusion.50
  39.7 0.8 copy.49
  40.5 7.9 %all-to-all-start.1 = ((bf16[128,4,128]{2,1,0:T(4,128)(2,1)}), bf16[128,4,128]{2,1,0:T(4,128)(2,1)S(1)}, u32[]{:S(2)}, u32[]{:S(2)}) async-start(bf16[128,4,128]{2,1,0:T(4,128)(2,1)} %copy.49), calls=%async_computation.1 | async-start | bytes 262144 | tf_op jit(solution)/shard_map/all_to_all | solution.py:129
  48.4 0.1 copy.51
  48.5 0.1 reshape.720
  48.6 2.0 %gather_fusion = bf16[16,256,256]{2,1,0:T(8,128)(2,1)} fusion(bf16[16,256,256]{2,1,0:T(8,128)(2,1)S(1)} %bitcast.153, s32[1024]{0:T(1024)S(1)} %pad_clamp_fusion), kind=kCustom, calls=%fused_computation | custom fusion | bytes 4194368 | tf_op jit(solution)/shard_map/gather | solution.py:132
  50.6 9.6 %all-to-all-done.1 = bf16[128,4,128]{2,1,0:T(4,128)(2,1)S(1)} async-done(((bf16[128,4,128]{2,1,0:T(4,128)(2,1)}), bf16[128,4,128]{2,1,0:T(4,128)(2,1)S(1)}, u32[]{:S(2)}, u32[]{:S(2)}) %all-to-all-start.1) | async-done | bytes 131104 | tf_op jit(solution)/shard_map/all_to_all | solution.py:129
  60.1 0.1 copy.50
  60.3 4.9 %collective-permute-start.1 = (bf16[2,128,256]{2,1,0:T(8,128)(2,1)S(1)}, bf16[2,128,256]{2,1,0:T(8,128)(2,1)S(1)}, u32[]{:S(2)}, u32[]{:S(2)}) collective-permute-start(bf16[2,128,256]{2,1,0:T(8,128)(2,1)S(1)} %bitcast.164), channel_id=1, source_target_pairs={{0,14},{2,0},{4,2},{6,4},{8,6},{10,8},{12,10},{14,12},{1,15},{3,1}... | collective-permute-start | bytes 393224 | tf_op jit(solution)/shard_map/ppermute | solution.py:95
  65.2 1.9 %collective-permute-start = (bf16[2,128,256]{2,1,0:T(8,128)(2,1)S(1)}, bf16[2,128,256]{2,1,0:T(8,128)(2,1)S(1)}, u32[]{:S(2)}, u32[]{:S(2)}) collective-permute-start(bf16[2,128,256]{2,1,0:T(8,128)(2,1)S(1)} %bitcast.165), channel_id=1, source_target_pairs={{0,2},{2,4},{4,6},{6,8},{8,10},{10,12},{12,14},{14,0},{1,3},{3,5},... | collective-permute-start | bytes 393224 | tf_op jit(solution)/shard_map/ppermute | solution.py:91
  67.1 1.1 %convolution_bitcast_fusion.9 = f32[128,256]{1,0:T(8,128)S(1)} fusion(bf16[16,256,256]{2,1,0:T(8,128)(2,1)} %gather_fusion, bf16[2,256,128]{1,2,0:T(8,128)(2,1)S(1)} %copy.50), kind=kOutput, calls=%fused_computation.10 | convolution fusion | flops 33554432 | bytes 524288 | tf_op jit(solution)/shard_map/qtc,qcj->tj/dot_general | solution.py:134
  68.3 5.5 %collective-permute-start.3 = (bf16[2,128,256]{2,1,0:T(8,128)(2,1)S(1)}, bf16[2,128,256]{2,1,0:T(8,128)(2,1)S(1)}, u32[]{:S(2)}, u32[]{:S(2)}) collective-permute-start(bf16[2,128,256]{2,1,0:T(8,128)(2,1)S(1)} %collective-permute-done.1), channel_id=1, source_target_pairs={{0,14},{2,0},{4,2},{6,4},{8,6},{10,8},{12,10},{14,12},{1,15},{3,1}... | collective-permute-start | bytes 393224 | tf_op jit(solution)/shard_map/ppermute | solution.py:95
  73.8 1.1 %convolution_bitcast_fusion.7 = f32[128,256]{1,0:T(8,128)S(1)} fusion(bf16[2,128,256]{2,1,0:T(8,128)(2,1)S(1)} %collective-permute-done.1, bf16[16,256,256]{2,1,0:T(8,128)(2,1)} %gather_fusion), kind=kOutput, calls=%fused_computation.8 | convolution fusion | flops 33554432 | bytes 524288 | tf_op jit(solution)/shard_map/qtc,qcj->tj/dot_general | solution.py:134
  75.0 1.9 %collective-permute-start.2 = (bf16[2,128,256]{2,1,0:T(8,128)(2,1)S(1)}, bf16[2,128,256]{2,1,0:T(8,128)(2,1)S(1)}, u32[]{:S(2)}, u32[]{:S(2)}) collective-permute-start(bf16[2,128,256]{2,1,0:T(8,128)(2,1)S(1)} %collective-permute-done), channel_id=1, source_target_pairs={{0,2},{2,4},{4,6},{6,8},{8,10},{10,12},{12,14},{14,0},{1,3},{3,5},... | collective-permute-start | bytes 393224 | tf_op jit(solution)/shard_map/ppermute | solution.py:91
  76.9 1.1 %fusion.2 = f32[128,256]{1,0:T(8,128)S(1)} fusion(f32[128,256]{1,0:T(8,128)S(1)} %convolution_bitcast_fusion.7, f32[128,256]{1,0:T(8,128)S(1)} %convolution_bitcast_fusion.9, bf16[2,128,256]{2,1,0:T(8,128)(2,1)S(1)} %collective-permute-done, bf16[16,256,256]{2,1,0:T(8,128)(2,1)} %gather_fusion), kind=kOutput, calls=%fused_computation.14 | convolution fusion | flops 33619968 | bytes 786432 | tf_op jit(solution)/shard_map/qtc,qcj->tj/dot_general | solution.py:134
  78.0 5.1 %collective-permute-start.5 = (bf16[2,128,256]{2,1,0:T(8,128)(2,1)S(1)}, bf16[2,128,256]{2,1,0:T(8,128)(2,1)S(1)}, u32[]{:S(2)}, u32[]{:S(2)}) collective-permute-start(bf16[2,128,256]{2,1,0:T(8,128)(2,1)S(1)} %collective-permute-done.3), channel_id=1, source_target_pairs={{0,14},{2,0},{4,2},{6,4},{8,6},{10,8},{12,10},{14,12},{1,15},{3,1}... | collective-permute-start | bytes 393224 | tf_op jit(solution)/shard_map/ppermute | solution.py:95
  83.2 1.1 %convolution_bitcast_fusion.5 = f32[128,256]{1,0:T(8,128)S(1)} fusion(bf16[2,128,256]{2,1,0:T(8,128)(2,1)S(1)} %collective-permute-done.3, bf16[16,256,256]{2,1,0:T(8,128)(2,1)} %gather_fusion), kind=kOutput, calls=%fused_computation.6 | convolution fusion | flops 33554432 | bytes 524288 | tf_op jit(solution)/shard_map/qtc,qcj->tj/dot_general | solution.py:134
  84.3 1.9 %collective-permute-start.4 = (bf16[2,128,256]{2,1,0:T(8,128)(2,1)S(1)}, bf16[2,128,256]{2,1,0:T(8,128)(2,1)S(1)}, u32[]{:S(2)}, u32[]{:S(2)}) collective-permute-start(bf16[2,128,256]{2,1,0:T(8,128)(2,1)S(1)} %collective-permute-done.2), channel_id=1, source_target_pairs={{0,2},{2,4},{4,6},{6,8},{8,10},{10,12},{12,14},{14,0},{1,3},{3,5},... | collective-permute-start | bytes 393224 | tf_op jit(solution)/shard_map/ppermute | solution.py:91
  86.3 0.2 fusion.4
  86.5 0.2 convolution_bitcast_fusion.3
  86.7 5.7 %collective-permute-done.4 = bf16[2,128,256]{2,1,0:T(8,128)(2,1)S(1)} collective-permute-done((bf16[2,128,256]{2,1,0:T(8,128)(2,1)S(1)}, bf16[2,128,256]{2,1,0:T(8,128)(2,1)S(1)}, u32[]{:S(2)}, u32[]{:S(2)}) %collective-permute-start.4) | collective-permute-done | bytes 131104 | tf_op jit(solution)/shard_map/ppermute | solution.py:91
  92.4 1.9 %collective-permute-start.6 = (bf16[2,128,256]{2,1,0:T(8,128)(2,1)S(1)}, bf16[2,128,256]{2,1,0:T(8,128)(2,1)S(1)}, u32[]{:S(2)}, u32[]{:S(2)}) collective-permute-start(bf16[2,128,256]{2,1,0:T(8,128)(2,1)S(1)} %collective-permute-done.4), channel_id=1, source_target_pairs={{0,2},{2,4},{4,6},{6,8},{8,10},{10,12},{12,14},{14,0},{1,3},{3,5},... | collective-permute-start | bytes 393224 | tf_op jit(solution)/shard_map/ppermute | solution.py:91
  94.3 0.2 fusion.6
  94.5 5.9 %collective-permute-done.6 = bf16[2,128,256]{2,1,0:T(8,128)(2,1)S(1)} collective-permute-done((bf16[2,128,256]{2,1,0:T(8,128)(2,1)S(1)}, bf16[2,128,256]{2,1,0:T(8,128)(2,1)S(1)}, u32[]{:S(2)}, u32[]{:S(2)}) %collective-permute-start.6) | collective-permute-done | bytes 131104 | tf_op jit(solution)/shard_map/ppermute | solution.py:91
  100.5 0.8 fusion.8
  (22 shorter events, 0.1 us)
Async XLA Ops:
  0.0 48.6 %copy-start = (bf16[4096,256]{1,0:T(8,128)(2,1)S(1)}, bf16[4096,256]{1,0:T(8,128)(2,1)}, u32[]{:S(2)}) copy-start(bf16[4096,256]{1,0:T(8,128)(2,1)} %param.13) | copy-start | bytes 6291460
  0.0 26.9 %copy-start.2 = (f32[4,8192]{1,0:T(4,128)S(1)}, f32[4,8192]{1,0:T(4,128)}, u32[]{:S(2)}) copy-start(f32[4,8192]{1,0:T(4,128)} %param.11) | copy-start | bytes 393220
  3.9 32.3 %all-to-all-start = ((bf16[64,3,4,128]{3,2,1,0:T(4,128)(2,1)}), bf16[64,3,4,128]{3,2,1,0:T(4,128)(2,1)S(1)}, u32[]{:S(2)}, u32[]{:S(2)}) async-start(bf16[64,3,4,128]{3,2,1,0:T(4,128)(2,1)} %copy.39), calls=%async_computation | async-start | bytes 393216 | tf_op jit(solution)/shard_map/all_to_all | solution.py:120
  38.4 1.0 copy-start.3
  40.5 19.7 %all-to-all-start.1 = ((bf16[128,4,128]{2,1,0:T(4,128)(2,1)}), bf16[128,4,128]{2,1,0:T(4,128)(2,1)S(1)}, u32[]{:S(2)}, u32[]{:S(2)}) async-start(bf16[128,4,128]{2,1,0:T(4,128)(2,1)} %copy.49), calls=%async_computation.1 | async-start | bytes 262144 | tf_op jit(solution)/shard_map/all_to_all | solution.py:129
  60.3 26.0 %copy-start.1 = (bf16[16,256,256]{2,1,0:T(8,128)(2,1)S(1)}, bf16[16,256,256]{2,1,0:T(8,128)(2,1)}, u32[]{:S(2)}) copy-start(bf16[16,256,256]{2,1,0:T(8,128)(2,1)} %gather_fusion) | copy-start | bytes 6291460
  60.3 8.0 %collective-permute-start.1 = (bf16[2,128,256]{2,1,0:T(8,128)(2,1)S(1)}, bf16[2,128,256]{2,1,0:T(8,128)(2,1)S(1)}, u32[]{:S(2)}, u32[]{:S(2)}) collective-permute-start(bf16[2,128,256]{2,1,0:T(8,128)(2,1)S(1)} %bitcast.164), channel_id=1, source_target_pairs={{0,14},{2,0},{4,2},{6,4},{8,6},{10,8},{12,10},{14,12},{1,15},{3,1}... | collective-permute-start | bytes 393224 | tf_op jit(solution)/shard_map/ppermute | solution.py:95
  65.2 9.8 %collective-permute-start = (bf16[2,128,256]{2,1,0:T(8,128)(2,1)S(1)}, bf16[2,128,256]{2,1,0:T(8,128)(2,1)S(1)}, u32[]{:S(2)}, u32[]{:S(2)}) collective-permute-start(bf16[2,128,256]{2,1,0:T(8,128)(2,1)S(1)} %bitcast.165), channel_id=1, source_target_pairs={{0,2},{2,4},{4,6},{6,8},{8,10},{10,12},{12,14},{14,0},{1,3},{3,5},... | collective-permute-start | bytes 393224 | tf_op jit(solution)/shard_map/ppermute | solution.py:91
  68.3 9.8 %collective-permute-start.3 = (bf16[2,128,256]{2,1,0:T(8,128)(2,1)S(1)}, bf16[2,128,256]{2,1,0:T(8,128)(2,1)S(1)}, u32[]{:S(2)}, u32[]{:S(2)}) collective-permute-start(bf16[2,128,256]{2,1,0:T(8,128)(2,1)S(1)} %collective-permute-done.1), channel_id=1, source_target_pairs={{0,14},{2,0},{4,2},{6,4},{8,6},{10,8},{12,10},{14,12},{1,15},{3,1}... | collective-permute-start | bytes 393224 | tf_op jit(solution)/shard_map/ppermute | solution.py:95
  75.0 9.4 %collective-permute-start.2 = (bf16[2,128,256]{2,1,0:T(8,128)(2,1)S(1)}, bf16[2,128,256]{2,1,0:T(8,128)(2,1)S(1)}, u32[]{:S(2)}, u32[]{:S(2)}) collective-permute-start(bf16[2,128,256]{2,1,0:T(8,128)(2,1)S(1)} %collective-permute-done), channel_id=1, source_target_pairs={{0,2},{2,4},{4,6},{6,8},{8,10},{10,12},{12,14},{14,0},{1,3},{3,5},... | collective-permute-start | bytes 393224 | tf_op jit(solution)/shard_map/ppermute | solution.py:91
  78.0 8.4 %collective-permute-start.5 = (bf16[2,128,256]{2,1,0:T(8,128)(2,1)S(1)}, bf16[2,128,256]{2,1,0:T(8,128)(2,1)S(1)}, u32[]{:S(2)}, u32[]{:S(2)}) collective-permute-start(bf16[2,128,256]{2,1,0:T(8,128)(2,1)S(1)} %collective-permute-done.3), channel_id=1, source_target_pairs={{0,14},{2,0},{4,2},{6,4},{8,6},{10,8},{12,10},{14,12},{1,15},{3,1}... | collective-permute-start | bytes 393224 | tf_op jit(solution)/shard_map/ppermute | solution.py:95
  84.3 8.1 %collective-permute-start.4 = (bf16[2,128,256]{2,1,0:T(8,128)(2,1)S(1)}, bf16[2,128,256]{2,1,0:T(8,128)(2,1)S(1)}, u32[]{:S(2)}, u32[]{:S(2)}) collective-permute-start(bf16[2,128,256]{2,1,0:T(8,128)(2,1)S(1)} %collective-permute-done.2), channel_id=1, source_target_pairs={{0,2},{2,4},{4,6},{6,8},{8,10},{10,12},{12,14},{14,0},{1,3},{3,5},... | collective-permute-start | bytes 393224 | tf_op jit(solution)/shard_map/ppermute | solution.py:91
  92.4 8.1 %collective-permute-start.6 = (bf16[2,128,256]{2,1,0:T(8,128)(2,1)S(1)}, bf16[2,128,256]{2,1,0:T(8,128)(2,1)S(1)}, u32[]{:S(2)}, u32[]{:S(2)}) collective-permute-start(bf16[2,128,256]{2,1,0:T(8,128)(2,1)S(1)} %collective-permute-done.4), channel_id=1, source_target_pairs={{0,2},{2,4},{4,6},{6,8},{8,10},{10,12},{12,14},{14,0},{1,3},{3,5},... | collective-permute-start | bytes 393224 | tf_op jit(solution)/shard_map/ppermute | solution.py:91

commit v15 on v12

--- a/solution.py
+++ b/solution.py
@@ -125,7 +125,7 @@
     convolved = long_convolution(signal, long_filter, skip_gain).astype(jnp.bfloat16)
     gated_t = (short_q.astype(jnp.float32) * convolved.astype(jnp.float32)).astype(jnp.bfloat16)
     outgoing = gated_t.reshape(per_group, groups, rows).transpose(1, 0, 2)
-    both = jnp.broadcast_to(outgoing[None], (2,) + outgoing.shape).reshape((2 * groups,) + outgoing.shape[1:])
+    both = jnp.concatenate([outgoing, outgoing], 0)
     returned = lax.all_to_all(both, ("yh",) + SEQ, split_axis=0, concat_axis=0, tiled=True)
     held = returned.reshape(2, width, rows).transpose(0, 2, 1)
     pieces, order = gather_pairs(held)

time: 95.7 us -> 95.6 us (level)
    unnamed x19 -> x18, local copies, waits for them, and re-layouts: 3.12 us -> 3.11 us
where the time goes in v15:
time: 95.6 us; the launch traced here: 95.1 us
  starting transfers between devices  52 us (54%)
  waiting for transfers between devices  28.9 us (30%)
  local copies, waits for them, and re-layouts  7.25 us (8%)
  matrix products  3.86 us (4%)
  other arithmetic  2.61 us (3%)
    all_to_all x1, starting transfers between devices, body(): lax.all_to_all(raw, SEQ, split_axis=0, concat_axis=0, tiled=True)  21.1 us
    ppermute x3, starting transfers between devices, gather_pairs(): left = lax.ppermute(left, 'x', [(i, (i - 1) % size) for i in range(size)])  14.8 us
    all_to_all x1, waiting for transfers between devices, body(): lax.all_to_all(both, ('yh',) + SEQ, split_axis=0, concat_axis=0, tiled=True)  9.89 us
    ppermute x4, waiting for transfers between devices, gather_pairs(): right = lax.ppermute(right, 'x', [(i, (i + 1) % size) for i in range(size)])  9.54 us
    all_to_all x1, waiting for transfers between devices, body(): lax.all_to_all(raw, SEQ, split_axis=0, concat_axis=0, tiled=True)  9.46 us
    ppermute x4, starting transfers between devices, gather_pairs(): right = lax.ppermute(right, 'x', [(i, (i + 1) % size) for i in range(size)])  8.35 us
    all_to_all x1, starting transfers between devices, body(): lax.all_to_all(both, ('yh',) + SEQ, split_axis=0, concat_axis=0, tiled=True)  7.77 us
    unnamed x18, local copies, waits for them, and re-layouts  3.11 us
  transfers between devices with their start and end apart: 9, of which 6 were waited for; matrix products, arithmetic and copies ran while one was open for 5% of the time, Pallas kernels for 0%

profile of v15, /device:TPU:8, one launch (start us, length us, event | category | flops | bytes accessed | tf_op | source)
XLA Modules:
  0.0 95.1 jit_solution(10041362826911152935)
XLA Ops:
  0.0 0.0 copy-start
  0.0 1.1 %copy.35 = bf16[128,256]{0,1:T(8,128)(2,1)S(1)} copy(bf16[128,256]{1,0:T(8,128)(2,1)} %param.7) | data formatting | bytes 131072 | tf_op args[0]
  1.1 1.0 %copy.36 = bf16[128,256]{0,1:T(8,128)(2,1)S(1)} copy(bf16[128,256]{1,0:T(8,128)(2,1)} %param.8) | data formatting | bytes 131072 | tf_op args[1]
  2.1 1.0 %copy.37 = bf16[128,256]{0,1:T(8,128)(2,1)S(1)} copy(bf16[128,256]{1,0:T(8,128)(2,1)} %param.9) | data formatting | bytes 131072 | tf_op args[2]
  3.0 0.2 maximum_bitcast_fusion
  3.2 0.7 copy.38
  3.9 21.1 %all-to-all-start = ((bf16[64,3,4,128]{3,2,1,0:T(4,128)(2,1)}), bf16[64,3,4,128]{3,2,1,0:T(4,128)(2,1)S(1)}, u32[]{:S(2)}, u32[]{:S(2)}) async-start(bf16[64,3,4,128]{3,2,1,0:T(4,128)(2,1)} %copy.38), calls=%async_computation | async-start | bytes 393216 | tf_op jit(solution)/shard_map/all_to_all | solution.py:120
  25.0 0.3 broadcast_multiply_fusion
  25.3 0.3 fusion.47
  25.6 0.9 fusion.50
  26.6 0.1 stack.96
  26.8 0.3 fusion.45
  27.0 0.4 convolution_bitcast_fusion
  27.5 9.5 %all-to-all-done = bf16[64,3,4,128]{3,2,1,0:T(4,128)(2,1)S(1)} async-done(((bf16[64,3,4,128]{3,2,1,0:T(4,128)(2,1)}), bf16[64,3,4,128]{3,2,1,0:T(4,128)(2,1)S(1)}, u32[]{:S(2)}, u32[]{:S(2)}) %all-to-all-start) | async-done | bytes 196640 | tf_op jit(solution)/shard_map/all_to_all | solution.py:120
  37.0 0.1 slice_bitcast_fusion.2
  37.0 0.3 multiply_convert_fusion.1
  37.4 0.3 convolution_bitcast_fusion.1
  37.7 0.1 multiply_add_fusion.3
  37.9 0.6 fusion.2
  38.5 0.6 fusion.6
  39.1 0.0 copy-start.3
  39.1 0.1 multiply_subtract_fusion.1
  39.2 0.4 fusion.10
  39.6 0.1 multiply_subtract_fusion
  39.7 0.4 fusion
  40.1 0.2 fusion.35
  40.3 0.7 pad_maximum_fusion.5
  41.1 7.8 %all-to-all-start.1 = ((bf16[128,4,128]{2,1,0:T(4,128)(2,1)}), bf16[128,4,128]{2,1,0:T(4,128)(2,1)S(1)}, u32[]{:S(2)}, u32[]{:S(2)}) async-start(bf16[128,4,128]{2,1,0:T(4,128)(2,1)} %pad_maximum_fusion.5), calls=%async_computation.1 | async-start | bytes 262144 | tf_op jit(solution)/shard_map/all_to_all | solution.py:129
  48.9 0.1 copy.49
  48.9 0.1 reshape.717
  49.0 2.0 %gather_fusion = bf16[16,256,256]{2,1,0:T(8,128)(2,1)} fusion(bf16[16,256,256]{2,1,0:T(8,128)(2,1)S(1)} %bitcast.134, s32[1024]{0:T(1024)S(1)} %pad_clamp_fusion), kind=kCustom, calls=%fused_computation | custom fusion | bytes 4194368 | tf_op jit(solution)/shard_map/gather | solution.py:132
  51.0 9.9 %all-to-all-done.1 = bf16[128,4,128]{2,1,0:T(4,128)(2,1)S(1)} async-done(((bf16[128,4,128]{2,1,0:T(4,128)(2,1)}), bf16[128,4,128]{2,1,0:T(4,128)(2,1)S(1)}, u32[]{:S(2)}, u32[]{:S(2)}) %all-to-all-start.1) | async-done | bytes 131104 | tf_op jit(solution)/shard_map/all_to_all | solution.py:129
  60.9 0.1 copy.48
  61.1 2.6 %collective-permute-start = (bf16[2,128,256]{2,1,0:T(8,128)(2,1)S(1)}, bf16[2,128,256]{2,1,0:T(8,128)(2,1)S(1)}, u32[]{:S(2)}, u32[]{:S(2)}) collective-permute-start(bf16[2,128,256]{2,1,0:T(8,128)(2,1)S(1)} %bitcast.145), channel_id=1, source_target_pairs={{0,2},{2,4},{4,6},{6,8},{8,10},{10,12},{12,14},{14,0},{1,3},{3,5},... | collective-permute-start | bytes 393224 | tf_op jit(solution)/shard_map/ppermute | solution.py:91
  63.7 4.6 %collective-permute-start.1 = (bf16[2,128,256]{2,1,0:T(8,128)(2,1)S(1)}, bf16[2,128,256]{2,1,0:T(8,128)(2,1)S(1)}, u32[]{:S(2)}, u32[]{:S(2)}) collective-permute-start(bf16[2,128,256]{2,1,0:T(8,128)(2,1)S(1)} %bitcast.146), channel_id=1, source_target_pairs={{0,14},{2,0},{4,2},{6,4},{8,6},{10,8},{12,10},{14,12},{1,15},{3,1}... | collective-permute-start | bytes 393224 | tf_op jit(solution)/shard_map/ppermute | solution.py:95
  68.3 1.5 %collective-permute-done = bf16[2,128,256]{2,1,0:T(8,128)(2,1)S(1)} collective-permute-done((bf16[2,128,256]{2,1,0:T(8,128)(2,1)S(1)}, bf16[2,128,256]{2,1,0:T(8,128)(2,1)S(1)}, u32[]{:S(2)}, u32[]{:S(2)}) %collective-permute-start) | collective-permute-done | bytes 131104 | tf_op jit(solution)/shard_map/ppermute | solution.py:91
  69.8 1.9 %collective-permute-start.2 = (bf16[2,128,256]{2,1,0:T(8,128)(2,1)S(1)}, bf16[2,128,256]{2,1,0:T(8,128)(2,1)S(1)}, u32[]{:S(2)}, u32[]{:S(2)}) collective-permute-start(bf16[2,128,256]{2,1,0:T(8,128)(2,1)S(1)} %collective-permute-done), channel_id=1, source_target_pairs={{0,2},{2,4},{4,6},{6,8},{8,10},{10,12},{12,14},{14,0},{1,3},{3,5},... | collective-permute-start | bytes 393224 | tf_op jit(solution)/shard_map/ppermute | solution.py:91
  71.7 0.0 collective-permute-done.1
  71.7 5.1 %collective-permute-start.3 = (bf16[2,128,256]{2,1,0:T(8,128)(2,1)S(1)}, bf16[2,128,256]{2,1,0:T(8,128)(2,1)S(1)}, u32[]{:S(2)}, u32[]{:S(2)}) collective-permute-start(bf16[2,128,256]{2,1,0:T(8,128)(2,1)S(1)} %collective-permute-done.1), channel_id=1, source_target_pairs={{0,14},{2,0},{4,2},{6,4},{8,6},{10,8},{12,10},{14,12},{1,15},{3,1}... | collective-permute-start | bytes 393224 | tf_op jit(solution)/shard_map/ppermute | solution.py:95
  76.9 1.0 %collective-permute-done.2 = bf16[2,128,256]{2,1,0:T(8,128)(2,1)S(1)} collective-permute-done((bf16[2,128,256]{2,1,0:T(8,128)(2,1)S(1)}, bf16[2,128,256]{2,1,0:T(8,128)(2,1)S(1)}, u32[]{:S(2)}, u32[]{:S(2)}) %collective-permute-start.2) | collective-permute-done | bytes 131104 | tf_op jit(solution)/shard_map/ppermute | solution.py:91
  77.9 1.9 %collective-permute-start.4 = (bf16[2,128,256]{2,1,0:T(8,128)(2,1)S(1)}, bf16[2,128,256]{2,1,0:T(8,128)(2,1)S(1)}, u32[]{:S(2)}, u32[]{:S(2)}) collective-permute-start(bf16[2,128,256]{2,1,0:T(8,128)(2,1)S(1)} %collective-permute-done.2), channel_id=1, source_target_pairs={{0,2},{2,4},{4,6},{6,8},{8,10},{10,12},{12,14},{14,0},{1,3},{3,5},... | collective-permute-start | bytes 393224 | tf_op jit(solution)/shard_map/ppermute | solution.py:91
  79.8 0.0 collective-permute-done.3
  79.8 5.1 %collective-permute-start.5 = (bf16[2,128,256]{2,1,0:T(8,128)(2,1)S(1)}, bf16[2,128,256]{2,1,0:T(8,128)(2,1)S(1)}, u32[]{:S(2)}, u32[]{:S(2)}) collective-permute-start(bf16[2,128,256]{2,1,0:T(8,128)(2,1)S(1)} %collective-permute-done.3), channel_id=1, source_target_pairs={{0,14},{2,0},{4,2},{6,4},{8,6},{10,8},{12,10},{14,12},{1,15},{3,1}... | collective-permute-start | bytes 393224 | tf_op jit(solution)/shard_map/ppermute | solution.py:95
  85.0 1.0 %collective-permute-done.4 = bf16[2,128,256]{2,1,0:T(8,128)(2,1)S(1)} collective-permute-done((bf16[2,128,256]{2,1,0:T(8,128)(2,1)S(1)}, bf16[2,128,256]{2,1,0:T(8,128)(2,1)S(1)}, u32[]{:S(2)}, u32[]{:S(2)}) %collective-permute-start.4) | collective-permute-done | bytes 131104 | tf_op jit(solution)/shard_map/ppermute | solution.py:91
  85.9 1.9 %collective-permute-start.6 = (bf16[2,128,256]{2,1,0:T(8,128)(2,1)S(1)}, bf16[2,128,256]{2,1,0:T(8,128)(2,1)S(1)}, u32[]{:S(2)}, u32[]{:S(2)}) collective-permute-start(bf16[2,128,256]{2,1,0:T(8,128)(2,1)S(1)} %collective-permute-done.4), channel_id=1, source_target_pairs={{0,2},{2,4},{4,6},{6,8},{8,10},{10,12},{12,14},{14,0},{1,3},{3,5},... | collective-permute-start | bytes 393224 | tf_op jit(solution)/shard_map/ppermute | solution.py:91
  87.9 0.0 collective-permute-done.5
  87.9 6.1 %collective-permute-done.6 = bf16[2,128,256]{2,1,0:T(8,128)(2,1)S(1)} collective-permute-done((bf16[2,128,256]{2,1,0:T(8,128)(2,1)S(1)}, bf16[2,128,256]{2,1,0:T(8,128)(2,1)S(1)}, u32[]{:S(2)}, u32[]{:S(2)}) %collective-permute-start.6) | collective-permute-done | bytes 131104 | tf_op jit(solution)/shard_map/ppermute | solution.py:91
  94.0 1.1 %fusion.1 = bf16[128,256]{1,0:T(8,128)(2,1)} fusion(bf16[8,2,128,256]{3,2,1,0:T(8,128)(2,1)S(1)} %bitcast_dynamic-update-slice_fusion.1, bf16[8,2,256,256]{3,2,1,0:T(8,128)(2,1)S(1)} %bitcast.135), kind=kOutput, calls=%fused_computation.6 | convolution fusion | flops 268468224 | bytes 3211264 | tf_op jit(solution)/shard_map/pqtc,pqcj->tj/dot_general | solution.py:133
  (21 shorter events, 0.2 us)
Async XLA Ops:
  0.0 49.0 %copy-start = (bf16[4096,256]{1,0:T(8,128)(2,1)S(1)}, bf16[4096,256]{1,0:T(8,128)(2,1)}, u32[]{:S(2)}) copy-start(bf16[4096,256]{1,0:T(8,128)(2,1)} %param.13) | copy-start | bytes 6291460
  0.0 27.0 %copy-start.2 = (f32[4,8192]{1,0:T(4,128)S(1)}, f32[4,8192]{1,0:T(4,128)}, u32[]{:S(2)}) copy-start(f32[4,8192]{1,0:T(4,128)} %param.11) | copy-start | bytes 393220
  3.9 33.0 %all-to-all-start = ((bf16[64,3,4,128]{3,2,1,0:T(4,128)(2,1)}), bf16[64,3,4,128]{3,2,1,0:T(4,128)(2,1)S(1)}, u32[]{:S(2)}, u32[]{:S(2)}) async-start(bf16[64,3,4,128]{3,2,1,0:T(4,128)(2,1)} %copy.38), calls=%async_computation | async-start | bytes 393216 | tf_op jit(solution)/shard_map/all_to_all | solution.py:120
  39.1 1.0 %copy-start.3 = (f32[4]{0:T(128)S(1)}, f32[4]{0:T(128)}, u32[]{:S(2)}) copy-start(f32[4]{0:T(128)} %param.12) | copy-start | bytes 52
  41.1 19.9 %all-to-all-start.1 = ((bf16[128,4,128]{2,1,0:T(4,128)(2,1)}), bf16[128,4,128]{2,1,0:T(4,128)(2,1)S(1)}, u32[]{:S(2)}, u32[]{:S(2)}) async-start(bf16[128,4,128]{2,1,0:T(4,128)(2,1)} %pad_maximum_fusion.5), calls=%async_computation.1 | async-start | bytes 262144 | tf_op jit(solution)/shard_map/all_to_all | solution.py:129
  61.1 33.0 %copy-start.1 = (bf16[16,256,256]{2,1,0:T(8,128)(2,1)S(1)}, bf16[16,256,256]{2,1,0:T(8,128)(2,1)}, u32[]{:S(2)}) copy-start(bf16[16,256,256]{2,1,0:T(8,128)(2,1)} %gather_fusion) | copy-start | bytes 6291460
  61.1 8.8 %collective-permute-start = (bf16[2,128,256]{2,1,0:T(8,128)(2,1)S(1)}, bf16[2,128,256]{2,1,0:T(8,128)(2,1)S(1)}, u32[]{:S(2)}, u32[]{:S(2)}) collective-permute-start(bf16[2,128,256]{2,1,0:T(8,128)(2,1)S(1)} %bitcast.145), channel_id=1, source_target_pairs={{0,2},{2,4},{4,6},{6,8},{8,10},{10,12},{12,14},{14,0},{1,3},{3,5},... | collective-permute-start | bytes 393224 | tf_op jit(solution)/shard_map/ppermute | solution.py:91
  63.7 8.0 %collective-permute-start.1 = (bf16[2,128,256]{2,1,0:T(8,128)(2,1)S(1)}, bf16[2,128,256]{2,1,0:T(8,128)(2,1)S(1)}, u32[]{:S(2)}, u32[]{:S(2)}) collective-permute-start(bf16[2,128,256]{2,1,0:T(8,128)(2,1)S(1)} %bitcast.146), channel_id=1, source_target_pairs={{0,14},{2,0},{4,2},{6,4},{8,6},{10,8},{12,10},{14,12},{1,15},{3,1}... | collective-permute-start | bytes 393224 | tf_op jit(solution)/shard_map/ppermute | solution.py:95
  69.8 8.1 %collective-permute-start.2 = (bf16[2,128,256]{2,1,0:T(8,128)(2,1)S(1)}, bf16[2,128,256]{2,1,0:T(8,128)(2,1)S(1)}, u32[]{:S(2)}, u32[]{:S(2)}) collective-permute-start(bf16[2,128,256]{2,1,0:T(8,128)(2,1)S(1)} %collective-permute-done), channel_id=1, source_target_pairs={{0,2},{2,4},{4,6},{6,8},{8,10},{10,12},{12,14},{14,0},{1,3},{3,5},... | collective-permute-start | bytes 393224 | tf_op jit(solution)/shard_map/ppermute | solution.py:91
  71.7 8.1 %collective-permute-start.3 = (bf16[2,128,256]{2,1,0:T(8,128)(2,1)S(1)}, bf16[2,128,256]{2,1,0:T(8,128)(2,1)S(1)}, u32[]{:S(2)}, u32[]{:S(2)}) collective-permute-start(bf16[2,128,256]{2,1,0:T(8,128)(2,1)S(1)} %collective-permute-done.1), channel_id=1, source_target_pairs={{0,14},{2,0},{4,2},{6,4},{8,6},{10,8},{12,10},{14,12},{1,15},{3,1}... | collective-permute-start | bytes 393224 | tf_op jit(solution)/shard_map/ppermute | solution.py:95
  77.9 8.1 %collective-permute-start.4 = (bf16[2,128,256]{2,1,0:T(8,128)(2,1)S(1)}, bf16[2,128,256]{2,1,0:T(8,128)(2,1)S(1)}, u32[]{:S(2)}, u32[]{:S(2)}) collective-permute-start(bf16[2,128,256]{2,1,0:T(8,128)(2,1)S(1)} %collective-permute-done.2), channel_id=1, source_target_pairs={{0,2},{2,4},{4,6},{6,8},{8,10},{10,12},{12,14},{14,0},{1,3},{3,5},... | collective-permute-start | bytes 393224 | tf_op jit(solution)/shard_map/ppermute | solution.py:91
  79.8 8.1 %collective-permute-start.5 = (bf16[2,128,256]{2,1,0:T(8,128)(2,1)S(1)}, bf16[2,128,256]{2,1,0:T(8,128)(2,1)S(1)}, u32[]{:S(2)}, u32[]{:S(2)}) collective-permute-start(bf16[2,128,256]{2,1,0:T(8,128)(2,1)S(1)} %collective-permute-done.3), channel_id=1, source_target_pairs={{0,14},{2,0},{4,2},{6,4},{8,6},{10,8},{12,10},{14,12},{1,15},{3,1}... | collective-permute-start | bytes 393224 | tf_op jit(solution)/shard_map/ppermute | solution.py:95
  85.9 8.1 %collective-permute-start.6 = (bf16[2,128,256]{2,1,0:T(8,128)(2,1)S(1)}, bf16[2,128,256]{2,1,0:T(8,128)(2,1)S(1)}, u32[]{:S(2)}, u32[]{:S(2)}) collective-permute-start(bf16[2,128,256]{2,1,0:T(8,128)(2,1)S(1)} %collective-permute-done.4), channel_id=1, source_target_pairs={{0,2},{2,4},{4,6},{6,8},{8,10},{10,12},{12,14},{14,0},{1,3},{3,5},... | collective-permute-start | bytes 393224 | tf_op jit(solution)/shard_map/ppermute | solution.py:91

commit v16 on v15

--- a/solution.py
+++ b/solution.py
@@ -130,7 +130,8 @@
     held = returned.reshape(2, width, rows).transpose(0, 2, 1)
     pieces, order = gather_pairs(held)
     weight = out_weight.reshape(-1, width, out_weight.shape[1])[order]
-    result = jnp.einsum("pqtc,pqcj->tj", pieces, weight, preferred_element_type=jnp.float32)
+    early = jnp.einsum("pqtc,pqcj->tj", pieces[:-1], weight[:-1], preferred_element_type=jnp.float32)
+    result = early + jnp.einsum("qtc,qcj->tj", pieces[-1], weight[-1], preferred_element_type=jnp.float32)
     return result.astype(jnp.bfloat16)
 
 

time: 95.6 us -> 95.4 us (level)
    unnamed x18 -> x17, local copies, waits for them, and re-layouts: 3.11 us -> 3.1 us
where the time goes in v16:
time: 95.4 us; the launch traced here: 94.8 us
  starting transfers between devices  52 us (55%)
  waiting for transfers between devices  28.4 us (30%)
  local copies, waits for them, and re-layouts  7.26 us (8%)
  matrix products  4.01 us (4%)
  other arithmetic  2.62 us (3%)
    all_to_all x1, starting transfers between devices, body(): lax.all_to_all(raw, SEQ, split_axis=0, concat_axis=0, tiled=True)  21.1 us
    ppermute x3, starting transfers between devices, gather_pairs(): left = lax.ppermute(left, 'x', [(i, (i - 1) % size) for i in range(size)])  14.8 us
    all_to_all x1, waiting for transfers between devices, body(): lax.all_to_all(both, ('yh',) + SEQ, split_axis=0, concat_axis=0, tiled=True)  9.87 us
    all_to_all x1, waiting for transfers between devices, body(): lax.all_to_all(raw, SEQ, split_axis=0, concat_axis=0, tiled=True)  9.46 us
    ppermute x4, waiting for transfers between devices, gather_pairs(): right = lax.ppermute(right, 'x', [(i, (i + 1) % size) for i in range(size)])  9.1 us
    ppermute x4, starting transfers between devices, gather_pairs(): right = lax.ppermute(right, 'x', [(i, (i + 1) % size) for i in range(size)])  8.35 us
    all_to_all x1, starting transfers between devices, body(): lax.all_to_all(both, ('yh',) + SEQ, split_axis=0, concat_axis=0, tiled=True)  7.77 us
    unnamed x17, local copies, waits for them, and re-layouts  3.1 us
  transfers between devices with their start and end apart: 9, of which 6 were waited for; matrix products, arithmetic and copies ran while one was open for 5% of the time, Pallas kernels for 0%

profile of v16, /device:TPU:8, one launch (start us, length us, event | category | flops | bytes accessed | tf_op | source)
XLA Modules:
  0.0 94.8 jit_solution(9014504314923877627)
XLA Ops:
  0.0 1.1 %copy.35 = bf16[128,256]{0,1:T(8,128)(2,1)S(1)} copy(bf16[128,256]{1,0:T(8,128)(2,1)} %param.7) | data formatting | bytes 131072 | tf_op args[0]
  1.1 1.0 %copy.36 = bf16[128,256]{0,1:T(8,128)(2,1)S(1)} copy(bf16[128,256]{1,0:T(8,128)(2,1)} %param.8) | data formatting | bytes 131072 | tf_op args[1]
  2.1 1.0 %copy.37 = bf16[128,256]{0,1:T(8,128)(2,1)S(1)} copy(bf16[128,256]{1,0:T(8,128)(2,1)} %param.9) | data formatting | bytes 131072 | tf_op args[2]
  3.0 0.2 maximum_bitcast_fusion
  3.2 0.8 copy.38
  4.0 21.1 %all-to-all-start = ((bf16[64,3,4,128]{3,2,1,0:T(4,128)(2,1)}), bf16[64,3,4,128]{3,2,1,0:T(4,128)(2,1)S(1)}, u32[]{:S(2)}, u32[]{:S(2)}) async-start(bf16[64,3,4,128]{3,2,1,0:T(4,128)(2,1)} %copy.38), calls=%async_computation | async-start | bytes 393216 | tf_op jit(solution)/shard_map/all_to_all | solution.py:120
  25.0 0.3 broadcast_multiply_fusion
  25.3 0.3 fusion.49
  25.6 0.9 fusion.52
  26.7 0.1 stack.92
  26.8 0.3 fusion.47
  27.0 0.4 convolution_bitcast_fusion
  27.5 9.5 %all-to-all-done = bf16[64,3,4,128]{3,2,1,0:T(4,128)(2,1)S(1)} async-done(((bf16[64,3,4,128]{3,2,1,0:T(4,128)(2,1)}), bf16[64,3,4,128]{3,2,1,0:T(4,128)(2,1)S(1)}, u32[]{:S(2)}, u32[]{:S(2)}) %all-to-all-start) | async-done | bytes 196640 | tf_op jit(solution)/shard_map/all_to_all | solution.py:120
  37.0 0.1 slice_bitcast_fusion.2
  37.0 0.3 multiply_convert_fusion.1
  37.4 0.3 convolution_bitcast_fusion.1
  37.7 0.1 multiply_add_fusion.3
  37.9 0.6 fusion.3
  38.5 0.6 fusion.7
  39.1 0.0 copy-start.3
  39.1 0.1 multiply_subtract_fusion.1
  39.2 0.4 fusion.11
  39.6 0.1 multiply_subtract_fusion
  39.7 0.4 fusion
  40.1 0.2 fusion.37
  40.4 0.7 pad_maximum_fusion.5
  41.1 7.8 %all-to-all-start.1 = ((bf16[128,4,128]{2,1,0:T(4,128)(2,1)}), bf16[128,4,128]{2,1,0:T(4,128)(2,1)S(1)}, u32[]{:S(2)}, u32[]{:S(2)}) async-start(bf16[128,4,128]{2,1,0:T(4,128)(2,1)} %pad_maximum_fusion.5), calls=%async_computation.1 | async-start | bytes 262144 | tf_op jit(solution)/shard_map/all_to_all | solution.py:129
  48.9 0.1 copy.49
  49.0 0.1 reshape.717
  49.1 2.0 %gather_fusion = bf16[16,256,256]{2,1,0:T(8,128)(2,1)} fusion(bf16[16,256,256]{2,1,0:T(8,128)(2,1)S(1)} %bitcast.137, s32[1024]{0:T(1024)S(1)} %pad_clamp_fusion), kind=kCustom, calls=%fused_computation | custom fusion | bytes 4194368 | tf_op jit(solution)/shard_map/gather | solution.py:132
  51.1 9.9 %all-to-all-done.1 = bf16[128,4,128]{2,1,0:T(4,128)(2,1)S(1)} async-done(((bf16[128,4,128]{2,1,0:T(4,128)(2,1)}), bf16[128,4,128]{2,1,0:T(4,128)(2,1)S(1)}, u32[]{:S(2)}, u32[]{:S(2)}) %all-to-all-start.1) | async-done | bytes 131104 | tf_op jit(solution)/shard_map/all_to_all | solution.py:129
  60.9 0.1 copy.48
  61.1 0.0 slice-start
  61.1 2.6 %collective-permute-start = (bf16[2,128,256]{2,1,0:T(8,128)(2,1)S(1)}, bf16[2,128,256]{2,1,0:T(8,128)(2,1)S(1)}, u32[]{:S(2)}, u32[]{:S(2)}) collective-permute-start(bf16[2,128,256]{2,1,0:T(8,128)(2,1)S(1)} %bitcast.148), channel_id=1, source_target_pairs={{0,2},{2,4},{4,6},{6,8},{8,10},{10,12},{12,14},{14,0},{1,3},{3,5},... | collective-permute-start | bytes 393224 | tf_op jit(solution)/shard_map/ppermute | solution.py:91
  63.7 4.6 %collective-permute-start.1 = (bf16[2,128,256]{2,1,0:T(8,128)(2,1)S(1)}, bf16[2,128,256]{2,1,0:T(8,128)(2,1)S(1)}, u32[]{:S(2)}, u32[]{:S(2)}) collective-permute-start(bf16[2,128,256]{2,1,0:T(8,128)(2,1)S(1)} %bitcast.149), channel_id=1, source_target_pairs={{0,14},{2,0},{4,2},{6,4},{8,6},{10,8},{12,10},{14,12},{1,15},{3,1}... | collective-permute-start | bytes 393224 | tf_op jit(solution)/shard_map/ppermute | solution.py:95
  68.3 1.5 %collective-permute-done = bf16[2,128,256]{2,1,0:T(8,128)(2,1)S(1)} collective-permute-done((bf16[2,128,256]{2,1,0:T(8,128)(2,1)S(1)}, bf16[2,128,256]{2,1,0:T(8,128)(2,1)S(1)}, u32[]{:S(2)}, u32[]{:S(2)}) %collective-permute-start) | collective-permute-done | bytes 131104 | tf_op jit(solution)/shard_map/ppermute | solution.py:91
  69.8 1.9 %collective-permute-start.2 = (bf16[2,128,256]{2,1,0:T(8,128)(2,1)S(1)}, bf16[2,128,256]{2,1,0:T(8,128)(2,1)S(1)}, u32[]{:S(2)}, u32[]{:S(2)}) collective-permute-start(bf16[2,128,256]{2,1,0:T(8,128)(2,1)S(1)} %collective-permute-done), channel_id=1, source_target_pairs={{0,2},{2,4},{4,6},{6,8},{8,10},{10,12},{12,14},{14,0},{1,3},{3,5},... | collective-permute-start | bytes 393224 | tf_op jit(solution)/shard_map/ppermute | solution.py:91
  71.8 5.1 %collective-permute-start.3 = (bf16[2,128,256]{2,1,0:T(8,128)(2,1)S(1)}, bf16[2,128,256]{2,1,0:T(8,128)(2,1)S(1)}, u32[]{:S(2)}, u32[]{:S(2)}) collective-permute-start(bf16[2,128,256]{2,1,0:T(8,128)(2,1)S(1)} %collective-permute-done.1), channel_id=1, source_target_pairs={{0,14},{2,0},{4,2},{6,4},{8,6},{10,8},{12,10},{14,12},{1,15},{3,1}... | collective-permute-start | bytes 393224 | tf_op jit(solution)/shard_map/ppermute | solution.py:95
  76.9 0.9 collective-permute-done.2
  77.9 1.9 %collective-permute-start.4 = (bf16[2,128,256]{2,1,0:T(8,128)(2,1)S(1)}, bf16[2,128,256]{2,1,0:T(8,128)(2,1)S(1)}, u32[]{:S(2)}, u32[]{:S(2)}) collective-permute-start(bf16[2,128,256]{2,1,0:T(8,128)(2,1)S(1)} %collective-permute-done.2), channel_id=1, source_target_pairs={{0,2},{2,4},{4,6},{6,8},{8,10},{10,12},{12,14},{14,0},{1,3},{3,5},... | collective-permute-start | bytes 393224 | tf_op jit(solution)/shard_map/ppermute | solution.py:91
  79.8 0.0 collective-permute-done.3
  79.8 5.1 %collective-permute-start.5 = (bf16[2,128,256]{2,1,0:T(8,128)(2,1)S(1)}, bf16[2,128,256]{2,1,0:T(8,128)(2,1)S(1)}, u32[]{:S(2)}, u32[]{:S(2)}) collective-permute-start(bf16[2,128,256]{2,1,0:T(8,128)(2,1)S(1)} %collective-permute-done.3), channel_id=1, source_target_pairs={{0,14},{2,0},{4,2},{6,4},{8,6},{10,8},{12,10},{14,12},{1,15},{3,1}... | collective-permute-start | bytes 393224 | tf_op jit(solution)/shard_map/ppermute | solution.py:95
  85.0 1.0 %collective-permute-done.4 = bf16[2,128,256]{2,1,0:T(8,128)(2,1)S(1)} collective-permute-done((bf16[2,128,256]{2,1,0:T(8,128)(2,1)S(1)}, bf16[2,128,256]{2,1,0:T(8,128)(2,1)S(1)}, u32[]{:S(2)}, u32[]{:S(2)}) %collective-permute-start.4) | collective-permute-done | bytes 131104 | tf_op jit(solution)/shard_map/ppermute | solution.py:91
  86.0 1.9 %collective-permute-start.6 = (bf16[2,128,256]{2,1,0:T(8,128)(2,1)S(1)}, bf16[2,128,256]{2,1,0:T(8,128)(2,1)S(1)}, u32[]{:S(2)}, u32[]{:S(2)}) collective-permute-start(bf16[2,128,256]{2,1,0:T(8,128)(2,1)S(1)} %collective-permute-done.4), channel_id=1, source_target_pairs={{0,2},{2,4},{4,6},{6,8},{8,10},{10,12},{12,14},{14,0},{1,3},{3,5},... | collective-permute-start | bytes 393224 | tf_op jit(solution)/shard_map/ppermute | solution.py:91
  87.9 0.0 collective-permute-done.5
  87.9 0.4 convolution_bitcast_fusion.3
  88.3 5.7 %collective-permute-done.6 = bf16[2,128,256]{2,1,0:T(8,128)(2,1)S(1)} collective-permute-done((bf16[2,128,256]{2,1,0:T(8,128)(2,1)S(1)}, bf16[2,128,256]{2,1,0:T(8,128)(2,1)S(1)}, u32[]{:S(2)}, u32[]{:S(2)}) %collective-permute-start.6) | collective-permute-done | bytes 131104 | tf_op jit(solution)/shard_map/ppermute | solution.py:91
  94.0 0.8 fusion.2
  (23 shorter events, 0.2 us)
Async XLA Ops:
  0.0 49.0 %copy-start = (bf16[4096,256]{1,0:T(8,128)(2,1)S(1)}, bf16[4096,256]{1,0:T(8,128)(2,1)}, u32[]{:S(2)}) copy-start(bf16[4096,256]{1,0:T(8,128)(2,1)} %param.13) | copy-start | bytes 6291460
  0.0 27.0 %copy-start.2 = (f32[4,8192]{1,0:T(4,128)S(1)}, f32[4,8192]{1,0:T(4,128)}, u32[]{:S(2)}) copy-start(f32[4,8192]{1,0:T(4,128)} %param.11) | copy-start | bytes 393220
  4.0 33.0 %all-to-all-start = ((bf16[64,3,4,128]{3,2,1,0:T(4,128)(2,1)}), bf16[64,3,4,128]{3,2,1,0:T(4,128)(2,1)S(1)}, u32[]{:S(2)}, u32[]{:S(2)}) async-start(bf16[64,3,4,128]{3,2,1,0:T(4,128)(2,1)} %copy.38), calls=%async_computation | async-start | bytes 393216 | tf_op jit(solution)/shard_map/all_to_all | solution.py:120
  39.1 1.0 %copy-start.3 = (f32[4]{0:T(128)S(1)}, f32[4]{0:T(128)}, u32[]{:S(2)}) copy-start(f32[4]{0:T(128)} %param.12) | copy-start | bytes 52
  41.1 19.9 %all-to-all-start.1 = ((bf16[128,4,128]{2,1,0:T(4,128)(2,1)}), bf16[128,4,128]{2,1,0:T(4,128)(2,1)S(1)}, u32[]{:S(2)}, u32[]{:S(2)}) async-start(bf16[128,4,128]{2,1,0:T(4,128)(2,1)} %pad_maximum_fusion.5), calls=%async_computation.1 | async-start | bytes 262144 | tf_op jit(solution)/shard_map/all_to_all | solution.py:129
  61.1 26.9 %slice-start = ((bf16[16,256,256]{2,1,0:T(8,128)(2,1)}), bf16[14,256,256]{2,1,0:T(8,128)(2,1)S(1)}, s32[]{:S(2)}) async-start(bf16[16,256,256]{2,1,0:T(8,128)(2,1)} %gather_fusion), calls=%async_computation.2 | async-start | bytes 3670016 | tf_op jit(solution)/shard_map/slice | solution.py:133
  61.1 8.8 %collective-permute-start = (bf16[2,128,256]{2,1,0:T(8,128)(2,1)S(1)}, bf16[2,128,256]{2,1,0:T(8,128)(2,1)S(1)}, u32[]{:S(2)}, u32[]{:S(2)}) collective-permute-start(bf16[2,128,256]{2,1,0:T(8,128)(2,1)S(1)} %bitcast.148), channel_id=1, source_target_pairs={{0,2},{2,4},{4,6},{6,8},{8,10},{10,12},{12,14},{14,0},{1,3},{3,5},... | collective-permute-start | bytes 393224 | tf_op jit(solution)/shard_map/ppermute | solution.py:91
  63.7 8.0 %collective-permute-start.1 = (bf16[2,128,256]{2,1,0:T(8,128)(2,1)S(1)}, bf16[2,128,256]{2,1,0:T(8,128)(2,1)S(1)}, u32[]{:S(2)}, u32[]{:S(2)}) collective-permute-start(bf16[2,128,256]{2,1,0:T(8,128)(2,1)S(1)} %bitcast.149), channel_id=1, source_target_pairs={{0,14},{2,0},{4,2},{6,4},{8,6},{10,8},{12,10},{14,12},{1,15},{3,1}... | collective-permute-start | bytes 393224 | tf_op jit(solution)/shard_map/ppermute | solution.py:95
  69.8 8.1 %collective-permute-start.2 = (bf16[2,128,256]{2,1,0:T(8,128)(2,1)S(1)}, bf16[2,128,256]{2,1,0:T(8,128)(2,1)S(1)}, u32[]{:S(2)}, u32[]{:S(2)}) collective-permute-start(bf16[2,128,256]{2,1,0:T(8,128)(2,1)S(1)} %collective-permute-done), channel_id=1, source_target_pairs={{0,2},{2,4},{4,6},{6,8},{8,10},{10,12},{12,14},{14,0},{1,3},{3,5},... | collective-permute-start | bytes 393224 | tf_op jit(solution)/shard_map/ppermute | solution.py:91
  71.8 8.1 %collective-permute-start.3 = (bf16[2,128,256]{2,1,0:T(8,128)(2,1)S(1)}, bf16[2,128,256]{2,1,0:T(8,128)(2,1)S(1)}, u32[]{:S(2)}, u32[]{:S(2)}) collective-permute-start(bf16[2,128,256]{2,1,0:T(8,128)(2,1)S(1)} %collective-permute-done.1), channel_id=1, source_target_pairs={{0,14},{2,0},{4,2},{6,4},{8,6},{10,8},{12,10},{14,12},{1,15},{3,1}... | collective-permute-start | bytes 393224 | tf_op jit(solution)/shard_map/ppermute | solution.py:95
  76.9 17.1 %copy-start.1 = (bf16[16,256,256]{2,1,0:T(8,128)(2,1)S(1)}, bf16[16,256,256]{2,1,0:T(8,128)(2,1)}, u32[]{:S(2)}) copy-start(bf16[16,256,256]{2,1,0:T(8,128)(2,1)} %gather_fusion) | copy-start | bytes 6291460
  77.9 8.1 %collective-permute-start.4 = (bf16[2,128,256]{2,1,0:T(8,128)(2,1)S(1)}, bf16[2,128,256]{2,1,0:T(8,128)(2,1)S(1)}, u32[]{:S(2)}, u32[]{:S(2)}) collective-permute-start(bf16[2,128,256]{2,1,0:T(8,128)(2,1)S(1)} %collective-permute-done.2), channel_id=1, source_target_pairs={{0,2},{2,4},{4,6},{6,8},{8,10},{10,12},{12,14},{14,0},{1,3},{3,5},... | collective-permute-start | bytes 393224 | tf_op jit(solution)/shard_map/ppermute | solution.py:91
  79.8 8.1 %collective-permute-start.5 = (bf16[2,128,256]{2,1,0:T(8,128)(2,1)S(1)}, bf16[2,128,256]{2,1,0:T(8,128)(2,1)S(1)}, u32[]{:S(2)}, u32[]{:S(2)}) collective-permute-start(bf16[2,128,256]{2,1,0:T(8,128)(2,1)S(1)} %collective-permute-done.3), channel_id=1, source_target_pairs={{0,14},{2,0},{4,2},{6,4},{8,6},{10,8},{12,10},{14,12},{1,15},{3,1}... | collective-permute-start | bytes 393224 | tf_op jit(solution)/shard_map/ppermute | solution.py:95
  86.0 8.1 %collective-permute-start.6 = (bf16[2,128,256]{2,1,0:T(8,128)(2,1)S(1)}, bf16[2,128,256]{2,1,0:T(8,128)(2,1)S(1)}, u32[]{:S(2)}, u32[]{:S(2)}) collective-permute-start(bf16[2,128,256]{2,1,0:T(8,128)(2,1)S(1)} %collective-permute-done.4), channel_id=1, source_target_pairs={{0,2},{2,4},{4,6},{6,8},{8,10},{10,12},{12,14},{14,0},{1,3},{3,5},... | collective-permute-start | bytes 393224 | tf_op jit(solution)/shard_map/ppermute | solution.py:91
